TPU v7x, 128 devices: a whole 4x4x4 slice. The times are simulated.
128 devices in a mesh: fsdp: 32 (over x_lo, z, y), grp: 4 (over x_hi, core).
Axes of the slice: x: 4 (x_hi: 2, x_lo: 2; x = x_hi * 2 + x_lo), y: 4, z: 4, core: 2. Of those that a mesh axis runs over, the one named last changes fastest.
Arguments:
- latents: bfloat16 [8192, 512], P('fsdp'), may hold values from -6 to 6
- queries: bfloat16 [8192, 128, 128], P('fsdp', 'grp')
- grad_out: bfloat16 [8192, 128, 128], P('fsdp', 'grp'), may hold values from -6 to 6
- kv_weight: bfloat16 [4, 32, 512, 256], P('grp', 'fsdp'), may hold values from -0.25 to 0.25
- doc_ids: int32 [8192], replicated, may hold values from 0 to 3, never falling along the last dimension, each value on 1 to 4096 neighbouring positions
- block_lists: int32 [128, 4], replicated, may hold values from 0 to 127, as said below
Outputs:
- grad_queries: bfloat16 [8192, 128, 128], P('fsdp', 'grp')
- grad_latents: float32 [8192, 512], P('fsdp', 'grp')
- grad_weight: float32 [4, 32, 512, 256], P('grp', 'fsdp')
Inputs may be any that keep to these rules, and one draw needn't show every extreme that they name: `block_lists`: row b belongs to query block b; its first entry is b and its 4 entries differ. Take the 4 rows of one run f (rows f * 4 to f * 4 + 3) without their first entries: for every d from 1 to 6 with f - d >= 0, exactly 2 of these entries, counted with repeats, are blocks of run f - d; all other entries are blocks of run f itself.
All inputs are finite; a program needn't handle non-finite values.
Results may differ from a plain program's by a relative error of at most 0.035.
The roundings to bfloat16 on the way count: a program that leaves them out, or rounds other values in their place, can miss the bound.
Values may be sent and summed in bfloat16 or wider, within the bound.
No kernel may reach another device: no remote copies, remote signals or barrier semaphores. Data moves between devices by JAX's collectives and lax.ppermute only.
A program may use at most 128 MiB of HBM per device.

v0:
```python
import jax
import jax.numpy as jnp
from jax import lax
from jax.sharding import PartitionSpec as P

BLK = 64
TOPK = 4
DIST = 6


NEG_FILL = -1e30


def passed_along(block, axis, distance):
    devices = range(lax.axis_size(axis))
    route = [(i - distance, i) for i in devices if i - distance in devices]
    return lax.ppermute(block, axis, route)


def head_pass(w_head, q_head, g_head, key_lat, visible, score_scale):
    head_width = q_head.shape[-1]
    block_count = q_head.shape[0]
    expanded = jnp.dot(key_lat, w_head, preferred_element_type=jnp.float32).astype(jnp.bfloat16)
    expanded = expanded.reshape(block_count, -1, 2 * head_width)
    key_rows = expanded[:, :, :head_width]
    value_rows = expanded[:, :, head_width:]
    scores = (
        jnp.einsum("qbd,qkd->qbk", q_head, key_rows, preferred_element_type=jnp.float32)
        * score_scale
    )
    scores = jnp.where(visible, scores, NEG_FILL)
    row_max = jnp.max(scores, axis=-1, keepdims=True)
    exp_scores = jnp.exp(scores - row_max)
    softmax_p = exp_scores / jnp.sum(exp_scores, axis=-1, keepdims=True)
    probs_low = softmax_p.astype(jnp.bfloat16)
    attended = jnp.einsum("qbk,qkd->qbd", probs_low, value_rows, preferred_element_type=jnp.float32)
    delta_rows = jnp.sum(g_head.astype(jnp.float32) * attended, axis=-1, keepdims=True)
    grad_probs = jnp.einsum("qbd,qkd->qbk", g_head, value_rows, preferred_element_type=jnp.float32)
    grad_scores = (softmax_p * (grad_probs - delta_rows)).astype(jnp.bfloat16)
    grad_q = (
        jnp.einsum("qbk,qkd->qbd", grad_scores, key_rows, preferred_element_type=jnp.float32)
        * score_scale
    ).astype(jnp.bfloat16)
    grad_k = (
        jnp.einsum("qbk,qbd->qkd", grad_scores, q_head, preferred_element_type=jnp.float32)
        * score_scale
    ).astype(jnp.bfloat16)
    grad_v = jnp.einsum(
        "qbk,qbd->qkd", probs_low, g_head, preferred_element_type=jnp.float32
    ).astype(jnp.bfloat16)
    grad_kv = jnp.concatenate([grad_k, grad_v], axis=-1).reshape(-1, 2 * head_width)
    lat_part = lax.dot_general(
        grad_kv, w_head, (((1,), (1,)), ((), ())), preferred_element_type=jnp.float32
    )
    grad_w = lax.dot_general(
        key_lat, grad_kv, (((0,), (0,)), ((), ())), preferred_element_type=jnp.float32
    )
    return (grad_q.reshape(-1, head_width), lat_part, grad_w)


def visibility(doc_ids, list_rows, query_start, block_count):
    offsets = jnp.arange(BLK, dtype=jnp.int32)
    key_pos = (list_rows[:, :, None] * BLK + offsets[None, None, :]).reshape(block_count, -1)
    query_pos = (query_start + jnp.arange(block_count * BLK, dtype=jnp.int32)).reshape(
        block_count, BLK
    )
    key_doc = jnp.take(doc_ids, key_pos)
    query_doc = jnp.take(doc_ids, query_pos)
    visible = (key_doc[:, None, :] == query_doc[:, :, None]) & (
        key_pos[:, None, :] <= query_pos[:, :, None]
    )
    return (key_pos, visible)


def earlier_count(flags):
    positions = jnp.arange(flags.shape[0])
    earlier = positions[None, :] < positions[:, None]
    return jnp.sum(flags & earlier, axis=1)


def slot_ranks(owner_ids):
    positions = jnp.arange(owner_ids.shape[0])
    same_owner = owner_ids[None, :] == owner_ids[:, None]
    earlier = positions[None, :] < positions[:, None]
    return jnp.sum(same_owner & earlier, axis=1)


def per_device(latents, queries, grad_out, kv_weight, doc_ids, block_lists):
    device_pos = lax.axis_index("fsdp")
    tok_rows, lat_width = latents.shape
    head_dim = queries.shape[2]
    head_count = queries.shape[1]
    block_count = tok_rows // BLK
    extra_picks = TOPK - 1
    slot_cap = block_count * extra_picks // DIST
    lat_share = lat_width // lax.axis_size("grp")
    score_scale = head_dim ** (-0.5)
    own_lists = lax.dynamic_slice_in_dim(block_lists, device_pos * block_count, block_count, 0)
    remote_ids = own_lists[:, 1:].reshape(-1)
    owner_ids = remote_ids // block_count
    owner_ranks = slot_ranks(owner_ids)
    remote_pool = jnp.where(
        owner_ids == device_pos,
        remote_ids % block_count,
        block_count + (device_pos - owner_ids - 1) * slot_cap + owner_ranks,
    )
    pool_index = jnp.concatenate(
        [
            jnp.arange(block_count, dtype=jnp.int32)[:, None],
            remote_pool.reshape(block_count, extra_picks),
        ],
        axis=1,
    )
    local_blocks = latents.reshape(block_count, BLK, lat_width)
    send_lists = []
    arrived = []
    for distance in range(1, DIST + 1):
        reader_lists = lax.dynamic_slice_in_dim(
            block_lists, (device_pos + distance) * block_count, block_count, 0
        )
        reader_remote = reader_lists[:, 1:].reshape(-1)
        wanted = reader_remote // block_count == device_pos
        reader_ranks = earlier_count(wanted[None, :] & jnp.ones((wanted.shape[0], 1), bool))
        choose_table = wanted[None, :] & (reader_ranks[None, :] == jnp.arange(slot_cap)[:, None])
        send_index = jnp.sum(
            jnp.where(choose_table, (reader_remote % block_count)[None, :], 0), axis=1
        )
        send_lists.append(send_index)
        outgoing = jnp.take(local_blocks, send_index, axis=0)
        arrived.append(passed_along(outgoing, "fsdp", distance))
    fetched = jnp.concatenate(arrived, axis=0)
    block_pool = jnp.concatenate([local_blocks, fetched], axis=0)
    key_lat = jnp.take(block_pool, pool_index.reshape(-1), axis=0).reshape(-1, lat_width)
    key_pos, visible = visibility(doc_ids, own_lists, device_pos * tok_rows, block_count)

    def run_head(head_idx, w_head, grad_q_all, grad_lat):
        q_head = lax.dynamic_index_in_dim(queries, head_idx, 1, False).reshape(
            block_count, BLK, head_dim
        )
        g_head = lax.dynamic_index_in_dim(grad_out, head_idx, 1, False).reshape(
            block_count, BLK, head_dim
        )
        grad_q, lat_part, grad_w = head_pass(w_head, q_head, g_head, key_lat, visible, score_scale)
        grad_q_all = lax.dynamic_update_index_in_dim(grad_q_all, grad_q, head_idx, 1)
        return (grad_q_all, grad_lat + lat_part, grad_w)

    zero_q = jnp.zeros(queries.shape, jnp.bfloat16)
    zero_lat = jnp.zeros(key_lat.shape, jnp.float32)
    zero_w = jnp.zeros((head_count,) + kv_weight.shape[2:], jnp.float32)
    w_piece = lax.all_gather(kv_weight, "fsdp", axis=1, tiled=True)

    def per_head(head_idx, inner_state):
        grad_q_all, grad_lat, grad_w_all = inner_state
        w_head = lax.dynamic_index_in_dim(w_piece[0], head_idx, 0, False)
        grad_q_all, grad_lat, grad_w = run_head(head_idx, w_head, grad_q_all, grad_lat)
        grad_w_all = lax.dynamic_update_index_in_dim(grad_w_all, grad_w, head_idx, 0)
        return (grad_q_all, grad_lat, grad_w_all)

    grad_q_all, grad_lat, grad_w_all = lax.fori_loop(
        0, w_piece.shape[1], per_head, (zero_q, zero_lat, zero_w)
    )
    grad_weight = lax.psum_scatter(
        grad_w_all.astype(jnp.bfloat16), "fsdp", scatter_dimension=0, tiled=True
    ).astype(jnp.float32)[None]
    slot_grads = grad_lat.reshape(block_count, TOPK, BLK, lat_width)
    lat_shares = lax.psum_scatter(slot_grads, "grp", scatter_dimension=3, tiled=True).reshape(
        block_count * TOPK, BLK * lat_share
    )
    flat_pool = pool_index.reshape(-1)
    own_table = (flat_pool[None, :] == jnp.arange(block_count)[:, None]).astype(jnp.float32)
    lat_total = jnp.dot(own_table, lat_shares, precision=lax.Precision.HIGHEST)
    for distance in range(1, DIST + 1):
        slot_ids = block_count + (distance - 1) * slot_cap + jnp.arange(slot_cap)
        pick_table = (flat_pool[None, :] == slot_ids[:, None]).astype(jnp.float32)
        outgoing = jnp.dot(pick_table, lat_shares, precision=lax.Precision.HIGHEST)
        returned = passed_along(outgoing, "fsdp", -distance)
        place_table = (
            send_lists[distance - 1][None, :] == jnp.arange(block_count)[:, None]
        ).astype(jnp.float32)
        lat_total = lat_total + jnp.dot(place_table, returned, precision=lax.Precision.HIGHEST)
    grad_latents = lat_total.reshape(tok_rows, lat_share)
    return (grad_q_all, grad_latents, grad_weight)


def solution(mesh):
    return jax.shard_map(
        per_device,
        mesh=mesh,
        in_specs=(
            P("fsdp", None),
            P("fsdp", "grp", None),
            P("fsdp", "grp", None),
            P("grp", "fsdp", None, None),
            P(),
            P(),
        ),
        out_specs=(P("fsdp", "grp", None), P("fsdp", "grp"), P("grp", "fsdp", None, None)),
        check_vma=False,
    )
```

profile of v0, /device:TPU:120, one launch (start us, length us, event | category | flops | bytes accessed | tf_op | source)
XLA Modules:
  0.0 902.3 jit_solution(2805591895599463974)
XLA Ops:
  11.3 1.9 collective-permute-start
  15.1 4.3 collective-permute-start.1
  21.7 3.1 collective-permute-start.2
  25.7 3.8 collective-permute-start.3
  30.9 6.4 collective-permute-start.4
  39.4 6.1 gather_fusion.1
  49.1 3.9 copy.63
  53.0 2.2 copy.65
  55.1 2.0 collective-permute-start.5
  60.5 5.6 collective-permute-done.5
  66.7 1.8 gather_fusion
  69.8 109.7 %all-gather.2.cloned.1.call-done = bf16[1,32,512,256]{3,2,0,1:T(8,128)(2,1)} async-done(((bf16[1,1,512,256]{3,2,0,1:T(8,128)(2,1)}), bf16[1,32,512,256]{3,2,0,1:T(8,128)(2,1)}) %all-gather.2.cloned.1.call-update) | async-done | bytes 8388624 | tf_op jit(solution)/shard_map/all_gather | solution.py:150
  179.5 495.0 %while.18 = (s32[]{:T(128)}, bf16[256,32,128]{2,0,1:T(8,128)(2,1)}, f32[1024,512]{1,0:T(8,128)S(1)}, bf16[32,512,256]{2,1,0:T(8,128)(2,1)}, bf16[256,32,128]{2,0...) while((s32[]{:T(128)}, bf16[256,32,128]{2,0,1:T(8,128)(2,1)}, ...), condition=%wide.region_17.19_spmd.clone, body=%wide.region_13.18_spmd.clone.sunk | while | flops 910001152 | bytes 22697220 | solution.py:159
  185.5 2.0 fusion.174
  201.0 2.0 fusion.174
  210.4 1.8 fusion.171
  216.5 2.0 fusion.174
  232.0 2.0 fusion.174
  241.4 1.8 fusion.171
  247.4 2.0 fusion.174
  262.9 2.0 fusion.174
  278.4 2.0 fusion.174
  293.9 2.0 fusion.174
  309.3 2.0 fusion.174
  324.8 2.0 fusion.174
  340.3 2.0 fusion.174
  355.8 2.0 fusion.174
  371.2 2.0 fusion.174
  380.6 1.8 fusion.171
  386.7 2.0 fusion.174
  396.1 1.8 fusion.171
  402.1 2.0 fusion.174
  417.6 2.0 fusion.174
  433.1 2.0 fusion.174
  448.5 2.0 fusion.174
  464.0 2.0 fusion.174
  479.5 2.0 fusion.174
  488.9 1.8 fusion.171
  495.0 2.0 fusion.174
  510.4 2.0 fusion.174
  525.9 2.0 fusion.174
  535.2 1.8 fusion.171
  541.3 2.0 fusion.174
  550.7 1.8 fusion.171
  556.8 2.0 fusion.174
  572.3 2.0 fusion.174
  581.7 1.8 fusion.171
  587.7 2.0 fusion.174
  603.2 2.0 fusion.174
  618.7 2.0 fusion.174
  634.1 2.0 fusion.174
  649.6 2.0 fusion.174
  659.0 1.8 fusion.171
  665.1 2.0 fusion.174
  676.7 4.3 copy.67
  680.9 33.7 %reduce-scatter.3.cloned.1.call-done = f32[4,4,64,128]{3,2,1,0:T(8,128)} async-done(((f32[4,4,64,512]{3,2,1,0:T(8,128)}), f32[4,4,64,128]{3,2,1,0:T(8,128)}) %reduce-scatter.3.cloned.1.call-update) | async-done | bytes 524304 | tf_op jit(solution)/shard_map/reduce_scatter | solution.py:166
  716.4 2.8 collective-permute-start.6
  720.7 4.5 collective-permute-start.8
  726.9 2.6 collective-permute-start.9
  731.1 1.9 collective-permute-start.10
  733.6 2.8 collective-permute-start.11
  737.6 4.5 collective-permute-start.7
  745.2 3.6 collective-permute-done.7
  749.8 144.2 %reduce-scatter.5.cloned.1.call-done = bf16[1,512,256]{2,1,0:T(8,128)(2,1)} async-done(((bf16[32,512,256]{2,1,0:T(8,128)(2,1)}), bf16[1,512,256]{2,1,0:T(8,128)(2,1)}) %reduce-scatter.5.cloned.1.call-update) | async-done | bytes 262160 | tf_op jit(solution)/shard_map/reduce_scatter | solution.py:162
  (919 shorter events, 447.3 us)
Async XLA Ops:
  7.2 32.2 %copy-start = (s32[8192]{0:T(1024)S(1)}, s32[8192]{0:T(1024)}, u32[]{:S(2)}) copy-start(s32[8192]{0:T(1024)} %param.14) | copy-start | bytes 98308
  7.2 17.8 %copy-start.5 = (bf16[256,512]{1,0:T(8,128)(2,1)S(1)}, bf16[256,512]{1,0:T(8,128)(2,1)}, u32[]{:S(2)}) copy-start(bf16[256,512]{1,0:T(8,128)(2,1)} %param.10) | copy-start | bytes 786436
  7.2 172.3 %all-gather.2.cloned.1.call-start = ((), (), s32[]{:S(2)}) async-start(), calls=%async_computation.2 | async-start | bytes 8650752 | tf_op jit(solution)/shard_map/all_gather | solution.py:150
  7.9 706.7 %reduce-scatter.3.cloned.1.call-start = ((), (), s32[]{:S(2)}) async-start(), calls=%async_computation.3 | async-start | bytes 2621440 | tf_op jit(solution)/shard_map/reduce_scatter | solution.py:166
  11.3 43.8 %collective-permute-start = (bf16[2,64,512]{2,1,0:T(8,128)(2,1)S(1)}, bf16[2,64,512]{2,1,0:T(8,128)(2,1)S(1)}, u32[]{:S(2)}, u32[]{:S(2)}) collective-permute-start(bf16[2,64,512]{2,1,0:T(8,128)(2,1)S(1)} %broadcast_select_fusion.5), channel_id=1, source_target_pairs={{0,4},{4,8},{8,12},{12,16},{16,20},{20,24},{24,28},{28,32},{32,36}... | collective-permute-start | bytes 393224 | tf_op jit(solution)/shard_map/ppermute | solution.py:17
  15.1 42.7 %collective-permute-start.1 = (bf16[2,64,512]{2,1,0:T(8,128)(2,1)S(1)}, bf16[2,64,512]{2,1,0:T(8,128)(2,1)S(1)}, u32[]{:S(2)}, u32[]{:S(2)}) collective-permute-start(bf16[2,64,512]{2,1,0:T(8,128)(2,1)S(1)} %broadcast_select_fusion.4), channel_id=1, source_target_pairs={{0,8},{4,12},{8,16},{12,20},{16,24},{20,28},{24,32},{28,36},{32,40... | collective-permute-start | bytes 393224 | tf_op jit(solution)/shard_map/ppermute | solution.py:17
  21.7 36.8 %collective-permute-start.2 = (bf16[2,64,512]{2,1,0:T(8,128)(2,1)S(1)}, bf16[2,64,512]{2,1,0:T(8,128)(2,1)S(1)}, u32[]{:S(2)}, u32[]{:S(2)}) collective-permute-start(bf16[2,64,512]{2,1,0:T(8,128)(2,1)S(1)} %broadcast_select_fusion.3), channel_id=1, source_target_pairs={{0,12},{4,16},{8,20},{12,24},{16,28},{20,32},{24,36},{28,40},{32,4... | collective-permute-start | bytes 393224 | tf_op jit(solution)/shard_map/ppermute | solution.py:17
  25.7 33.5 %collective-permute-start.3 = (bf16[2,64,512]{2,1,0:T(8,128)(2,1)S(1)}, bf16[2,64,512]{2,1,0:T(8,128)(2,1)S(1)}, u32[]{:S(2)}, u32[]{:S(2)}) collective-permute-start(bf16[2,64,512]{2,1,0:T(8,128)(2,1)S(1)} %broadcast_select_fusion.2), channel_id=1, source_target_pairs={{0,16},{4,20},{8,24},{12,28},{16,32},{20,36},{24,40},{28,44},{32,4... | collective-permute-start | bytes 393224 | tf_op jit(solution)/shard_map/ppermute | solution.py:17
  30.9 29.0 %collective-permute-start.4 = (bf16[2,64,512]{2,1,0:T(8,128)(2,1)S(1)}, bf16[2,64,512]{2,1,0:T(8,128)(2,1)S(1)}, u32[]{:S(2)}, u32[]{:S(2)}) collective-permute-start(bf16[2,64,512]{2,1,0:T(8,128)(2,1)S(1)} %broadcast_select_fusion.1), channel_id=1, source_target_pairs={{0,20},{4,24},{8,28},{12,32},{16,36},{20,40},{24,44},{28,48},{32,5... | collective-permute-start | bytes 393224 | tf_op jit(solution)/shard_map/ppermute | solution.py:17
  49.1 3.9 copy-start.8
  53.0 2.2 copy-start.9
  55.1 10.9 %collective-permute-start.5 = (bf16[2,64,512]{2,1,0:T(8,128)(2,1)S(1)}, bf16[2,64,512]{2,1,0:T(8,128)(2,1)S(1)}, u32[]{:S(2)}, u32[]{:S(2)}) collective-permute-start(bf16[2,64,512]{2,1,0:T(8,128)(2,1)S(1)} %copy-done.9), channel_id=1, source_target_pairs={{0,24},{4,28},{8,32},{12,36},{16,40},{20,44},{24,48},{28,52},{32,5... | collective-permute-start | bytes 393224 | tf_op jit(solution)/shard_map/ppermute | solution.py:17
  181.5 6.1 copy-start.3
  197.0 6.1 copy-start.3
  212.4 6.1 copy-start.3
  223.3 1.8 copy-start.7
  227.9 6.1 copy-start.3
  243.4 6.1 copy-start.3
  258.9 6.1 copy-start.3
  274.3 6.1 copy-start.3
  289.8 6.1 copy-start.3
  305.3 6.1 copy-start.3
  316.2 1.8 copy-start.7
  320.7 6.1 copy-start.3
  336.2 6.1 copy-start.3
  347.1 1.8 copy-start.7
  351.7 6.1 copy-start.3
  367.2 6.1 copy-start.3
  382.6 6.1 copy-start.3
  393.5 1.8 copy-start.7
  398.1 6.1 copy-start.3
  409.0 1.8 copy-start.7
  413.5 6.1 copy-start.3
  429.0 6.1 copy-start.3
  444.5 6.1 copy-start.3
  460.0 6.1 copy-start.3
  475.4 6.1 copy-start.3
  490.9 6.1 copy-start.3
  506.4 6.1 copy-start.3
  521.8 6.1 copy-start.3
  537.3 6.1 copy-start.3
  552.7 6.1 copy-start.3
  563.6 1.8 copy-start.7
  568.2 6.1 copy-start.3
  579.1 1.8 copy-start.7
  583.7 6.1 copy-start.3
  594.6 1.8 copy-start.7
  599.2 6.1 copy-start.3
  610.0 1.8 copy-start.7
  614.6 6.1 copy-start.3
  625.5 1.8 copy-start.7
  630.1 6.1 copy-start.3
  641.0 1.8 copy-start.7
  645.6 6.1 copy-start.3
  656.4 1.8 copy-start.7
  661.0 6.1 copy-start.3
  675.9 218.1 %reduce-scatter.5.cloned.1.call-start = ((), (), s32[]{:S(2)}) async-start(), calls=%async_computation.4 | async-start | bytes 8650752 | tf_op jit(solution)/shard_map/reduce_scatter | solution.py:162
  714.7 18.4 %copy-start.2 = (f32[4,4,64,128]{3,2,1,0:T(8,128)S(1)}, f32[4,4,64,128]{3,2,1,0:T(8,128)}, u32[]{:S(2)}) copy-start(f32[4,4,64,128]{3,2,1,0:T(8,128)} %reduce-scatter.3.cloned.1.call-done) | copy-start | bytes 1572868
  716.4 21.2 %collective-permute-start.6 = (f32[2,8192]{1,0:T(2,128)S(1)}, f32[2,8192]{1,0:T(2,128)S(1)}, u32[]{:S(2)}, u32[]{:S(2)}) collective-permute-start(f32[2,8192]{1,0:T(2,128)S(1)} %fusion.39), channel_id=1, source_target_pairs={{4,0},{8,4},{12,8},{16,12},{20,16},{24,20},{28,24},{32,28},{36,32}... | collective-permute-start | bytes 196616 | tf_op jit(solution)/shard_map/ppermute | solution.py:17
  720.7 21.7 %collective-permute-start.8 = (f32[2,8192]{1,0:T(2,128)S(1)}, f32[2,8192]{1,0:T(2,128)S(1)}, u32[]{:S(2)}, u32[]{:S(2)}) collective-permute-start(f32[2,8192]{1,0:T(2,128)S(1)} %fusion.35), channel_id=1, source_target_pairs={{12,0},{16,4},{20,8},{24,12},{28,16},{32,20},{36,24},{40,28},{44,3... | collective-permute-start | bytes 196616 | tf_op jit(solution)/shard_map/ppermute | solution.py:17
  726.9 15.8 %collective-permute-start.9 = (f32[2,8192]{1,0:T(2,128)S(1)}, f32[2,8192]{1,0:T(2,128)S(1)}, u32[]{:S(2)}, u32[]{:S(2)}) collective-permute-start(f32[2,8192]{1,0:T(2,128)S(1)} %fusion.33), channel_id=1, source_target_pairs={{16,0},{20,4},{24,8},{28,12},{32,16},{36,20},{40,24},{44,28},{48,3... | collective-permute-start | bytes 196616 | tf_op jit(solution)/shard_map/ppermute | solution.py:17
  731.1 11.9 %collective-permute-start.10 = (f32[2,8192]{1,0:T(2,128)S(1)}, f32[2,8192]{1,0:T(2,128)S(1)}, u32[]{:S(2)}, u32[]{:S(2)}) collective-permute-start(f32[2,8192]{1,0:T(2,128)S(1)} %fusion.31), channel_id=1, source_target_pairs={{20,0},{24,4},{28,8},{32,12},{36,16},{40,20},{44,24},{48,28},{52,3... | collective-permute-start | bytes 196616 | tf_op jit(solution)/shard_map/ppermute | solution.py:17
  733.6 11.3 %collective-permute-start.11 = (f32[2,8192]{1,0:T(2,128)S(1)}, f32[2,8192]{1,0:T(2,128)S(1)}, u32[]{:S(2)}, u32[]{:S(2)}) collective-permute-start(f32[2,8192]{1,0:T(2,128)S(1)} %fusion.29), channel_id=1, source_target_pairs={{24,0},{28,4},{32,8},{36,12},{40,16},{44,20},{48,24},{52,28},{56,3... | collective-permute-start | bytes 196616 | tf_op jit(solution)/shard_map/ppermute | solution.py:17
  737.6 11.2 %collective-permute-start.7 = (f32[2,8192]{1,0:T(2,128)S(1)}, f32[2,8192]{1,0:T(2,128)S(1)}, u32[]{:S(2)}, u32[]{:S(2)}) collective-permute-start(f32[2,8192]{1,0:T(2,128)S(1)} %fusion.37), channel_id=1, source_target_pairs={{8,0},{12,4},{16,8},{20,12},{24,16},{28,20},{32,24},{36,28},{40,32... | collective-permute-start | bytes 196616 | tf_op jit(solution)/shard_map/ppermute | solution.py:17
  (85 other events, 113.4 us)
Sparse Core Ops, SparseCore 0:
  9.6 169.7 all-gather.1
  676.0 38.6 reduce-scatter.2
  717.1 176.8 reduce-scatter.4
where the time goes:
time: 919 us; the launch traced here: 902 us
  matrix products  341 us (37%)
  waiting for transfers between devices  300 us (33%)
  local copies, waits for them, and re-layouts  172 us (19%)
  starting transfers between devices  40.7 us (4%)
  other arithmetic  29.9 us (3%)
  between operations  14.4 us (2%)
    reduce_scatter x1, waiting for transfers between devices, per_device(): lax.psum_scatter(grad_w_all.astype(jnp.bfloat16), 'fsdp', scatter_dimensi...  144 us
    all_gather x1, waiting for transfers between devices, per_device(): w_piece = lax.all_gather(kv_weight, 'fsdp', axis=1, tiled=True)  110 us
    dot_general x32, matrix products, head_pass(): jnp.einsum('qbk,qkd->qbd', probs_low, value_rows, preferred_element_type=...  65 us
    dot_general x32, matrix products, head_pass(): jnp.dot(key_lat, w_head, preferred_element_type=jnp.float32)  57.5 us
    dot_general x32, matrix products, head_pass(): lax.dot_general(grad_kv, w_head, (((1,), (1,)), ((), ())), preferred_elem...  55.5 us
    dynamic_slice x32, local copies, waits for them, and re-layouts, run_head(): lax.dynamic_index_in_dim(grad_out, head_idx, 1, False)  53.8 us
    dot_general x32, matrix products, head_pass(): lax.dot_general(key_lat, grad_kv, (((0,), (0,)), ((), ())), preferred_ele...  53.6 us
    dot_general x32, matrix products, head_pass(): jnp.einsum('qbk,qbd->qkd', probs_low, g_head, preferred_element_type=jnp....  45.6 us
  transfers between devices with their start and end apart: 15, of which 6 were waited for; matrix products, arithmetic and copies ran while one was open for 5% of the time, Pallas kernels for 0%

commit v1 on v0

--- a/solution.py
+++ b/solution.py
@@ -17,45 +17,49 @@
     return lax.ppermute(block, axis, route)
 
 
-def head_pass(w_head, q_head, g_head, key_lat, visible, score_scale):
-    head_width = q_head.shape[-1]
-    block_count = q_head.shape[0]
-    expanded = jnp.dot(key_lat, w_head, preferred_element_type=jnp.float32).astype(jnp.bfloat16)
-    expanded = expanded.reshape(block_count, -1, 2 * head_width)
-    key_rows = expanded[:, :, :head_width]
-    value_rows = expanded[:, :, head_width:]
+def all_heads(w_all, queries, grad_out, key_lat, visible, score_scale, block_count):
+    tok_rows, head_count, head_dim = queries.shape
+    expanded = jnp.einsum(
+        "sl,hlc->hsc", key_lat, w_all, preferred_element_type=jnp.float32
+    ).astype(jnp.bfloat16)
+    expanded = expanded.reshape(head_count, block_count, -1, 2 * head_dim)
+    key_rows = expanded[..., :head_dim]
+    value_rows = expanded[..., head_dim:]
+    q_all = queries.reshape(block_count, BLK, head_count, head_dim)
+    g_all = grad_out.reshape(block_count, BLK, head_count, head_dim)
     scores = (
-        jnp.einsum("qbd,qkd->qbk", q_head, key_rows, preferred_element_type=jnp.float32)
+        jnp.einsum("qbhd,hqkd->hqbk", q_all, key_rows, preferred_element_type=jnp.float32)
         * score_scale
     )
-    scores = jnp.where(visible, scores, NEG_FILL)
+    scores = jnp.where(visible[None], scores, NEG_FILL)
     row_max = jnp.max(scores, axis=-1, keepdims=True)
     exp_scores = jnp.exp(scores - row_max)
     softmax_p = exp_scores / jnp.sum(exp_scores, axis=-1, keepdims=True)
     probs_low = softmax_p.astype(jnp.bfloat16)
-    attended = jnp.einsum("qbk,qkd->qbd", probs_low, value_rows, preferred_element_type=jnp.float32)
-    delta_rows = jnp.sum(g_head.astype(jnp.float32) * attended, axis=-1, keepdims=True)
-    grad_probs = jnp.einsum("qbd,qkd->qbk", g_head, value_rows, preferred_element_type=jnp.float32)
+    attended = jnp.einsum(
+        "hqbk,hqkd->hqbd", probs_low, value_rows, preferred_element_type=jnp.float32
+    )
+    g_t = jnp.transpose(g_all, (2, 0, 1, 3))
+    delta_rows = jnp.sum(g_t.astype(jnp.float32) * attended, axis=-1, keepdims=True)
+    grad_probs = jnp.einsum(
+        "hqbd,hqkd->hqbk", g_t, value_rows, preferred_element_type=jnp.float32
+    )
     grad_scores = (softmax_p * (grad_probs - delta_rows)).astype(jnp.bfloat16)
     grad_q = (
-        jnp.einsum("qbk,qkd->qbd", grad_scores, key_rows, preferred_element_type=jnp.float32)
+        jnp.einsum("hqbk,hqkd->qbhd", grad_scores, key_rows, preferred_element_type=jnp.float32)
         * score_scale
     ).astype(jnp.bfloat16)
     grad_k = (
-        jnp.einsum("qbk,qbd->qkd", grad_scores, q_head, preferred_element_type=jnp.float32)
+        jnp.einsum("hqbk,qbhd->hqkd", grad_scores, q_all, preferred_element_type=jnp.float32)
         * score_scale
     ).astype(jnp.bfloat16)
     grad_v = jnp.einsum(
-        "qbk,qbd->qkd", probs_low, g_head, preferred_element_type=jnp.float32
+        "hqbk,hqbd->hqkd", probs_low, g_t, preferred_element_type=jnp.float32
     ).astype(jnp.bfloat16)
-    grad_kv = jnp.concatenate([grad_k, grad_v], axis=-1).reshape(-1, 2 * head_width)
-    lat_part = lax.dot_general(
-        grad_kv, w_head, (((1,), (1,)), ((), ())), preferred_element_type=jnp.float32
-    )
-    grad_w = lax.dot_general(
-        key_lat, grad_kv, (((0,), (0,)), ((), ())), preferred_element_type=jnp.float32
-    )
-    return (grad_q.reshape(-1, head_width), lat_part, grad_w)
+    grad_kv = jnp.concatenate([grad_k, grad_v], axis=-1).reshape(head_count, -1, 2 * head_dim)
+    lat_part = jnp.einsum("hsc,hlc->sl", grad_kv, w_all, preferred_element_type=jnp.float32)
+    grad_w = jnp.einsum("sl,hsc->hlc", key_lat, grad_kv, preferred_element_type=jnp.float32)
+    return (grad_q.reshape(tok_rows, head_count, head_dim), lat_part, grad_w)
 
 
 def visibility(doc_ids, list_rows, query_start, block_count):
@@ -133,31 +137,9 @@
     key_lat = jnp.take(block_pool, pool_index.reshape(-1), axis=0).reshape(-1, lat_width)
     key_pos, visible = visibility(doc_ids, own_lists, device_pos * tok_rows, block_count)
 
-    def run_head(head_idx, w_head, grad_q_all, grad_lat):
-        q_head = lax.dynamic_index_in_dim(queries, head_idx, 1, False).reshape(
-            block_count, BLK, head_dim
-        )
-        g_head = lax.dynamic_index_in_dim(grad_out, head_idx, 1, False).reshape(
-            block_count, BLK, head_dim
-        )
-        grad_q, lat_part, grad_w = head_pass(w_head, q_head, g_head, key_lat, visible, score_scale)
-        grad_q_all = lax.dynamic_update_index_in_dim(grad_q_all, grad_q, head_idx, 1)
-        return (grad_q_all, grad_lat + lat_part, grad_w)
-
-    zero_q = jnp.zeros(queries.shape, jnp.bfloat16)
-    zero_lat = jnp.zeros(key_lat.shape, jnp.float32)
-    zero_w = jnp.zeros((head_count,) + kv_weight.shape[2:], jnp.float32)
-    w_piece = lax.all_gather(kv_weight, "fsdp", axis=1, tiled=True)
-
-    def per_head(head_idx, inner_state):
-        grad_q_all, grad_lat, grad_w_all = inner_state
-        w_head = lax.dynamic_index_in_dim(w_piece[0], head_idx, 0, False)
-        grad_q_all, grad_lat, grad_w = run_head(head_idx, w_head, grad_q_all, grad_lat)
-        grad_w_all = lax.dynamic_update_index_in_dim(grad_w_all, grad_w, head_idx, 0)
-        return (grad_q_all, grad_lat, grad_w_all)
-
-    grad_q_all, grad_lat, grad_w_all = lax.fori_loop(
-        0, w_piece.shape[1], per_head, (zero_q, zero_lat, zero_w)
+    w_piece = lax.all_gather(kv_weight, "fsdp", axis=1, tiled=True)[0]
+    grad_q_all, grad_lat, grad_w_all = all_heads(
+        w_piece, queries, grad_out, key_lat, visible, score_scale, block_count
     )
     grad_weight = lax.psum_scatter(
         grad_w_all.astype(jnp.bfloat16), "fsdp", scatter_dimension=0, tiled=True

time: 919 us -> 562 us (0.61)
  the two profiles are of different devices: /device:TPU:120 before, /device:TPU:6 now
where the time goes in v1:
time: 562 us; the launch traced here: 556 us
  waiting for transfers between devices  257 us (46%)
  matrix products  122 us (22%)
  local copies, waits for them, and re-layouts  92.2 us (16%)
  starting transfers between devices  41 us (7%)
  other arithmetic  29.8 us (5%)
  between operations  15 us (3%)
    reduce_scatter x1, waiting for transfers between devices, per_device(): lax.psum_scatter(grad_w_all.astype(jnp.bfloat16), 'fsdp', scatter_dimensi...  136 us
    all_gather x1, waiting for transfers between devices, per_device(): w_piece = lax.all_gather(kv_weight, 'fsdp', axis=1, tiled=True)[0]  111 us
    ppermute x12, starting transfers between devices, passed_along(): return lax.ppermute(block, axis, route)  40.9 us
    dot_general x1, matrix products, all_heads(): jnp.einsum('hsc,hlc->sl', grad_kv, w_all, preferred_element_type=jnp.floa...  31.8 us
    dot_general x1, local copies, waits for them, and re-layouts, all_heads(): jnp.einsum('hsc,hlc->sl', grad_kv, w_all, preferred_element_type=jnp.floa...  28.1 us
    concatenate x1, local copies, waits for them, and re-layouts, all_heads(): jnp.concatenate([grad_k, grad_v], axis=-1)  22.7 us
    dot_general x1, matrix products, all_heads(): jnp.einsum('sl,hsc->hlc', key_lat, grad_kv, preferred_element_type=jnp.fl...  17 us
    unnamed x26, local copies, waits for them, and re-layouts  15.8 us
  transfers between devices with their start and end apart: 15, of which 4 were waited for; matrix products, arithmetic and copies ran while one was open for 18% of the time, Pallas kernels for 0%

profile of v1, /device:TPU:6, one launch (start us, length us, event | category | flops | bytes accessed | tf_op | source)
XLA Modules:
  0.0 556.5 jit_solution(12916337724615350167)
XLA Ops:
  7.3 0.7 all-gather.2.cloned.1.call-update
  8.0 1.0 constant_dynamic-slice_fusion.6
  9.7 1.5 gather_fusion.3
  11.3 3.5 collective-permute-start
  15.1 1.5 gather_fusion.4
  16.7 4.8 collective-permute-start.1
  22.2 1.5 gather_fusion.5
  23.8 4.6 collective-permute-start.2
  28.7 1.5 gather_fusion.6
  30.3 3.8 collective-permute-start.3
  34.8 1.5 gather_fusion.7
  36.3 0.7 broadcast_select_fusion.2
  37.0 3.6 collective-permute-start.4
  42.1 1.5 gather_fusion.8
  43.8 5.8 %gather_fusion.1 = s32[1024]{0:T(1024)S(1)} fusion(s32[8192]{0:T(1024)} %param.12, s32[1024]{0:T(1024)S(1)} %get-tuple-element.40), kind=kCustom, calls=%fused_computation.7 | custom fusion | bytes 12288 | tf_op jit(solution)/shard_map/jit(_take)/gather | solution.py:71
  49.6 1.7 gather_fusion.2
  51.8 0.7 constant_dynamic-update-slice_fusion.6
  52.5 3.7 copy.68
  56.2 2.7 collective-permute-start.5
  58.9 0.7 constant_dynamic-update-slice_fusion.5
  59.5 0.7 constant_dynamic-update-slice_fusion.4
  60.2 0.7 constant_dynamic-update-slice_fusion.3
  60.9 1.5 constant_dynamic-update-slice_fusion.2
  62.4 1.6 constant_dynamic-update-slice_fusion.1
  64.0 5.0 collective-permute-done.5
  69.0 0.7 constant_dynamic-update-slice_fusion
  69.7 1.9 gather_fusion
  71.5 1.2 broadcast_select_fusion
  72.7 111.0 %all-gather.2.cloned.1.call-done = bf16[1,32,512,256]{3,2,0,1:T(8,128)(2,1)} async-done(((bf16[1,1,512,256]{3,2,0,1:T(8,128)(2,1)}), bf16[1,32,512,256]{3,2,0,1:T(8,128)(2,1)}) %all-gather.2.cloned.1.call-update) | async-done | bytes 8388624 | tf_op jit(solution)/shard_map/all_gather | solution.py:140
  183.7 14.9 %convolution_convert_fusion = bf16[1024,32,256]{2,0,1:T(8,128)(2,1)} fusion(bf16[1024,512,1]{1,0,2:T(8,128)(2,1)} %bitcast.117, bf16[1,32,512,256]{3,2,0,1:T(8,128)(2,1)} %all-gather.2.cloned.1.call-done), kind=kOutput, calls=%fused_computation.14 | convolution fusion | flops 8598323200 | bytes 26214400 | tf_op jit(solution)/shard_map/sl,hlc->hsc/dot_general | solution.py:22
  198.6 9.1 %fusion.32 = f32[32,4,256,64]{2,3,1,0:T(8,128)} fusion(bf16[4,64,32,128]{3,2,1,0:T(8,128)(2,1)S(1)} %bitcast.91, bf16[32,4,256,256]{3,2,1,0:T(8,128)(2,1)} %bitcast.109), kind=kOutput, calls=%fused_computation.46 | convolution fusion | flops 536870912 | bytes 18874368 | tf_op jit(solution)/shard_map/qbhd,hqkd->hqbk/dot_general | solution.py:31
  207.7 10.5 %fusion.117 = (f32[32,4,64]{2,1,0:T(4,128)S(1)}, f32[32,4,64,256]{3,2,1,0:T(8,128)S(1)}) fusion(f32[32,4,256,64]{2,3,1,0:T(8,128)} %fusion.32, pred[4,64,256]{2,1,0:T(8,128)(4,1)S(1)} %compare_and_fusion), kind=kOutput, calls=%fused_computation.249 | output fusion | flops 12583167 | bytes 16875520 | tf_op jit(solution)/shard_map/sub | solution.py:36
  218.2 3.2 copy-done.7
  221.4 5.3 multiply_reduce_fusion
  226.8 9.9 %convolution_convert_fusion.1 = bf16[32,4,256,128]{2,3,1,0:T(8,128)(2,1)} fusion(bf16[32,4,64,128]{3,2,1,0:T(8,128)(2,1)} %bitcast.114, f32[32,4,64,256]{3,2,1,0:T(8,128)} %copy-done.7, f32[32,4,64]{2,1,0:T(4,128)S(1)} %get-tuple-element.25), kind=kOutput, calls=%fused_computation.34 | convolution fusion | flops 545259520 | bytes 18907136 | tf_op jit(solution)/shard_map/hqbk,hqbd->hqkd/dot_general | solution.py:56
  236.6 8.1 %fusion.8 = bf16[32,4,64,256]{3,2,1,0:T(8,128)(2,1)S(1)} fusion(f32[32,4,64]{2,1,0:T(4,128)S(1)} %multiply_reduce_fusion, f32[32,4,64,256]{3,2,1,0:T(8,128)} %copy-done.7, f32[32,4,64]{2,1,0:T(4,128)S(1)} %get-tuple-element.25, bf16[32,4,64,128]{3,2,1,0:T(8,128)(2,1)} %bitcast.115, bf16[32,4,256,256]{3,2,1,0:T(8,128)(2,1)} %bitcast.111), kind=kOutput, calls=%fused_computation.23 | convolution fusion | flops 545259520 | bytes 23134208 | tf_op jit(solution)/shard_map/hqbd,hqkd->hqbk/dot_general | solution.py:44
  244.7 1.9 copy-done.3
  246.6 6.1 %multiply_convert_fusion = bf16[32,4,256,128]{2,3,1,0:T(8,128)(2,1)} fusion(bf16[32,4,64,256]{3,2,1,0:T(8,128)(2,1)S(1)} %fusion.8, bf16[4,64,32,128]{3,2,1,0:T(8,128)(2,1)S(1)} %bitcast.92), kind=kOutput, calls=%fused_computation.13 | convolution fusion | flops 545259520 | bytes 14680064 | tf_op jit(solution)/shard_map/hqbk,qbhd->hqkd/dot_general | solution.py:53
  252.7 13.7 %pad_maximum_fusion = bf16[32,4,256,256]{2,3,1,0:T(8,128)(2,1)} fusion(bf16[32,4,256,128]{2,3,1,0:T(8,128)(2,1)} %convolution_convert_fusion.1, bf16[32,4,256,128]{2,3,1,0:T(8,128)(2,1)} %multiply_convert_fusion), kind=kLoop, calls=%fused_computation.10 | loop fusion | flops 33554432 | bytes 33554432 | tf_op jit(solution)/shard_map/concatenate | solution.py:59
  266.5 28.1 %copy.81 = bf16[32,4,256,256]{3,0,2,1:T(8,128)(2,1)} copy(bf16[32,4,256,256]{2,3,1,0:T(8,128)(2,1)} %pad_maximum_fusion) | data formatting | bytes 33554432 | tf_op jit(solution)/shard_map/hsc,hlc->sl/dot_general | solution.py:60
  294.5 31.8 %fusion.34 = f32[4,4,64,512]{3,2,1,0:T(8,128)} fusion(bf16[1,32,512,256]{3,2,0,1:T(8,128)(2,1)} %all-gather.2.cloned.1.call-done, bf16[4,4,64,256,32]{3,4,2,1,0:T(8,128)(2,1)} %bitcast.101), kind=kOutput, calls=%fused_computation.48 | convolution fusion | flops 8589934592 | bytes 27262976 | tf_op jit(solution)/shard_map/hsc,hlc->sl/dot_general | solution.py:60
  326.4 22.7 %copy.73 = bf16[32,4,256,256]{3,2,1,0:T(8,128)(2,1)} copy(bf16[32,4,256,256]{2,3,1,0:T(8,128)(2,1)} %pad_maximum_fusion) | data formatting | bytes 33554432 | tf_op jit(solution)/shard_map/concatenate | solution.py:59
  349.1 17.0 %convert_bitcast_fusion = bf16[32,512,256]{1,2,0:T(8,128)(2,1)} fusion(bf16[32,1024,256]{2,1,0:T(8,128)(2,1)} %bitcast.100, bf16[1024,512,1]{1,0,2:T(8,128)(2,1)S(1)} %bitcast.118), kind=kOutput, calls=%fused_computation.28 | convolution fusion | flops 8594128896 | bytes 26214400 | tf_op jit(solution)/shard_map/sl,hsc->hlc/dot_general | solution.py:61
  366.3 6.5 %fusion.24 = bf16[4,64,32,128]{3,1,2,0:T(8,128)(2,1)S(1)} fusion(bf16[32,4,64,256]{3,2,1,0:T(8,128)(2,1)} %copy-done.3, bf16[32,4,256,256]{3,2,1,0:T(8,128)(2,1)} %bitcast.112), kind=kOutput, calls=%fused_computation.44 | convolution fusion | flops 538968064 | bytes 14680064 | tf_op jit(solution)/shard_map/hqbk,hqkd->qbhd/dot_general | solution.py:49
  372.8 2.7 copy.71
  375.5 1.6 fusion.39
  377.1 1.9 collective-permute-start.11
  379.1 1.6 fusion.41
  380.7 1.9 collective-permute-start.10
  382.6 1.6 fusion.43
  384.2 4.9 collective-permute-start.9
  389.2 1.6 fusion.45
  390.8 1.9 collective-permute-start.8
  392.7 1.6 fusion.49
  394.4 4.9 collective-permute-start.6
  399.2 1.6 fusion.51
  400.9 1.6 fusion.47
  402.5 2.3 collective-permute-start.7
  406.1 4.4 collective-permute-done.7
  410.5 0.3 fusion.6
  410.8 0.7 reshape.715
  411.5 135.9 %reduce-scatter.5.cloned.1.call-done = bf16[1,512,256]{1,2,0:T(8,128)(2,1)} async-done(((bf16[32,512,256]{1,2,0:T(8,128)(2,1)}), bf16[1,512,256]{1,2,0:T(8,128)(2,1)}) %reduce-scatter.5.cloned.1.call-update) | async-done | bytes 262160 | tf_op jit(solution)/shard_map/reduce_scatter | solution.py:144
  547.5 1.0 bitcast_convert_fusion
  548.5 1.0 copy.77
  (131 shorter events, 6.2 us)
Async XLA Ops:
  7.2 191.4 %copy-start = (bf16[256,32,128]{2,1,0:T(8,128)(2,1)S(1)}, bf16[256,32,128]{2,1,0:T(8,128)(2,1)}, u32[]{:S(2)}) copy-start(bf16[256,32,128]{2,1,0:T(8,128)(2,1)} %param.9) | copy-start | bytes 6291460
  7.2 44.6 %copy-start.4 = (bf16[256,512]{1,0:T(8,128)(2,1)S(1)}, bf16[256,512]{1,0:T(8,128)(2,1)}, u32[]{:S(2)}) copy-start(bf16[256,512]{1,0:T(8,128)(2,1)} %param.8) | copy-start | bytes 786436
  7.2 42.4 %copy-start.2 = (s32[8192]{0:T(1024)S(1)}, s32[8192]{0:T(1024)}, u32[]{:S(2)}) copy-start(s32[8192]{0:T(1024)} %param.12) | copy-start | bytes 98308
  7.2 176.5 %all-gather.2.cloned.1.call-start = ((), (), s32[]{:S(2)}) async-start(), calls=%async_computation.2 | async-start | bytes 8650752 | tf_op jit(solution)/shard_map/all_gather | solution.py:140
  7.9 367.6 %reduce-scatter.3.cloned.1.call-start = ((), (), s32[]{:S(2)}) async-start(), calls=%async_computation.3 | async-start | bytes 2621440 | tf_op jit(solution)/shard_map/reduce_scatter | solution.py:148
  11.3 44.9 %collective-permute-start = (bf16[2,64,512]{2,1,0:T(8,128)(2,1)S(1)}, bf16[2,64,512]{2,1,0:T(8,128)(2,1)S(1)}, u32[]{:S(2)}, u32[]{:S(2)}) collective-permute-start(bf16[2,64,512]{2,1,0:T(8,128)(2,1)S(1)} %broadcast_select_fusion.6), channel_id=1, source_target_pairs={{0,4},{4,8},{8,12},{12,16},{16,20},{20,24},{24,28},{28,32},{32,36}... | collective-permute-start | bytes 393224 | tf_op jit(solution)/shard_map/ppermute | solution.py:17
  16.7 42.9 %collective-permute-start.1 = (bf16[2,64,512]{2,1,0:T(8,128)(2,1)S(1)}, bf16[2,64,512]{2,1,0:T(8,128)(2,1)S(1)}, u32[]{:S(2)}, u32[]{:S(2)}) collective-permute-start(bf16[2,64,512]{2,1,0:T(8,128)(2,1)S(1)} %broadcast_select_fusion.5), channel_id=1, source_target_pairs={{0,8},{4,12},{8,16},{12,20},{16,24},{20,28},{24,32},{28,36},{32,40... | collective-permute-start | bytes 393224 | tf_op jit(solution)/shard_map/ppermute | solution.py:17
  23.8 36.4 %collective-permute-start.2 = (bf16[2,64,512]{2,1,0:T(8,128)(2,1)S(1)}, bf16[2,64,512]{2,1,0:T(8,128)(2,1)S(1)}, u32[]{:S(2)}, u32[]{:S(2)}) collective-permute-start(bf16[2,64,512]{2,1,0:T(8,128)(2,1)S(1)} %broadcast_select_fusion.4), channel_id=1, source_target_pairs={{0,12},{4,16},{8,20},{12,24},{16,28},{20,32},{24,36},{28,40},{32,4... | collective-permute-start | bytes 393224 | tf_op jit(solution)/shard_map/ppermute | solution.py:17
  30.3 30.6 %collective-permute-start.3 = (bf16[2,64,512]{2,1,0:T(8,128)(2,1)S(1)}, bf16[2,64,512]{2,1,0:T(8,128)(2,1)}, u32[]{:S(2)}, u32[]{:S(2)}) collective-permute-start(bf16[2,64,512]{2,1,0:T(8,128)(2,1)S(1)} %broadcast_select_fusion.3), channel_id=1, source_target_pairs={{0,16},{4,20},{8,24},{12,28},{16,32},{20,36},{24,40},{28,44},{32,4... | collective-permute-start | bytes 393224 | tf_op jit(solution)/shard_map/ppermute | solution.py:17
  37.0 25.4 %collective-permute-start.4 = (bf16[2,64,512]{2,1,0:T(8,128)(2,1)}, bf16[2,64,512]{2,1,0:T(8,128)(2,1)}, u32[]{:S(2)}, u32[]{:S(2)}) collective-permute-start(bf16[2,64,512]{2,1,0:T(8,128)(2,1)} %broadcast_select_fusion.2), channel_id=1, source_target_pairs={{0,20},{4,24},{8,28},{12,32},{16,36},{20,40},{24,44},{28,48},{32,5... | collective-permute-start | bytes 393224 | tf_op jit(solution)/shard_map/ppermute | solution.py:17
  56.2 12.8 %collective-permute-start.5 = (bf16[2,64,512]{2,1,0:T(8,128)(2,1)S(1)}, bf16[2,64,512]{2,1,0:T(8,128)(2,1)S(1)}, u32[]{:S(2)}, u32[]{:S(2)}) collective-permute-start(bf16[2,64,512]{2,1,0:T(8,128)(2,1)S(1)} %broadcast_select_fusion.1), channel_id=1, source_target_pairs={{0,24},{4,28},{8,32},{12,36},{16,40},{20,44},{24,48},{28,52},{32,5... | collective-permute-start | bytes 393224 | tf_op jit(solution)/shard_map/ppermute | solution.py:17
  207.7 13.7 %copy-start.5 = (bf16[256,32,128]{2,0,1:T(8,128)(2,1)S(1)}, bf16[256,32,128]{2,0,1:T(8,128)(2,1)}, u32[]{:S(2)}) copy-start(bf16[256,32,128]{2,0,1:T(8,128)(2,1)} %copy.68) | copy-start | bytes 6291460
  218.2 3.2 copy-start.7
  244.7 1.9 copy-start.3
  326.3 22.8 %copy-start.6 = (bf16[16,64,512]{2,1,0:T(8,128)(2,1)S(1)}, bf16[16,64,512]{2,1,0:T(8,128)(2,1)}, u32[]{:S(2)}) copy-start(bf16[16,64,512]{2,1,0:T(8,128)(2,1)} %broadcast_select_fusion) | copy-start | bytes 3145732
  326.3 221.1 %reduce-scatter.5.cloned.1.call-start = ((), (), s32[]{:S(2)}) async-start(), calls=%async_computation.4 | async-start | bytes 8650752 | tf_op jit(solution)/shard_map/reduce_scatter | solution.py:144
  366.3 183.2 %copy-start.1 = (bf16[256,32,128]{2,1,0:T(8,128)(2,1)S(1)}, bf16[256,32,128]{2,1,0:T(8,128)(2,1)}, u32[]{:S(2)}) copy-start(bf16[256,32,128]{2,1,0:T(8,128)(2,1)} %param.9) | copy-start | bytes 6291460
  377.1 27.9 %collective-permute-start.11 = (f32[2,8192]{1,0:T(2,128)S(1)}, f32[2,8192]{1,0:T(2,128)S(1)}, u32[]{:S(2)}, u32[]{:S(2)}) collective-permute-start(f32[2,8192]{1,0:T(2,128)S(1)} %fusion.39), channel_id=1, source_target_pairs={{24,0},{28,4},{32,8},{36,12},{40,16},{44,20},{48,24},{52,28},{56,3... | collective-permute-start | bytes 196616 | tf_op jit(solution)/shard_map/ppermute | solution.py:17
  380.7 24.6 %collective-permute-start.10 = (f32[2,8192]{1,0:T(2,128)S(1)}, f32[2,8192]{1,0:T(2,128)S(1)}, u32[]{:S(2)}, u32[]{:S(2)}) collective-permute-start(f32[2,8192]{1,0:T(2,128)S(1)} %fusion.41), channel_id=1, source_target_pairs={{20,0},{24,4},{28,8},{32,12},{36,16},{40,20},{44,24},{48,28},{52,3... | collective-permute-start | bytes 196616 | tf_op jit(solution)/shard_map/ppermute | solution.py:17
  384.2 21.3 %collective-permute-start.9 = (f32[2,8192]{1,0:T(2,128)S(1)}, f32[2,8192]{1,0:T(2,128)S(1)}, u32[]{:S(2)}, u32[]{:S(2)}) collective-permute-start(f32[2,8192]{1,0:T(2,128)S(1)} %fusion.43), channel_id=1, source_target_pairs={{16,0},{20,4},{24,8},{28,12},{32,16},{36,20},{40,24},{44,28},{48,3... | collective-permute-start | bytes 196616 | tf_op jit(solution)/shard_map/ppermute | solution.py:17
  390.8 15.0 %collective-permute-start.8 = (f32[2,8192]{1,0:T(2,128)S(1)}, f32[2,8192]{1,0:T(2,128)S(1)}, u32[]{:S(2)}, u32[]{:S(2)}) collective-permute-start(f32[2,8192]{1,0:T(2,128)S(1)} %fusion.45), channel_id=1, source_target_pairs={{12,0},{16,4},{20,8},{24,12},{28,16},{32,20},{36,24},{40,28},{44,3... | collective-permute-start | bytes 196616 | tf_op jit(solution)/shard_map/ppermute | solution.py:17
  394.4 8.1 %collective-permute-start.6 = (f32[2,8192]{1,0:T(2,128)S(1)}, f32[2,8192]{1,0:T(2,128)S(1)}, u32[]{:S(2)}, u32[]{:S(2)}) collective-permute-start(f32[2,8192]{1,0:T(2,128)S(1)} %fusion.49), channel_id=1, source_target_pairs={{4,0},{8,4},{12,8},{16,12},{20,16},{24,20},{28,24},{32,28},{36,32}... | collective-permute-start | bytes 196616 | tf_op jit(solution)/shard_map/ppermute | solution.py:17
  402.5 8.0 %collective-permute-start.7 = (f32[2,8192]{1,0:T(2,128)S(1)}, f32[2,8192]{1,0:T(2,128)S(1)}, u32[]{:S(2)}, u32[]{:S(2)}) collective-permute-start(f32[2,8192]{1,0:T(2,128)S(1)} %fusion.47), channel_id=1, source_target_pairs={{8,0},{12,4},{16,8},{20,12},{24,16},{28,20},{32,24},{36,28},{40,32... | collective-permute-start | bytes 196616 | tf_op jit(solution)/shard_map/ppermute | solution.py:17
Sparse Core Ops, SparseCore 0:
  9.7 174.0 all-gather.1
  326.5 34.6 reduce-scatter.2
  366.3 181.0 reduce-scatter.4

commit v2 on v1

--- a/solution.py
+++ b/solution.py
@@ -137,13 +137,14 @@
     key_lat = jnp.take(block_pool, pool_index.reshape(-1), axis=0).reshape(-1, lat_width)
     key_pos, visible = visibility(doc_ids, own_lists, device_pos * tok_rows, block_count)
 
-    w_piece = lax.all_gather(kv_weight, "fsdp", axis=1, tiled=True)[0]
+    fsdp_size = lax.axis_size("fsdp")
+    w_copies = jnp.broadcast_to(kv_weight[0], (fsdp_size,) + kv_weight.shape[2:])
+    w_piece = lax.all_to_all(w_copies, "fsdp", 0, 0, tiled=True)
     grad_q_all, grad_lat, grad_w_all = all_heads(
         w_piece, queries, grad_out, key_lat, visible, score_scale, block_count
     )
-    grad_weight = lax.psum_scatter(
-        grad_w_all.astype(jnp.bfloat16), "fsdp", scatter_dimension=0, tiled=True
-    ).astype(jnp.float32)[None]
+    run_partials = lax.all_to_all(grad_w_all.astype(jnp.bfloat16), "fsdp", 0, 0, tiled=True)
+    grad_weight = jnp.sum(run_partials.astype(jnp.float32), axis=0, keepdims=True)[None]
     slot_grads = grad_lat.reshape(block_count, TOPK, BLK, lat_width)
     lat_shares = lax.psum_scatter(slot_grads, "grp", scatter_dimension=3, tiled=True).reshape(
         block_count * TOPK, BLK * lat_share

time: 562 us -> 481 us (0.86)
  the two profiles are of different devices: /device:TPU:6 before, /device:TPU:120 now
where the time goes in v2:
time: 481 us; the launch traced here: 474 us
  waiting for transfers between devices  155 us (32%)
  matrix products  122 us (25%)
  local copies, waits for them, and re-layouts  91.2 us (19%)
  starting transfers between devices  55.7 us (12%)
  other arithmetic  35.5 us (7%)
  between operations  15 us (3%)
    ppermute x12, waiting for transfers between devices, passed_along(): return lax.ppermute(block, axis, route)  114 us
    reduce_scatter x1, waiting for transfers between devices, per_device(): lax.psum_scatter(slot_grads, 'grp', scatter_dimension=3, tiled=True)  41.5 us
    ppermute x12, starting transfers between devices, passed_along(): return lax.ppermute(block, axis, route)  38.5 us
    dot_general x1, matrix products, all_heads(): jnp.einsum('hsc,hlc->sl', grad_kv, w_all, preferred_element_type=jnp.floa...  31.7 us
    dot_general x1, local copies, waits for them, and re-layouts, all_heads(): jnp.einsum('hsc,hlc->sl', grad_kv, w_all, preferred_element_type=jnp.floa...  28.1 us
    concatenate x1, local copies, waits for them, and re-layouts, all_heads(): jnp.concatenate([grad_k, grad_v], axis=-1)  22.6 us
    dot_general x1, matrix products, all_heads(): jnp.einsum('sl,hsc->hlc', key_lat, grad_kv, preferred_element_type=jnp.fl...  17 us
    unnamed x28, local copies, waits for them, and re-layouts  15.8 us
  transfers between devices with their start and end apart: 15, of which 9 were waited for; matrix products, arithmetic and copies ran while one was open for 18% of the time, Pallas kernels for 0%

profile of v2, /device:TPU:120, one launch (start us, length us, event | category | flops | bytes accessed | tf_op | source)
XLA Modules:
  0.0 474.3 jit_solution(8637719795201963846)
XLA Ops:
  7.2 5.3 %broadcast_in_dim.109 = bf16[32,512,256]{2,1,0:T(8,128)(2,1)} broadcast(bf16[512,256]{1,0:T(8,128)(2,1)} %bitcast.118), dimensions={1,2} | broadcast | bytes 8650752 | tf_op jit(solution)/shard_map/broadcast_in_dim | solution.py:141
  12.5 8.1 %all-to-all-start = ((bf16[32,512,256]{2,1,0:T(8,128)(2,1)}), bf16[32,512,256]{2,1,0:T(8,128)(2,1)}, u32[]{:S(2)}, u32[]{:S(2)}) async-start(bf16[32,512,256]{2,1,0:T(8,128)(2,1)} %broadcast_in_dim.109), calls=%async_computation | async-start | bytes 16777216 | tf_op jit(solution)/shard_map/all_to_all | solution.py:142
  22.0 3.4 collective-permute-start
  26.3 4.3 collective-permute-start.1
  31.9 2.8 collective-permute-start.2
  35.6 3.4 collective-permute-start.3
  40.3 0.7 broadcast_select_fusion.2
  41.0 5.8 %collective-permute-start.4 = (bf16[2,64,512]{2,1,0:T(8,128)(2,1)}, bf16[2,64,512]{2,1,0:T(8,128)(2,1)}, u32[]{:S(2)}, u32[]{:S(2)}) collective-permute-start(bf16[2,64,512]{2,1,0:T(8,128)(2,1)} %broadcast_select_fusion.2), channel_id=1, source_target_pairs={{0,20},{4,24},{8,28},{12,32},{16,36},{20,40},{24,44},{28,48},{32,5... | collective-permute-start | bytes 393224 | tf_op jit(solution)/shard_map/ppermute | solution.py:17
  49.0 6.2 %gather_fusion.1 = s32[1024]{0:T(1024)S(1)} fusion(s32[8192]{0:T(1024)S(1)} %copy-done.2, s32[1024]{0:T(1024)S(1)} %get-tuple-element.34), kind=kCustom, calls=%fused_computation.7 | custom fusion | bytes 12288 | tf_op jit(solution)/shard_map/jit(_take)/gather | solution.py:71
  55.2 1.7 gather_fusion.2
  57.2 0.7 broadcast_select_fusion.1
  58.0 0.7 constant_dynamic-update-slice_fusion.6
  58.7 3.7 copy.64
  62.6 89.4 %collective-permute-done = bf16[2,64,512]{2,1,0:T(8,128)(2,1)S(1)} collective-permute-done((bf16[2,64,512]{2,1,0:T(8,128)(2,1)S(1)}, bf16[2,64,512]{2,1,0:T(8,128)(2,1)S(1)}, u32[]{:S(2)}, u32[]{:S(2)}) %collective-permute-start) | collective-permute-done | bytes 131104 | tf_op jit(solution)/shard_map/ppermute | solution.py:17
  151.9 2.1 collective-permute-start.5
  154.0 0.7 constant_dynamic-update-slice_fusion.5
  154.7 0.6 constant_dynamic-update-slice_fusion.4
  155.4 2.2 collective-permute-done.2
  157.6 0.7 constant_dynamic-update-slice_fusion.3
  158.2 2.1 collective-permute-done.3
  160.4 1.6 constant_dynamic-update-slice_fusion.2
  161.9 1.3 collective-permute-done.4
  163.3 1.6 constant_dynamic-update-slice_fusion.1
  164.8 0.7 constant_dynamic-update-slice_fusion
  165.5 1.8 gather_fusion
  167.3 1.2 broadcast_select_fusion
  168.6 1.3 bitcast_select_fusion.4
  169.9 14.9 %convolution_convert_fusion = bf16[1024,32,256]{2,0,1:T(8,128)(2,1)} fusion(bf16[32,512,256]{2,1,0:T(8,128)(2,1)} %all-to-all-done, bf16[1024,512]{1,0:T(8,128)(2,1)} %bitcast_select_fusion.4), kind=kOutput, calls=%fused_computation.15 | convolution fusion | flops 8598323200 | bytes 26214400 | tf_op jit(solution)/shard_map/sl,hlc->hsc/dot_general | solution.py:22
  184.7 9.1 %fusion.31 = f32[32,4,256,64]{2,3,1,0:T(8,128)} fusion(bf16[4,64,32,128]{3,2,1,0:T(8,128)(2,1)S(1)} %bitcast.90, bf16[32,4,256,256]{3,2,1,0:T(8,128)(2,1)} %bitcast.108), kind=kOutput, calls=%fused_computation.46 | convolution fusion | flops 536870912 | bytes 18874368 | tf_op jit(solution)/shard_map/qbhd,hqkd->hqbk/dot_general | solution.py:31
  193.9 10.5 %fusion.117 = (f32[32,4,64]{2,1,0:T(4,128)S(1)}, f32[32,4,64,256]{3,2,1,0:T(8,128)S(1)}) fusion(f32[32,4,256,64]{2,3,1,0:T(8,128)} %fusion.31, pred[4,64,256]{2,1,0:T(8,128)(4,1)S(1)} %compare_and_fusion), kind=kOutput, calls=%fused_computation.250 | output fusion | flops 12583167 | bytes 16875520 | tf_op jit(solution)/shard_map/sub | solution.py:36
  204.4 3.2 copy-done.8
  207.6 5.6 %multiply_reduce_fusion = f32[32,4,64]{2,1,0:T(4,128)S(1)} fusion(bf16[32,4,64,128]{3,2,1,0:T(8,128)(2,1)S(1)} %bitcast.116, bf16[32,4,256,256]{3,2,1,0:T(8,128)(2,1)} %bitcast.109, f32[32,4,64,256]{3,2,1,0:T(8,128)S(1)} %get-tuple-element.20, f32[32,4,64]{2,1,0:T(4,128)S(1)} %get-tuple-element.19), kind=kOutput, calls=%fused_computation.38 | convolution fusion | flops 544202752 | bytes 18939904 | tf_op jit(solution)/shard_map/hqbk,hqkd->hqbd/dot_general | solution.py:39
  213.2 9.9 %convolution_convert_fusion.1 = bf16[32,4,256,128]{2,3,1,0:T(8,128)(2,1)} fusion(bf16[32,4,64,128]{3,2,1,0:T(8,128)(2,1)} %bitcast.114, f32[32,4,64,256]{3,2,1,0:T(8,128)} %copy-done.8, f32[32,4,64]{2,1,0:T(4,128)S(1)} %get-tuple-element.19), kind=kOutput, calls=%fused_computation.34 | convolution fusion | flops 545259520 | bytes 18907136 | tf_op jit(solution)/shard_map/hqbk,hqbd->hqkd/dot_general | solution.py:56
  223.1 8.1 %fusion.8 = bf16[32,4,64,256]{3,2,1,0:T(8,128)(2,1)S(1)} fusion(f32[32,4,64]{2,1,0:T(4,128)S(1)} %multiply_reduce_fusion, f32[32,4,64,256]{3,2,1,0:T(8,128)} %copy-done.8, f32[32,4,64]{2,1,0:T(4,128)S(1)} %get-tuple-element.19, bf16[32,4,64,128]{3,2,1,0:T(8,128)(2,1)} %bitcast.115, bf16[32,4,256,256]{3,2,1,0:T(8,128)(2,1)} %bitcast.110), kind=kOutput, calls=%fused_computation.24 | convolution fusion | flops 545259520 | bytes 23134208 | tf_op jit(solution)/shard_map/hqbd,hqkd->hqbk/dot_general | solution.py:44
  231.1 1.9 copy-done.3
  233.1 6.1 %multiply_convert_fusion = bf16[32,4,256,128]{2,3,1,0:T(8,128)(2,1)} fusion(bf16[32,4,64,256]{3,2,1,0:T(8,128)(2,1)S(1)} %fusion.8, bf16[4,64,32,128]{3,2,1,0:T(8,128)(2,1)S(1)} %bitcast.91), kind=kOutput, calls=%fused_computation.14 | convolution fusion | flops 545259520 | bytes 14680064 | tf_op jit(solution)/shard_map/hqbk,qbhd->hqkd/dot_general | solution.py:53
  239.2 13.7 %pad_maximum_fusion = bf16[32,4,256,256]{2,3,1,0:T(8,128)(2,1)} fusion(bf16[32,4,256,128]{2,3,1,0:T(8,128)(2,1)} %convolution_convert_fusion.1, bf16[32,4,256,128]{2,3,1,0:T(8,128)(2,1)} %multiply_convert_fusion), kind=kLoop, calls=%fused_computation.10 | loop fusion | flops 33554432 | bytes 33554432 | tf_op jit(solution)/shard_map/concatenate | solution.py:59
  252.9 28.1 %copy.77 = bf16[32,4,256,256]{3,0,2,1:T(8,128)(2,1)} copy(bf16[32,4,256,256]{2,3,1,0:T(8,128)(2,1)} %pad_maximum_fusion) | data formatting | bytes 33554432 | tf_op jit(solution)/shard_map/hsc,hlc->sl/dot_general | solution.py:60
  281.0 22.6 %copy.69 = bf16[32,4,256,256]{3,2,1,0:T(8,128)(2,1)} copy(bf16[32,4,256,256]{2,3,1,0:T(8,128)(2,1)} %pad_maximum_fusion) | data formatting | bytes 33554432 | tf_op jit(solution)/shard_map/concatenate | solution.py:59
  303.6 17.0 %convert_bitcast_fusion = bf16[32,512,256]{1,2,0:T(8,128)(2,1)} fusion(bf16[32,1024,256]{2,1,0:T(8,128)(2,1)} %bitcast.100, bf16[1024,512,1]{1,0,2:T(8,128)(2,1)S(1)} %bitcast.117), kind=kOutput, calls=%fused_computation.28 | convolution fusion | flops 8594128896 | bytes 26214400 | tf_op jit(solution)/shard_map/sl,hsc->hlc/dot_general | solution.py:61
  320.6 9.1 %all-to-all-start.1 = ((bf16[32,512,256]{1,2,0:T(8,128)(2,1)}), bf16[32,512,256]{1,2,0:T(8,128)(2,1)}, u32[]{:S(2)}, u32[]{:S(2)}) async-start(bf16[32,512,256]{1,2,0:T(8,128)(2,1)} %convert_bitcast_fusion), calls=%async_computation.2 | async-start | bytes 16777216 | tf_op jit(solution)/shard_map/all_to_all | solution.py:146
  329.7 31.7 %fusion.33 = f32[4,4,64,512]{3,2,1,0:T(8,128)} fusion(bf16[32,512,256]{2,1,0:T(8,128)(2,1)} %all-to-all-done, bf16[4,4,64,256,32]{3,4,2,1,0:T(8,128)(2,1)} %bitcast.99), kind=kOutput, calls=%fused_computation.48 | convolution fusion | flops 8589934592 | bytes 27262976 | tf_op jit(solution)/shard_map/hsc,hlc->sl/dot_general | solution.py:60
  361.5 6.4 %fusion.23 = bf16[4,64,32,128]{3,1,2,0:T(8,128)(2,1)S(1)} fusion(bf16[32,4,64,256]{3,2,1,0:T(8,128)(2,1)} %copy-done.3, bf16[32,4,256,256]{3,2,1,0:T(8,128)(2,1)} %bitcast.111), kind=kOutput, calls=%fused_computation.44 | convolution fusion | flops 538968064 | bytes 14680064 | tf_op jit(solution)/shard_map/hqbk,hqkd->qbhd/dot_general | solution.py:49
  367.9 2.7 copy.67
  370.6 41.5 %reduce-scatter.2.cloned.1.call-done = f32[4,4,64,128]{3,2,1,0:T(8,128)} async-done(((f32[4,4,64,512]{3,2,1,0:T(8,128)}), f32[4,4,64,128]{3,2,1,0:T(8,128)}) %reduce-scatter.2.cloned.1.call-update) | async-done | bytes 524304 | tf_op jit(solution)/shard_map/reduce_scatter | solution.py:149
  412.1 1.6 fusion.39
  413.7 4.8 %collective-permute-start.11 = (f32[2,8192]{1,0:T(2,128)S(1)}, f32[2,8192]{1,0:T(2,128)S(1)}, u32[]{:S(2)}, u32[]{:S(2)}) collective-permute-start(f32[2,8192]{1,0:T(2,128)S(1)} %fusion.39), channel_id=1, source_target_pairs={{24,0},{28,4},{32,8},{36,12},{40,16},{44,20},{48,24},{52,28},{56,3... | collective-permute-start | bytes 196616 | tf_op jit(solution)/shard_map/ppermute | solution.py:17
  418.6 1.6 fusion.41
  420.2 1.9 collective-permute-start.10
  422.1 1.6 fusion.43
  423.7 1.9 collective-permute-start.9
  425.7 1.6 fusion.45
  427.3 4.3 collective-permute-start.8
  431.6 1.6 fusion.49
  433.2 1.9 collective-permute-start.6
  435.2 1.6 fusion.51
  436.8 1.6 fusion.47
  438.4 11.4 %collective-permute-done.6 = f32[2,8192]{1,0:T(2,128)S(1)} collective-permute-done((f32[2,8192]{1,0:T(2,128)S(1)}, f32[2,8192]{1,0:T(2,128)S(1)}, u32[]{:S(2)}, u32[]{:S(2)}) %collective-permute-start.6) | collective-permute-done | bytes 65568 | tf_op jit(solution)/shard_map/ppermute | solution.py:17
  449.8 1.9 collective-permute-start.7
  452.5 3.9 collective-permute-done.9
  456.8 3.6 collective-permute-done.7
  460.7 0.7 reshape.692
  461.5 4.7 convert_reduce_fusion
  466.2 1.0 copy.73
  (135 shorter events, 9.9 us)
Async XLA Ops:
  7.2 177.6 %copy-start = (bf16[256,32,128]{2,1,0:T(8,128)(2,1)S(1)}, bf16[256,32,128]{2,1,0:T(8,128)(2,1)}, u32[]{:S(2)}) copy-start(bf16[256,32,128]{2,1,0:T(8,128)(2,1)} %param.9) | copy-start | bytes 6291460
  12.4 8.1 %copy-start.7 = (s32[128,4]{0,1:T(4,128)S(1)}, s32[128,4]{0,1:T(4,128)}, u32[]{:S(2)}) copy-start(s32[128,4]{0,1:T(4,128)} %param.13) | copy-start | bytes 6148
  12.4 8.9 %copy-start.4 = (bf16[256,512]{1,0:T(8,128)(2,1)S(1)}, bf16[256,512]{1,0:T(8,128)(2,1)}, u32[]{:S(2)}) copy-start(bf16[256,512]{1,0:T(8,128)(2,1)} %param.8) | copy-start | bytes 786436
  12.5 36.6 %copy-start.2 = (s32[8192]{0:T(1024)S(1)}, s32[8192]{0:T(1024)}, u32[]{:S(2)}) copy-start(s32[8192]{0:T(1024)} %param.12) | copy-start | bytes 98308
  12.5 157.4 %all-to-all-start = ((bf16[32,512,256]{2,1,0:T(8,128)(2,1)}), bf16[32,512,256]{2,1,0:T(8,128)(2,1)}, u32[]{:S(2)}, u32[]{:S(2)}) async-start(bf16[32,512,256]{2,1,0:T(8,128)(2,1)} %broadcast_in_dim.109), calls=%async_computation | async-start | bytes 16777216 | tf_op jit(solution)/shard_map/all_to_all | solution.py:142
  22.0 129.9 %collective-permute-start = (bf16[2,64,512]{2,1,0:T(8,128)(2,1)S(1)}, bf16[2,64,512]{2,1,0:T(8,128)(2,1)S(1)}, u32[]{:S(2)}, u32[]{:S(2)}) collective-permute-start(bf16[2,64,512]{2,1,0:T(8,128)(2,1)S(1)} %broadcast_select_fusion.6), channel_id=1, source_target_pairs={{0,4},{4,8},{8,12},{12,16},{16,20},{20,24},{24,28},{28,32},{32,36}... | collective-permute-start | bytes 393224 | tf_op jit(solution)/shard_map/ppermute | solution.py:17
  26.3 128.4 %collective-permute-start.1 = (bf16[2,64,512]{2,1,0:T(8,128)(2,1)S(1)}, bf16[2,64,512]{2,1,0:T(8,128)(2,1)S(1)}, u32[]{:S(2)}, u32[]{:S(2)}) collective-permute-start(bf16[2,64,512]{2,1,0:T(8,128)(2,1)S(1)} %broadcast_select_fusion.5), channel_id=1, source_target_pairs={{0,8},{4,12},{8,16},{12,20},{16,24},{20,28},{24,32},{28,36},{32,40... | collective-permute-start | bytes 393224 | tf_op jit(solution)/shard_map/ppermute | solution.py:17
  31.9 125.6 %collective-permute-start.2 = (bf16[2,64,512]{2,1,0:T(8,128)(2,1)S(1)}, bf16[2,64,512]{2,1,0:T(8,128)(2,1)S(1)}, u32[]{:S(2)}, u32[]{:S(2)}) collective-permute-start(bf16[2,64,512]{2,1,0:T(8,128)(2,1)S(1)} %broadcast_select_fusion.4), channel_id=1, source_target_pairs={{0,12},{4,16},{8,20},{12,24},{16,28},{20,32},{24,36},{28,40},{32,4... | collective-permute-start | bytes 393224 | tf_op jit(solution)/shard_map/ppermute | solution.py:17
  35.6 124.7 %collective-permute-start.3 = (bf16[2,64,512]{2,1,0:T(8,128)(2,1)S(1)}, bf16[2,64,512]{2,1,0:T(8,128)(2,1)}, u32[]{:S(2)}, u32[]{:S(2)}) collective-permute-start(bf16[2,64,512]{2,1,0:T(8,128)(2,1)S(1)} %broadcast_select_fusion.3), channel_id=1, source_target_pairs={{0,16},{4,20},{8,24},{12,28},{16,32},{20,36},{24,40},{28,44},{32,4... | collective-permute-start | bytes 393224 | tf_op jit(solution)/shard_map/ppermute | solution.py:17
  41.0 122.3 %collective-permute-start.4 = (bf16[2,64,512]{2,1,0:T(8,128)(2,1)}, bf16[2,64,512]{2,1,0:T(8,128)(2,1)}, u32[]{:S(2)}, u32[]{:S(2)}) collective-permute-start(bf16[2,64,512]{2,1,0:T(8,128)(2,1)} %broadcast_select_fusion.2), channel_id=1, source_target_pairs={{0,20},{4,24},{8,28},{12,32},{16,36},{20,40},{24,44},{28,48},{32,5... | collective-permute-start | bytes 393224 | tf_op jit(solution)/shard_map/ppermute | solution.py:17
  151.9 12.9 %collective-permute-start.5 = (bf16[2,64,512]{2,1,0:T(8,128)(2,1)}, bf16[2,64,512]{2,1,0:T(8,128)(2,1)S(1)}, u32[]{:S(2)}, u32[]{:S(2)}) collective-permute-start(bf16[2,64,512]{2,1,0:T(8,128)(2,1)} %broadcast_select_fusion.1), channel_id=1, source_target_pairs={{0,24},{4,28},{8,32},{12,36},{16,40},{20,44},{24,48},{28,52},{32,5... | collective-permute-start | bytes 393224 | tf_op jit(solution)/shard_map/ppermute | solution.py:17
  193.9 13.7 %copy-start.5 = (bf16[256,32,128]{2,0,1:T(8,128)(2,1)S(1)}, bf16[256,32,128]{2,0,1:T(8,128)(2,1)}, u32[]{:S(2)}) copy-start(bf16[256,32,128]{2,0,1:T(8,128)(2,1)} %copy.64) | copy-start | bytes 6291460
  204.4 3.2 copy-start.8
  231.1 2.0 copy-start.3
  281.0 22.6 %copy-start.6 = (bf16[16,64,512]{2,1,0:T(8,128)(2,1)S(1)}, bf16[16,64,512]{2,1,0:T(8,128)(2,1)}, u32[]{:S(2)}) copy-start(bf16[16,64,512]{2,1,0:T(8,128)(2,1)} %broadcast_select_fusion) | copy-start | bytes 3145732
  320.6 140.9 %all-to-all-start.1 = ((bf16[32,512,256]{1,2,0:T(8,128)(2,1)}), bf16[32,512,256]{1,2,0:T(8,128)(2,1)}, u32[]{:S(2)}, u32[]{:S(2)}) async-start(bf16[32,512,256]{1,2,0:T(8,128)(2,1)} %convert_bitcast_fusion), calls=%async_computation.2 | async-start | bytes 16777216 | tf_op jit(solution)/shard_map/all_to_all | solution.py:146
  329.7 82.4 %reduce-scatter.2.cloned.1.call-start = ((), (), s32[]{:S(2)}) async-start(), calls=%async_computation.3 | async-start | bytes 2621440 | tf_op jit(solution)/shard_map/reduce_scatter | solution.py:149
  367.9 99.3 %copy-start.1 = (bf16[256,32,128]{2,1,0:T(8,128)(2,1)S(1)}, bf16[256,32,128]{2,1,0:T(8,128)(2,1)}, u32[]{:S(2)}) copy-start(bf16[256,32,128]{2,1,0:T(8,128)(2,1)} %param.9) | copy-start | bytes 6291460
  413.7 38.2 %collective-permute-start.11 = (f32[2,8192]{1,0:T(2,128)S(1)}, f32[2,8192]{1,0:T(2,128)S(1)}, u32[]{:S(2)}, u32[]{:S(2)}) collective-permute-start(f32[2,8192]{1,0:T(2,128)S(1)} %fusion.39), channel_id=1, source_target_pairs={{24,0},{28,4},{32,8},{36,12},{40,16},{44,20},{48,24},{52,28},{56,3... | collective-permute-start | bytes 196616 | tf_op jit(solution)/shard_map/ppermute | solution.py:17
  420.2 32.0 %collective-permute-start.10 = (f32[2,8192]{1,0:T(2,128)S(1)}, f32[2,8192]{1,0:T(2,128)S(1)}, u32[]{:S(2)}, u32[]{:S(2)}) collective-permute-start(f32[2,8192]{1,0:T(2,128)S(1)} %fusion.41), channel_id=1, source_target_pairs={{20,0},{24,4},{28,8},{32,12},{36,16},{40,20},{44,24},{48,28},{52,3... | collective-permute-start | bytes 196616 | tf_op jit(solution)/shard_map/ppermute | solution.py:17
  423.7 32.6 %collective-permute-start.9 = (f32[2,8192]{1,0:T(2,128)S(1)}, f32[2,8192]{1,0:T(2,128)S(1)}, u32[]{:S(2)}, u32[]{:S(2)}) collective-permute-start(f32[2,8192]{1,0:T(2,128)S(1)} %fusion.43), channel_id=1, source_target_pairs={{16,0},{20,4},{24,8},{28,12},{32,16},{36,20},{40,24},{44,28},{48,3... | collective-permute-start | bytes 196616 | tf_op jit(solution)/shard_map/ppermute | solution.py:17
  427.3 29.3 %collective-permute-start.8 = (f32[2,8192]{1,0:T(2,128)S(1)}, f32[2,8192]{1,0:T(2,128)S(1)}, u32[]{:S(2)}, u32[]{:S(2)}) collective-permute-start(f32[2,8192]{1,0:T(2,128)S(1)} %fusion.45), channel_id=1, source_target_pairs={{12,0},{16,4},{20,8},{24,12},{28,16},{32,20},{36,24},{40,28},{44,3... | collective-permute-start | bytes 196616 | tf_op jit(solution)/shard_map/ppermute | solution.py:17
  433.2 16.5 %collective-permute-start.6 = (f32[2,8192]{1,0:T(2,128)S(1)}, f32[2,8192]{1,0:T(2,128)S(1)}, u32[]{:S(2)}, u32[]{:S(2)}) collective-permute-start(f32[2,8192]{1,0:T(2,128)S(1)} %fusion.49), channel_id=1, source_target_pairs={{4,0},{8,4},{12,8},{16,12},{20,16},{24,20},{28,24},{32,28},{36,32}... | collective-permute-start | bytes 196616 | tf_op jit(solution)/shard_map/ppermute | solution.py:17
  449.8 10.7 %collective-permute-start.7 = (f32[2,8192]{1,0:T(2,128)S(1)}, f32[2,8192]{1,0:T(2,128)S(1)}, u32[]{:S(2)}, u32[]{:S(2)}) collective-permute-start(f32[2,8192]{1,0:T(2,128)S(1)} %fusion.47), channel_id=1, source_target_pairs={{8,0},{12,4},{16,8},{20,12},{24,16},{28,20},{32,24},{36,28},{40,32... | collective-permute-start | bytes 196616 | tf_op jit(solution)/shard_map/ppermute | solution.py:17
Sparse Core Ops, SparseCore 0:
  361.5 50.5 reduce-scatter.1

commit v3 on v2

--- a/solution.py
+++ b/solution.py
@@ -17,14 +17,20 @@
     return lax.ppermute(block, axis, route)
 
 
-def all_heads(w_all, queries, grad_out, key_lat, visible, score_scale, block_count):
+def all_heads(w_keys, w_values, queries, grad_out, key_lat, visible, score_scale, block_count):
     tok_rows, head_count, head_dim = queries.shape
-    expanded = jnp.einsum(
-        "sl,hlc->hsc", key_lat, w_all, preferred_element_type=jnp.float32
-    ).astype(jnp.bfloat16)
-    expanded = expanded.reshape(head_count, block_count, -1, 2 * head_dim)
-    key_rows = expanded[..., :head_dim]
-    value_rows = expanded[..., head_dim:]
+
+    def expand(w_part):
+        rows = jnp.einsum("sl,hlc->hsc", key_lat, w_part, preferred_element_type=jnp.float32)
+        return rows.astype(jnp.bfloat16).reshape(head_count, block_count, -1, head_dim)
+
+    def weight_grad(grad_part):
+        return jnp.einsum(
+            "sl,hsc->hlc", key_lat, grad_part, preferred_element_type=jnp.float32
+        ).astype(jnp.bfloat16)
+
+    key_rows = expand(w_keys)
+    value_rows = expand(w_values)
     q_all = queries.reshape(block_count, BLK, head_count, head_dim)
     g_all = grad_out.reshape(block_count, BLK, head_count, head_dim)
     scores = (
@@ -36,10 +42,14 @@
     exp_scores = jnp.exp(scores - row_max)
     softmax_p = exp_scores / jnp.sum(exp_scores, axis=-1, keepdims=True)
     probs_low = softmax_p.astype(jnp.bfloat16)
+    g_t = jnp.transpose(g_all, (2, 0, 1, 3))
+    grad_v = jnp.einsum(
+        "hqbk,hqbd->hqkd", probs_low, g_t, preferred_element_type=jnp.float32
+    ).astype(jnp.bfloat16).reshape(head_count, -1, head_dim)
+    grad_w_values = weight_grad(grad_v)
     attended = jnp.einsum(
         "hqbk,hqkd->hqbd", probs_low, value_rows, preferred_element_type=jnp.float32
     )
-    g_t = jnp.transpose(g_all, (2, 0, 1, 3))
     delta_rows = jnp.sum(g_t.astype(jnp.float32) * attended, axis=-1, keepdims=True)
     grad_probs = jnp.einsum(
         "hqbd,hqkd->hqbk", g_t, value_rows, preferred_element_type=jnp.float32
@@ -52,14 +62,12 @@
     grad_k = (
         jnp.einsum("hqbk,qbhd->hqkd", grad_scores, q_all, preferred_element_type=jnp.float32)
         * score_scale
-    ).astype(jnp.bfloat16)
-    grad_v = jnp.einsum(
-        "hqbk,hqbd->hqkd", probs_low, g_t, preferred_element_type=jnp.float32
-    ).astype(jnp.bfloat16)
-    grad_kv = jnp.concatenate([grad_k, grad_v], axis=-1).reshape(head_count, -1, 2 * head_dim)
-    lat_part = jnp.einsum("hsc,hlc->sl", grad_kv, w_all, preferred_element_type=jnp.float32)
-    grad_w = jnp.einsum("sl,hsc->hlc", key_lat, grad_kv, preferred_element_type=jnp.float32)
-    return (grad_q.reshape(tok_rows, head_count, head_dim), lat_part, grad_w)
+    ).astype(jnp.bfloat16).reshape(head_count, -1, head_dim)
+    lat_part = jnp.einsum(
+        "hsc,hlc->sl", grad_k, w_keys, preferred_element_type=jnp.float32
+    ) + jnp.einsum("hsc,hlc->sl", grad_v, w_values, preferred_element_type=jnp.float32)
+    grad_w_keys = weight_grad(grad_k)
+    return (grad_q.reshape(tok_rows, head_count, head_dim), lat_part, grad_w_keys, grad_w_values)
 
 
 def visibility(doc_ids, list_rows, query_start, block_count):
@@ -138,17 +146,27 @@
     key_pos, visible = visibility(doc_ids, own_lists, device_pos * tok_rows, block_count)
 
     fsdp_size = lax.axis_size("fsdp")
-    w_copies = jnp.broadcast_to(kv_weight[0], (fsdp_size,) + kv_weight.shape[2:])
-    w_piece = lax.all_to_all(w_copies, "fsdp", 0, 0, tiled=True)
-    grad_q_all, grad_lat, grad_w_all = all_heads(
-        w_piece, queries, grad_out, key_lat, visible, score_scale, block_count
-    )
-    run_partials = lax.all_to_all(grad_w_all.astype(jnp.bfloat16), "fsdp", 0, 0, tiled=True)
-    grad_weight = jnp.sum(run_partials.astype(jnp.float32), axis=0, keepdims=True)[None]
-    slot_grads = grad_lat.reshape(block_count, TOPK, BLK, lat_width)
-    lat_shares = lax.psum_scatter(slot_grads, "grp", scatter_dimension=3, tiled=True).reshape(
-        block_count * TOPK, BLK * lat_share
-    )
+
+    def gather_heads(w_part):
+        copies = jnp.broadcast_to(w_part, (fsdp_size,) + w_part.shape)
+        return lax.all_to_all(copies, "fsdp", 0, 0, tiled=True)
+
+    def reduce_runs(partials):
+        per_run = lax.all_to_all(partials, "fsdp", 0, 0, tiled=True)
+        return jnp.sum(per_run.astype(jnp.float32), axis=0)
+
+    w_keys = gather_heads(kv_weight[0, 0, :, :head_dim])
+    w_values = gather_heads(kv_weight[0, 0, :, head_dim:])
+    grad_q_all, grad_lat, grad_w_keys, grad_w_values = all_heads(
+        w_keys, w_values, queries, grad_out, key_lat, visible, score_scale, block_count
+    )
+    grad_weight = jnp.concatenate(
+        [reduce_runs(grad_w_keys), reduce_runs(grad_w_values)], axis=-1
+    )[None, None]
+    grp_size = lax.axis_size("grp")
+    lat_pieces = jnp.moveaxis(grad_lat.reshape(-1, grp_size, lat_share), 1, 0)
+    lat_pieces = lax.all_to_all(lat_pieces, "grp", 0, 0, tiled=True)
+    lat_shares = jnp.sum(lat_pieces, axis=0).reshape(block_count * TOPK, BLK * lat_share)
     flat_pool = pool_index.reshape(-1)
     own_table = (flat_pool[None, :] == jnp.arange(block_count)[:, None]).astype(jnp.float32)
     lat_total = jnp.dot(own_table, lat_shares, precision=lax.Precision.HIGHEST)

time: 481 us -> 385 us (0.80)
  local copies, waits for them, and re-layouts: 91.2 us -> 41.6 us
  waiting for transfers between devices: 155 us -> 110 us
  starting transfers between devices: 55.7 us -> 93.9 us
  other arithmetic: 35.5 us -> 21.4 us
  between operations: 15 us -> 1.96 us
  matrix products: 122 us -> 111 us
    ppermute x12, waiting for transfers between devices: 114 us -> 50.5 us  [passed_along(): return lax.ppermute(block, axis, route)]
    all_to_all x2 -> x5, waiting for transfers between devices: 0.01 us -> 59.5 us  [the longest x2 42 us: reduce_runs(): per_run = lax.all_to_all(partials, 'fsdp', 0, 0, tiled=True)]
    reduce_scatter x1 -> x0, waiting for transfers between devices: 41.5 us -> none  [per_device(): lax.psum_scatter(slot_grads, 'grp', scatter_dimension=3, tiled=True)]
    all_to_all x2 -> x5, starting transfers between devices: 17.1 us -> 47.3 us  [the longest x2 22.5 us: reduce_runs(): per_run = lax.all_to_all(partials, 'fsdp', 0, 0, tiled=True)]
    dot_general x1 -> x0, local copies, waits for them, and re-layouts: 28.1 us -> none  [all_heads(): jnp.einsum('hsc,hlc->sl', grad_kv, w_all, preferred_element_type=jnp.floa...]
    concatenate x1 -> x0, local copies, waits for them, and re-layouts: 22.6 us -> none  [all_heads(): jnp.concatenate([grad_k, grad_v], axis=-1)]
    concatenate x1 -> x0, other arithmetic: 13.7 us -> none  [all_heads(): jnp.concatenate([grad_k, grad_v], axis=-1)]
    dot_general x3 -> x6, matrix products: 63.5 us -> 55.2 us  [the longest x2 19.6 us: expand(): jnp.einsum('sl,hlc->hsc', key_lat, w_part, preferred_element_type=jnp.flo...]
  transfers between devices with their start and end apart: 15 -> 17, of which waited for: 9 -> 6; matrix products, arithmetic and copies ran while one was open for 18% -> 28% of each run, Pallas kernels for 0% -> 0%
where the time goes in v3:
time: 385 us; the launch traced here: 380 us
  matrix products  111 us (29%)
  waiting for transfers between devices  110 us (29%)
  starting transfers between devices  93.9 us (24%)
  local copies, waits for them, and re-layouts  41.6 us (11%)
  other arithmetic  21.4 us (6%)
    ppermute x12, waiting for transfers between devices, passed_along(): return lax.ppermute(block, axis, route)  50.5 us
    ppermute x12, starting transfers between devices, passed_along(): return lax.ppermute(block, axis, route)  46.6 us
    all_to_all x2, waiting for transfers between devices, reduce_runs(): per_run = lax.all_to_all(partials, 'fsdp', 0, 0, tiled=True)  42 us
    all_to_all x2, starting transfers between devices, reduce_runs(): per_run = lax.all_to_all(partials, 'fsdp', 0, 0, tiled=True)  22.5 us
    all_to_all x2, starting transfers between devices, gather_heads(): return lax.all_to_all(copies, 'fsdp', 0, 0, tiled=True)  20.8 us
    dot_general x2, matrix products, expand(): jnp.einsum('sl,hlc->hsc', key_lat, w_part, preferred_element_type=jnp.flo...  19.6 us
    dot_general x2, matrix products, weight_grad(): jnp.einsum('sl,hsc->hlc', key_lat, grad_part, preferred_element_type=jnp....  19.2 us
    all_to_all x1, waiting for transfers between devices, per_device(): lat_pieces = lax.all_to_all(lat_pieces, 'grp', 0, 0, tiled=True)  16.4 us
  transfers between devices with their start and end apart: 17, of which 6 were waited for; matrix products, arithmetic and copies ran while one was open for 28% of the time, Pallas kernels for 0%

profile of v3, /device:TPU:120, one launch (start us, length us, event | category | flops | bytes accessed | tf_op | source)
XLA Modules:
  0.0 379.9 jit_solution(4149278086600211338)
XLA Ops:
  0.7 1.1 slice_bitcast_fusion
  1.8 2.9 broadcast_in_dim.110
  4.7 7.9 %all-to-all-start = ((bf16[32,512,128]{2,1,0:T(8,128)(2,1)}), bf16[32,512,128]{2,1,0:T(8,128)(2,1)}, u32[]{:S(2)}, u32[]{:S(2)}) async-start(bf16[32,512,128]{2,1,0:T(8,128)(2,1)} %broadcast_in_dim.110), calls=%async_computation | async-start | bytes 8388608 | tf_op jit(solution)/shard_map/all_to_all | solution.py:152
  13.5 0.6 gather_fusion.3
  14.1 3.4 collective-permute-start
  17.8 0.6 gather_fusion.4
  18.4 4.3 %collective-permute-start.1 = (bf16[2,64,512]{2,1,0:T(8,128)(2,1)S(1)}, bf16[2,64,512]{2,1,0:T(8,128)(2,1)S(1)}, u32[]{:S(2)}, u32[]{:S(2)}) collective-permute-start(bf16[2,64,512]{2,1,0:T(8,128)(2,1)S(1)} %broadcast_select_fusion.5), channel_id=1, source_target_pairs={{0,8},{4,12},{8,16},{12,20},{16,24},{20,28},{24,32},{28,36},{32,40... | collective-permute-start | bytes 393224 | tf_op jit(solution)/shard_map/ppermute | solution.py:17
  23.4 0.6 gather_fusion.5
  24.0 2.8 collective-permute-start.2
  27.1 0.6 gather_fusion.6
  27.6 0.7 broadcast_select_fusion.3
  28.4 3.4 collective-permute-start.3
  33.0 0.7 broadcast_select_fusion.2
  33.8 5.8 %collective-permute-start.4 = (bf16[2,64,512]{2,1,0:T(8,128)(2,1)}, bf16[2,64,512]{2,1,0:T(8,128)(2,1)}, u32[]{:S(2)}, u32[]{:S(2)}) collective-permute-start(bf16[2,64,512]{2,1,0:T(8,128)(2,1)} %broadcast_select_fusion.2), channel_id=1, source_target_pairs={{0,20},{4,24},{8,28},{12,32},{16,36},{20,40},{24,44},{28,48},{32,5... | collective-permute-start | bytes 393224 | tf_op jit(solution)/shard_map/ppermute | solution.py:17
  41.8 6.2 %gather_fusion.1 = s32[1024]{0:T(1024)S(1)} fusion(s32[8192]{0:T(1024)S(1)} %copy-done.2, s32[1024]{0:T(1024)S(1)} %get-tuple-element.39), kind=kCustom, calls=%fused_computation.7 | custom fusion | bytes 12288 | tf_op jit(solution)/shard_map/jit(_take)/gather | solution.py:79
  47.9 1.7 gather_fusion.2
  50.0 0.7 broadcast_select_fusion.1
  50.7 0.7 constant_dynamic-update-slice_fusion.6
  51.6 3.7 copy.79
  55.3 10.6 %collective-permute-done = bf16[2,64,512]{2,1,0:T(8,128)(2,1)S(1)} collective-permute-done((bf16[2,64,512]{2,1,0:T(8,128)(2,1)S(1)}, bf16[2,64,512]{2,1,0:T(8,128)(2,1)S(1)}, u32[]{:S(2)}, u32[]{:S(2)}) %collective-permute-start) | collective-permute-done | bytes 131104 | tf_op jit(solution)/shard_map/ppermute | solution.py:17
  65.9 9.8 %collective-permute-start.5 = (bf16[2,64,512]{2,1,0:T(8,128)(2,1)}, bf16[2,64,512]{2,1,0:T(8,128)(2,1)S(1)}, u32[]{:S(2)}, u32[]{:S(2)}) collective-permute-start(bf16[2,64,512]{2,1,0:T(8,128)(2,1)} %broadcast_select_fusion.1), channel_id=1, source_target_pairs={{0,24},{4,28},{8,32},{12,36},{16,40},{20,44},{24,48},{28,52},{32,5... | collective-permute-start | bytes 393224 | tf_op jit(solution)/shard_map/ppermute | solution.py:17
  75.8 0.7 constant_dynamic-update-slice_fusion.5
  76.4 0.7 constant_dynamic-update-slice_fusion.4
  77.1 0.7 constant_dynamic-update-slice_fusion.3
  77.7 1.6 constant_dynamic-update-slice_fusion.2
  79.3 2.9 broadcast_in_dim.192
  82.2 12.8 %all-to-all-start.1 = ((bf16[32,512,128]{2,1,0:T(8,128)(2,1)}), bf16[32,512,128]{2,1,0:T(8,128)(2,1)}, u32[]{:S(2)}, u32[]{:S(2)}) async-start(bf16[32,512,128]{2,1,0:T(8,128)(2,1)} %broadcast_in_dim.192), calls=%async_computation.1 | async-start | bytes 8388608 | tf_op jit(solution)/shard_map/all_to_all | solution.py:152
  95.1 1.6 constant_dynamic-update-slice_fusion.1
  96.7 0.7 constant_dynamic-update-slice_fusion
  97.3 1.8 gather_fusion
  99.4 9.2 %convolution_convert_fusion.1 = bf16[1024,32,128]{2,0,1:T(8,128)(2,1)} fusion(bf16[32,512,128]{2,1,0:T(8,128)(2,1)} %all-to-all-done, bf16[1024,512]{1,0:T(8,128)(2,1)S(1)} %bitcast_select_fusion.4), kind=kOutput, calls=%fused_computation.26 | convolution fusion | flops 4299161600 | bytes 13631488 | tf_op jit(solution)/shard_map/sl,hlc->hsc/dot_general | solution.py:24
  108.7 9.1 %fusion.20 = f32[32,4,256,64]{2,3,1,0:T(8,128)} fusion(bf16[32,4,256,128]{3,2,1,0:T(8,128)(2,1)} %bitcast.99, bf16[4,64,32,128]{3,2,1,0:T(8,128)(2,1)S(1)} %bitcast.95), kind=kOutput, calls=%fused_computation.42 | convolution fusion | flops 536870912 | bytes 18874368 | tf_op jit(solution)/shard_map/qbhd,hqkd->hqbk/dot_general | solution.py:37
  117.8 10.5 %fusion.87 = (f32[32,4,64]{2,1,0:T(4,128)S(1)}, f32[32,4,64,256]{3,2,1,0:T(8,128)S(1)}) fusion(f32[32,4,256,64]{2,3,1,0:T(8,128)} %fusion.20, pred[4,64,256]{2,1,0:T(8,128)(4,1)S(1)} %compare_and_fusion), kind=kOutput, calls=%fused_computation.234 | output fusion | flops 12583167 | bytes 16875520 | tf_op jit(solution)/shard_map/sub | solution.py:42
  128.3 3.2 copy-done.10
  131.5 6.1 %convolution_convert_fusion.2 = bf16[32,4,256,128]{3,2,1,0:T(8,128)(2,1)} fusion(bf16[32,4,64,128]{3,2,1,0:T(8,128)(2,1)S(1)} %bitcast.110, f32[32,4,64,256]{3,2,1,0:T(8,128)S(1)} %get-tuple-element.25, f32[32,4,64]{2,1,0:T(4,128)S(1)} %get-tuple-element.24), kind=kOutput, calls=%fused_computation.27 | convolution fusion | flops 545259520 | bytes 18907136 | tf_op jit(solution)/shard_map/hqbk,hqbd->hqkd/dot_general | solution.py:46
  137.7 1.1 all-to-all-done.1
  138.8 10.4 %convolution_convert_fusion = bf16[1024,32,128]{2,0,1:T(8,128)(2,1)} fusion(bf16[32,512,128]{2,1,0:T(8,128)(2,1)} %all-to-all-done.1, bf16[1024,512]{1,0:T(8,128)(2,1)} %copy-done.8), kind=kOutput, calls=%fused_computation.25 | convolution fusion | flops 4299161600 | bytes 13631488 | tf_op jit(solution)/shard_map/sl,hlc->hsc/dot_general | solution.py:24
  149.2 8.4 %multiply_reduce_fusion = f32[32,4,64]{2,1,0:T(4,128)S(1)} fusion(bf16[32,4,64,128]{3,2,1,0:T(8,128)(2,1)S(1)} %bitcast.111, bf16[32,4,256,128]{3,2,1,0:T(8,128)(2,1)} %bitcast.120, f32[32,4,64,256]{3,2,1,0:T(8,128)} %copy-done.10, f32[32,4,64]{2,1,0:T(4,128)S(1)} %get-tuple-element.24), kind=kOutput, calls=%fused_computation.33 | convolution fusion | flops 544202752 | bytes 18939904 | tf_op jit(solution)/shard_map/hqbk,hqkd->hqbd/dot_general | solution.py:50
  157.6 12.4 %fusion.5 = bf16[32,4,64,256]{3,2,1,0:T(8,128)(2,1)} fusion(f32[32,4,64]{2,1,0:T(4,128)S(1)} %multiply_reduce_fusion, f32[32,4,64,256]{3,2,1,0:T(8,128)} %copy-done.10, f32[32,4,64]{2,1,0:T(4,128)S(1)} %get-tuple-element.24, bf16[32,4,256,128]{3,2,1,0:T(8,128)(2,1)} %bitcast.121, bf16[32,4,64,128]{3,2,1,0:T(8,128)(2,1)} %bitcast.109), kind=kOutput, calls=%fused_computation.18 | convolution fusion | flops 545259520 | bytes 23134208 | tf_op jit(solution)/shard_map/hqbd,hqkd->hqbk/dot_general | solution.py:54
  170.1 9.6 %multiply_convert_fusion = bf16[32,4,256,128]{3,2,1,0:T(8,128)(2,1)} fusion(bf16[32,4,64,256]{3,2,1,0:T(8,128)(2,1)} %fusion.5, bf16[4,64,32,128]{3,2,1,0:T(8,128)(2,1)S(1)} %bitcast.96), kind=kOutput, calls=%fused_computation.10 | convolution fusion | flops 545259520 | bytes 14680064 | tf_op jit(solution)/shard_map/hqbk,qbhd->hqkd/dot_general | solution.py:63
  179.8 8.3 %fusion.88 = f32[1024,512,1]{0,1,2:T(8,128)S(1)} fusion(bf16[32,1024,128]{2,1,0:T(8,128)(2,1)} %bitcast.97, bf16[32,512,128]{2,1,0:T(8,128)(2,1)} %all-to-all-done), kind=kOutput, calls=%fused_computation.235 | convolution fusion | flops 4294967296 | bytes 14680064 | tf_op jit(solution)/shard_map/hsc,hlc->sl/dot_general | solution.py:66
  188.1 8.0 %bitcast_add_fusion = f32[1024,512]{0,1:T(8,128)} fusion(f32[1024,512,1]{0,1,2:T(8,128)S(1)} %fusion.88, bf16[32,1024,128]{2,1,0:T(8,128)(2,1)S(1)} %bitcast.119, bf16[32,512,128]{2,1,0:T(8,128)(2,1)} %all-to-all-done.1), kind=kOutput, calls=%fused_computation.40 | convolution fusion | flops 4295491584 | bytes 16777216 | tf_op jit(solution)/shard_map/hsc,hlc->sl/dot_general | solution.py:68
  196.2 4.0 %all-to-all-start.2 = ((f32[4,1024,128]{1,2,0:T(8,128)}), f32[4,1024,128]{1,2,0:T(8,128)S(1)}, u32[]{:S(2)}, u32[]{:S(2)}) async-start(f32[4,1024,128]{1,2,0:T(8,128)} %bitcast.112), calls=%async_computation.2 | async-start | bytes 4194304 | tf_op jit(solution)/shard_map/all_to_all | solution.py:168
  200.3 1.0 copy-done.6
  201.4 9.6 %convert_bitcast_fusion = bf16[32,512,128]{1,2,0:T(8,128)(2,1)} fusion(bf16[32,1024,128]{2,1,0:T(8,128)(2,1)} %bitcast.116, bf16[1024,512,1]{1,0,2:T(8,128)(2,1)S(1)} %bitcast.113), kind=kOutput, calls=%fused_computation.30 | convolution fusion | flops 4297064448 | bytes 13631488 | tf_op jit(solution)/shard_map/sl,hsc->hlc/dot_general | solution.py:28
  211.0 16.4 %all-to-all-done.2 = f32[4,1024,128]{1,2,0:T(8,128)S(1)} async-done(((f32[4,1024,128]{1,2,0:T(8,128)}), f32[4,1024,128]{1,2,0:T(8,128)S(1)}, u32[]{:S(2)}, u32[]{:S(2)}) %all-to-all-start.2) | async-done | bytes 2097184 | tf_op jit(solution)/shard_map/all_to_all | solution.py:168
  227.3 13.0 %all-to-all-start.4 = ((bf16[32,512,128]{1,2,0:T(8,128)(2,1)}), bf16[32,512,128]{1,2,0:T(8,128)(2,1)}, u32[]{:S(2)}, u32[]{:S(2)}) async-start(bf16[32,512,128]{1,2,0:T(8,128)(2,1)} %convert_bitcast_fusion), calls=%async_computation.4 | async-start | bytes 8388608 | tf_op jit(solution)/shard_map/all_to_all | solution.py:155
  240.4 9.6 %convert_bitcast_fusion.1 = bf16[32,512,128]{1,2,0:T(8,128)(2,1)} fusion(bf16[32,1024,128]{2,1,0:T(8,128)(2,1)} %bitcast.98, bf16[1024,512,1]{1,0,2:T(8,128)(2,1)S(1)} %bitcast.114), kind=kOutput, calls=%fused_computation.31 | convolution fusion | flops 4297064448 | bytes 13631488 | tf_op jit(solution)/shard_map/sl,hsc->hlc/dot_general | solution.py:28
  250.0 42.0 %all-to-all-done.4 = bf16[32,512,128]{1,2,0:T(8,128)(2,1)} async-done(((bf16[32,512,128]{1,2,0:T(8,128)(2,1)}), bf16[32,512,128]{1,2,0:T(8,128)(2,1)}, u32[]{:S(2)}, u32[]{:S(2)}) %all-to-all-start.4) | async-done | bytes 4194336 | tf_op jit(solution)/shard_map/all_to_all | solution.py:155
  292.0 9.6 %all-to-all-start.3 = ((bf16[32,512,128]{1,2,0:T(8,128)(2,1)}), bf16[32,512,128]{1,2,0:T(8,128)(2,1)}, u32[]{:S(2)}, u32[]{:S(2)}) async-start(bf16[32,512,128]{1,2,0:T(8,128)(2,1)} %convert_bitcast_fusion.1), calls=%async_computation.3 | async-start | bytes 8388608 | tf_op jit(solution)/shard_map/all_to_all | solution.py:155
  301.5 6.4 %fusion.14 = bf16[4,64,32,128]{3,1,2,0:T(8,128)(2,1)S(1)} fusion(bf16[32,4,256,128]{3,2,1,0:T(8,128)(2,1)} %bitcast.100, bf16[32,4,64,256]{3,2,1,0:T(8,128)(2,1)} %fusion.5), kind=kOutput, calls=%fused_computation.39 | convolution fusion | flops 538968064 | bytes 14680064 | tf_op jit(solution)/shard_map/hqbk,hqkd->qbhd/dot_general | solution.py:59
  308.0 2.7 copy.82
  311.5 3.8 collective-permute-start.11
  315.6 1.9 collective-permute-start.10
  317.9 2.5 collective-permute-start.9
  320.7 5.2 %collective-permute-start.8 = (f32[2,8192]{1,0:T(2,128)S(1)}, f32[2,8192]{1,0:T(2,128)S(1)}, u32[]{:S(2)}, u32[]{:S(2)}) collective-permute-start(f32[2,8192]{1,0:T(2,128)S(1)} %fusion.45), channel_id=1, source_target_pairs={{12,0},{16,4},{20,8},{24,12},{28,16},{32,20},{36,24},{40,28},{44,3... | collective-permute-start | bytes 196616 | tf_op jit(solution)/shard_map/ppermute | solution.py:17
  326.2 1.9 collective-permute-start.6
  328.7 32.4 %collective-permute-done.6 = f32[2,8192]{1,0:T(2,128)S(1)} collective-permute-done((f32[2,8192]{1,0:T(2,128)S(1)}, f32[2,8192]{1,0:T(2,128)S(1)}, u32[]{:S(2)}, u32[]{:S(2)}) %collective-permute-start.6) | collective-permute-done | bytes 65568 | tf_op jit(solution)/shard_map/ppermute | solution.py:17
  361.1 1.9 collective-permute-start.7
  364.4 7.4 %collective-permute-done.7 = f32[2,8192]{1,0:T(2,128)S(1)} collective-permute-done((f32[2,8192]{1,0:T(2,128)S(1)}, f32[2,8192]{1,0:T(2,128)S(1)}, u32[]{:S(2)}, u32[]{:S(2)}) %collective-permute-start.7) | collective-permute-done | bytes 65568 | tf_op jit(solution)/shard_map/ppermute | solution.py:17
  372.1 0.7 reshape.725
  372.9 2.8 convert_reduce_fusion
  375.7 2.8 convert_reduce_fusion.1
  378.5 1.0 copy.87
  (154 shorter events, 10.6 us)
Async XLA Ops:
  0.6 108.0 %copy-start = (bf16[256,32,128]{2,1,0:T(8,128)(2,1)S(1)}, bf16[256,32,128]{2,1,0:T(8,128)(2,1)}, u32[]{:S(2)}) copy-start(bf16[256,32,128]{2,1,0:T(8,128)(2,1)} %param.9) | copy-start | bytes 6291460
  0.6 12.0 %copy-start.9 = (s32[128,4]{0,1:T(4,128)S(1)}, s32[128,4]{0,1:T(4,128)}, u32[]{:S(2)}) copy-start(s32[128,4]{0,1:T(4,128)} %param.13) | copy-start | bytes 6148
  0.7 12.8 %copy-start.3 = (bf16[256,512]{1,0:T(8,128)(2,1)S(1)}, bf16[256,512]{1,0:T(8,128)(2,1)}, u32[]{:S(2)}) copy-start(bf16[256,512]{1,0:T(8,128)(2,1)} %param.8) | copy-start | bytes 786436
  0.7 41.1 %copy-start.2 = (s32[8192]{0:T(1024)S(1)}, s32[8192]{0:T(1024)}, u32[]{:S(2)}) copy-start(s32[8192]{0:T(1024)} %param.12) | copy-start | bytes 98308
  4.7 74.6 %all-to-all-start = ((bf16[32,512,128]{2,1,0:T(8,128)(2,1)}), bf16[32,512,128]{2,1,0:T(8,128)(2,1)}, u32[]{:S(2)}, u32[]{:S(2)}) async-start(bf16[32,512,128]{2,1,0:T(8,128)(2,1)} %broadcast_in_dim.110), calls=%async_computation | async-start | bytes 8388608 | tf_op jit(solution)/shard_map/all_to_all | solution.py:152
  14.1 51.8 %collective-permute-start = (bf16[2,64,512]{2,1,0:T(8,128)(2,1)S(1)}, bf16[2,64,512]{2,1,0:T(8,128)(2,1)S(1)}, u32[]{:S(2)}, u32[]{:S(2)}) collective-permute-start(bf16[2,64,512]{2,1,0:T(8,128)(2,1)S(1)} %broadcast_select_fusion.6), channel_id=1, source_target_pairs={{0,4},{4,8},{8,12},{12,16},{16,20},{20,24},{24,28},{28,32},{32,36}... | collective-permute-start | bytes 393224 | tf_op jit(solution)/shard_map/ppermute | solution.py:17
  18.4 58.0 %collective-permute-start.1 = (bf16[2,64,512]{2,1,0:T(8,128)(2,1)S(1)}, bf16[2,64,512]{2,1,0:T(8,128)(2,1)S(1)}, u32[]{:S(2)}, u32[]{:S(2)}) collective-permute-start(bf16[2,64,512]{2,1,0:T(8,128)(2,1)S(1)} %broadcast_select_fusion.5), channel_id=1, source_target_pairs={{0,8},{4,12},{8,16},{12,20},{16,24},{20,28},{24,32},{28,36},{32,40... | collective-permute-start | bytes 393224 | tf_op jit(solution)/shard_map/ppermute | solution.py:17
  24.0 53.1 %collective-permute-start.2 = (bf16[2,64,512]{2,1,0:T(8,128)(2,1)S(1)}, bf16[2,64,512]{2,1,0:T(8,128)(2,1)S(1)}, u32[]{:S(2)}, u32[]{:S(2)}) collective-permute-start(bf16[2,64,512]{2,1,0:T(8,128)(2,1)S(1)} %broadcast_select_fusion.4), channel_id=1, source_target_pairs={{0,12},{4,16},{8,20},{12,24},{16,28},{20,32},{24,36},{28,40},{32,4... | collective-permute-start | bytes 393224 | tf_op jit(solution)/shard_map/ppermute | solution.py:17
  28.4 49.4 %collective-permute-start.3 = (bf16[2,64,512]{2,1,0:T(8,128)(2,1)}, bf16[2,64,512]{2,1,0:T(8,128)(2,1)}, u32[]{:S(2)}, u32[]{:S(2)}) collective-permute-start(bf16[2,64,512]{2,1,0:T(8,128)(2,1)} %broadcast_select_fusion.3), channel_id=1, source_target_pairs={{0,16},{4,20},{8,24},{12,28},{16,32},{20,36},{24,40},{28,44},{32,4... | collective-permute-start | bytes 393224 | tf_op jit(solution)/shard_map/ppermute | solution.py:17
  33.8 61.3 %collective-permute-start.4 = (bf16[2,64,512]{2,1,0:T(8,128)(2,1)}, bf16[2,64,512]{2,1,0:T(8,128)(2,1)}, u32[]{:S(2)}, u32[]{:S(2)}) collective-permute-start(bf16[2,64,512]{2,1,0:T(8,128)(2,1)} %broadcast_select_fusion.2), channel_id=1, source_target_pairs={{0,20},{4,24},{8,28},{12,32},{16,36},{20,40},{24,44},{28,48},{32,5... | collective-permute-start | bytes 393224 | tf_op jit(solution)/shard_map/ppermute | solution.py:17
  65.9 30.8 %collective-permute-start.5 = (bf16[2,64,512]{2,1,0:T(8,128)(2,1)}, bf16[2,64,512]{2,1,0:T(8,128)(2,1)S(1)}, u32[]{:S(2)}, u32[]{:S(2)}) collective-permute-start(bf16[2,64,512]{2,1,0:T(8,128)(2,1)} %broadcast_select_fusion.1), channel_id=1, source_target_pairs={{0,24},{4,28},{8,32},{12,36},{16,40},{20,44},{24,48},{28,52},{32,5... | collective-permute-start | bytes 393224 | tf_op jit(solution)/shard_map/ppermute | solution.py:17
  82.2 56.6 %all-to-all-start.1 = ((bf16[32,512,128]{2,1,0:T(8,128)(2,1)}), bf16[32,512,128]{2,1,0:T(8,128)(2,1)}, u32[]{:S(2)}, u32[]{:S(2)}) async-start(bf16[32,512,128]{2,1,0:T(8,128)(2,1)} %broadcast_in_dim.192), calls=%async_computation.1 | async-start | bytes 8388608 | tf_op jit(solution)/shard_map/all_to_all | solution.py:152
  99.4 9.2 %copy-start.8 = (bf16[1024,512]{1,0:T(8,128)(2,1)}, bf16[1024,512]{1,0:T(8,128)(2,1)S(1)}, u32[]{:S(2)}) copy-start(bf16[1024,512]{1,0:T(8,128)(2,1)S(1)} %bitcast_select_fusion.4) | copy-start | bytes 3145732
  117.8 13.7 %copy-start.4 = (bf16[256,32,128]{2,0,1:T(8,128)(2,1)S(1)}, bf16[256,32,128]{2,0,1:T(8,128)(2,1)}, u32[]{:S(2)}) copy-start(bf16[256,32,128]{2,0,1:T(8,128)(2,1)} %copy.79) | copy-start | bytes 6291460
  128.3 3.2 copy-start.10
  138.8 10.4 %copy-start.5 = (bf16[256,32,128]{2,0,1:T(8,128)(2,1)S(1)}, bf16[256,32,128]{2,0,1:T(8,128)(2,1)}, u32[]{:S(2)}) copy-start(bf16[256,32,128]{2,0,1:T(8,128)(2,1)} %copy.79) | copy-start | bytes 6291460
  170.1 18.0 %slice-start = ((s8[8388608]{0:T(1024)(128)(4,1)}), s8[4194304]{0:T(1024)(128)(4,1)S(1)}, s32[]{:S(2)}) async-start(s8[8388608]{0:T(1024)(128)(4,1)} %bitcast.117), calls=%async_computation.5 | async-start | bytes 8388608
  179.8 8.4 %slice-start.1 = ((s8[8388608]{0:T(1024)(128)(4,1)}), s8[4194304]{0:T(1024)(128)(4,1)S(1)}, s32[]{:S(2)}) async-start(s8[8388608]{0:T(1024)(128)(4,1)} %bitcast.117), calls=%async_computation.6 | async-start | bytes 8388608
  196.2 31.2 %all-to-all-start.2 = ((f32[4,1024,128]{1,2,0:T(8,128)}), f32[4,1024,128]{1,2,0:T(8,128)S(1)}, u32[]{:S(2)}, u32[]{:S(2)}) async-start(f32[4,1024,128]{1,2,0:T(8,128)} %bitcast.112), calls=%async_computation.2 | async-start | bytes 4194304 | tf_op jit(solution)/shard_map/all_to_all | solution.py:168
  200.3 1.0 copy-start.6
  211.0 29.4 %copy-start.7 = (bf16[16,64,512]{2,1,0:T(8,128)(2,1)S(1)}, bf16[16,64,512]{2,1,0:T(8,128)(2,1)}, u32[]{:S(2)}) copy-start(bf16[16,64,512]{2,1,0:T(8,128)(2,1)} %copy-done.6) | copy-start | bytes 3145732
  227.3 64.6 %all-to-all-start.4 = ((bf16[32,512,128]{1,2,0:T(8,128)(2,1)}), bf16[32,512,128]{1,2,0:T(8,128)(2,1)}, u32[]{:S(2)}, u32[]{:S(2)}) async-start(bf16[32,512,128]{1,2,0:T(8,128)(2,1)} %convert_bitcast_fusion), calls=%async_computation.4 | async-start | bytes 8388608 | tf_op jit(solution)/shard_map/all_to_all | solution.py:155
  292.0 83.7 %all-to-all-start.3 = ((bf16[32,512,128]{1,2,0:T(8,128)(2,1)}), bf16[32,512,128]{1,2,0:T(8,128)(2,1)}, u32[]{:S(2)}, u32[]{:S(2)}) async-start(bf16[32,512,128]{1,2,0:T(8,128)(2,1)} %convert_bitcast_fusion.1), calls=%async_computation.3 | async-start | bytes 8388608 | tf_op jit(solution)/shard_map/all_to_all | solution.py:155
  311.1 68.4 %copy-start.1 = (bf16[256,32,128]{2,1,0:T(8,128)(2,1)S(1)}, bf16[256,32,128]{2,1,0:T(8,128)(2,1)}, u32[]{:S(2)}) copy-start(bf16[256,32,128]{2,1,0:T(8,128)(2,1)} %param.9) | copy-start | bytes 6291460
  311.5 51.9 %collective-permute-start.11 = (f32[2,8192]{1,0:T(2,128)S(1)}, f32[2,8192]{1,0:T(2,128)S(1)}, u32[]{:S(2)}, u32[]{:S(2)}) collective-permute-start(f32[2,8192]{1,0:T(2,128)S(1)} %fusion.39), channel_id=1, source_target_pairs={{24,0},{28,4},{32,8},{36,12},{40,16},{44,20},{48,24},{52,28},{56,3... | collective-permute-start | bytes 196616 | tf_op jit(solution)/shard_map/ppermute | solution.py:17
  315.6 48.0 %collective-permute-start.10 = (f32[2,8192]{1,0:T(2,128)S(1)}, f32[2,8192]{1,0:T(2,128)S(1)}, u32[]{:S(2)}, u32[]{:S(2)}) collective-permute-start(f32[2,8192]{1,0:T(2,128)S(1)} %fusion.41), channel_id=1, source_target_pairs={{20,0},{24,4},{28,8},{32,12},{36,16},{40,20},{44,24},{48,28},{52,3... | collective-permute-start | bytes 196616 | tf_op jit(solution)/shard_map/ppermute | solution.py:17
  317.9 46.0 %collective-permute-start.9 = (f32[2,8192]{1,0:T(2,128)S(1)}, f32[2,8192]{1,0:T(2,128)S(1)}, u32[]{:S(2)}, u32[]{:S(2)}) collective-permute-start(f32[2,8192]{1,0:T(2,128)S(1)} %fusion.43), channel_id=1, source_target_pairs={{16,0},{20,4},{24,8},{28,12},{32,16},{36,20},{40,24},{44,28},{48,3... | collective-permute-start | bytes 196616 | tf_op jit(solution)/shard_map/ppermute | solution.py:17
  320.7 43.4 %collective-permute-start.8 = (f32[2,8192]{1,0:T(2,128)S(1)}, f32[2,8192]{1,0:T(2,128)S(1)}, u32[]{:S(2)}, u32[]{:S(2)}) collective-permute-start(f32[2,8192]{1,0:T(2,128)S(1)} %fusion.45), channel_id=1, source_target_pairs={{12,0},{16,4},{20,8},{24,12},{28,16},{32,20},{36,24},{40,28},{44,3... | collective-permute-start | bytes 196616 | tf_op jit(solution)/shard_map/ppermute | solution.py:17
  326.2 35.0 %collective-permute-start.6 = (f32[2,8192]{1,0:T(2,128)S(1)}, f32[2,8192]{1,0:T(2,128)S(1)}, u32[]{:S(2)}, u32[]{:S(2)}) collective-permute-start(f32[2,8192]{1,0:T(2,128)S(1)} %fusion.49), channel_id=1, source_target_pairs={{4,0},{8,4},{12,8},{16,12},{20,16},{24,20},{28,24},{32,28},{36,32}... | collective-permute-start | bytes 196616 | tf_op jit(solution)/shard_map/ppermute | solution.py:17
  361.1 10.7 %collective-permute-start.7 = (f32[2,8192]{1,0:T(2,128)S(1)}, f32[2,8192]{1,0:T(2,128)S(1)}, u32[]{:S(2)}, u32[]{:S(2)}) collective-permute-start(f32[2,8192]{1,0:T(2,128)S(1)} %fusion.47), channel_id=1, source_target_pairs={{8,0},{12,4},{16,8},{20,12},{24,16},{28,20},{32,24},{36,28},{40,32... | collective-permute-start | bytes 196616 | tf_op jit(solution)/shard_map/ppermute | solution.py:17

commit v4 on v3

--- a/solution.py
+++ b/solution.py
@@ -43,10 +43,21 @@
     softmax_p = exp_scores / jnp.sum(exp_scores, axis=-1, keepdims=True)
     probs_low = softmax_p.astype(jnp.bfloat16)
     g_t = jnp.transpose(g_all, (2, 0, 1, 3))
+    probs_low, value_rows = lax.optimization_barrier((probs_low, value_rows))
     grad_v = jnp.einsum(
         "hqbk,hqbd->hqkd", probs_low, g_t, preferred_element_type=jnp.float32
     ).astype(jnp.bfloat16).reshape(head_count, -1, head_dim)
     grad_w_values = weight_grad(grad_v)
+    return grad_w_values, *score_grads(
+        probs_low, softmax_p, g_t, q_all, key_rows, value_rows, w_keys, w_values,
+        grad_v, score_scale, weight_grad, tok_rows
+    )
+
+
+def score_grads(probs_low, softmax_p, g_t, q_all, key_rows, value_rows, w_keys, w_values,
+                grad_v, score_scale, weight_grad, tok_rows):
+    head_count = key_rows.shape[0]
+    head_dim = key_rows.shape[-1]
     attended = jnp.einsum(
         "hqbk,hqkd->hqbd", probs_low, value_rows, preferred_element_type=jnp.float32
     )
@@ -67,7 +78,7 @@
         "hsc,hlc->sl", grad_k, w_keys, preferred_element_type=jnp.float32
     ) + jnp.einsum("hsc,hlc->sl", grad_v, w_values, preferred_element_type=jnp.float32)
     grad_w_keys = weight_grad(grad_k)
-    return (grad_q.reshape(tok_rows, head_count, head_dim), lat_part, grad_w_keys, grad_w_values)
+    return (grad_q.reshape(tok_rows, head_count, head_dim), lat_part, grad_w_keys)
 
 
 def visibility(doc_ids, list_rows, query_start, block_count):
@@ -101,7 +112,6 @@
     device_pos = lax.axis_index("fsdp")
     tok_rows, lat_width = latents.shape
     head_dim = queries.shape[2]
-    head_count = queries.shape[1]
     block_count = tok_rows // BLK
     extra_picks = TOPK - 1
     slot_cap = block_count * extra_picks // DIST
@@ -143,7 +153,7 @@
     fetched = jnp.concatenate(arrived, axis=0)
     block_pool = jnp.concatenate([local_blocks, fetched], axis=0)
     key_lat = jnp.take(block_pool, pool_index.reshape(-1), axis=0).reshape(-1, lat_width)
-    key_pos, visible = visibility(doc_ids, own_lists, device_pos * tok_rows, block_count)
+    _, visible = visibility(doc_ids, own_lists, device_pos * tok_rows, block_count)
 
     fsdp_size = lax.axis_size("fsdp")
 
@@ -157,12 +167,12 @@
 
     w_keys = gather_heads(kv_weight[0, 0, :, :head_dim])
     w_values = gather_heads(kv_weight[0, 0, :, head_dim:])
-    grad_q_all, grad_lat, grad_w_keys, grad_w_values = all_heads(
+    grad_w_values, grad_q_all, grad_lat, grad_w_keys = all_heads(
         w_keys, w_values, queries, grad_out, key_lat, visible, score_scale, block_count
     )
-    grad_weight = jnp.concatenate(
-        [reduce_runs(grad_w_keys), reduce_runs(grad_w_values)], axis=-1
-    )[None, None]
+    value_part = reduce_runs(grad_w_values)
+    key_part = reduce_runs(grad_w_keys)
+    grad_weight = jnp.concatenate([key_part, value_part], axis=-1)[None, None]
     grp_size = lax.axis_size("grp")
     lat_pieces = jnp.moveaxis(grad_lat.reshape(-1, grp_size, lat_share), 1, 0)
     lat_pieces = lax.all_to_all(lat_pieces, "grp", 0, 0, tiled=True)

time: 385 us -> 386 us (level)
  matrix products: 111 us -> 107 us
    unnamed x36 -> x38, local copies, waits for them, and re-layouts: 15 us -> 15.8 us
  transfers between devices with their start and end apart: 17 -> 17, of which waited for: 6 -> 6; matrix products, arithmetic and copies ran while one was open for 28% -> 27% of each run, Pallas kernels for 0% -> 0%
where the time goes in v4:
time: 386 us; the launch traced here: 381 us
  waiting for transfers between devices  112 us (29%)
  matrix products  107 us (28%)
  starting transfers between devices  94 us (24%)
  local copies, waits for them, and re-layouts  42.4 us (11%)
  other arithmetic  23.5 us (6%)
    ppermute x12, waiting for transfers between devices, passed_along(): return lax.ppermute(block, axis, route)  51.1 us
    ppermute x12, starting transfers between devices, passed_along(): return lax.ppermute(block, axis, route)  46.8 us
    all_to_all x2, waiting for transfers between devices, reduce_runs(): per_run = lax.all_to_all(partials, 'fsdp', 0, 0, tiled=True)  42 us
    all_to_all x2, starting transfers between devices, reduce_runs(): per_run = lax.all_to_all(partials, 'fsdp', 0, 0, tiled=True)  22.8 us
    all_to_all x2, starting transfers between devices, gather_heads(): return lax.all_to_all(copies, 'fsdp', 0, 0, tiled=True)  20.5 us
    dot_general x2, matrix products, expand(): jnp.einsum('sl,hlc->hsc', key_lat, w_part, preferred_element_type=jnp.flo...  19.6 us
    dot_general x2, matrix products, weight_grad(): jnp.einsum('sl,hsc->hlc', key_lat, grad_part, preferred_element_type=jnp....  19.2 us
    all_to_all x1, waiting for transfers between devices, per_device(): lat_pieces = lax.all_to_all(lat_pieces, 'grp', 0, 0, tiled=True)  16.4 us
  transfers between devices with their start and end apart: 17, of which 6 were waited for; matrix products, arithmetic and copies ran while one was open for 27% of the time, Pallas kernels for 0%

profile of v4, /device:TPU:120, one launch (start us, length us, event | category | flops | bytes accessed | tf_op | source)
XLA Modules:
  0.0 380.8 jit_solution(9256990060977785299)
XLA Ops:
  0.6 1.1 slice_bitcast_fusion
  1.8 2.9 broadcast_in_dim.110
  4.7 8.1 %all-to-all-start = ((bf16[32,512,128]{2,1,0:T(8,128)(2,1)}), bf16[32,512,128]{2,1,0:T(8,128)(2,1)}, u32[]{:S(2)}, u32[]{:S(2)}) async-start(bf16[32,512,128]{2,1,0:T(8,128)(2,1)} %broadcast_in_dim.110), calls=%async_computation | async-start | bytes 8388608 | tf_op jit(solution)/shard_map/all_to_all | solution.py:162
  13.6 0.6 gather_fusion.3
  14.2 3.4 collective-permute-start
  17.9 0.6 gather_fusion.4
  18.5 4.3 %collective-permute-start.1 = (bf16[2,64,512]{2,1,0:T(8,128)(2,1)S(1)}, bf16[2,64,512]{2,1,0:T(8,128)(2,1)S(1)}, u32[]{:S(2)}, u32[]{:S(2)}) collective-permute-start(bf16[2,64,512]{2,1,0:T(8,128)(2,1)S(1)} %broadcast_select_fusion.5), channel_id=1, source_target_pairs={{0,8},{4,12},{8,16},{12,20},{16,24},{20,28},{24,32},{28,36},{32,40... | collective-permute-start | bytes 393224 | tf_op jit(solution)/shard_map/ppermute | solution.py:17
  23.5 0.6 gather_fusion.5
  24.1 2.8 collective-permute-start.2
  27.2 0.6 gather_fusion.6
  27.8 3.4 collective-permute-start.3
  32.5 0.7 broadcast_select_fusion.2
  33.2 5.8 %collective-permute-start.4 = (bf16[2,64,512]{2,1,0:T(8,128)(2,1)}, bf16[2,64,512]{2,1,0:T(8,128)(2,1)}, u32[]{:S(2)}, u32[]{:S(2)}) collective-permute-start(bf16[2,64,512]{2,1,0:T(8,128)(2,1)} %broadcast_select_fusion.2), channel_id=1, source_target_pairs={{0,20},{4,24},{8,28},{12,32},{16,36},{20,40},{24,44},{28,48},{32,5... | collective-permute-start | bytes 393224 | tf_op jit(solution)/shard_map/ppermute | solution.py:17
  41.2 6.2 %gather_fusion.1 = s32[1024]{0:T(1024)S(1)} fusion(s32[8192]{0:T(1024)S(1)} %copy-done.2, s32[1024]{0:T(1024)S(1)} %get-tuple-element.43), kind=kCustom, calls=%fused_computation.7 | custom fusion | bytes 12288 | tf_op jit(solution)/shard_map/jit(_take)/gather | solution.py:90
  47.4 1.7 gather_fusion.2
  49.4 0.7 broadcast_select_fusion.1
  50.2 0.7 constant_dynamic-update-slice_fusion.6
  51.1 3.7 copy.79
  54.8 11.0 %collective-permute-done = bf16[2,64,512]{2,1,0:T(8,128)(2,1)S(1)} collective-permute-done((bf16[2,64,512]{2,1,0:T(8,128)(2,1)S(1)}, bf16[2,64,512]{2,1,0:T(8,128)(2,1)S(1)}, u32[]{:S(2)}, u32[]{:S(2)}) %collective-permute-start) | collective-permute-done | bytes 131104 | tf_op jit(solution)/shard_map/ppermute | solution.py:17
  65.8 10.1 %collective-permute-start.5 = (bf16[2,64,512]{2,1,0:T(8,128)(2,1)S(1)}, bf16[2,64,512]{2,1,0:T(8,128)(2,1)S(1)}, u32[]{:S(2)}, u32[]{:S(2)}) collective-permute-start(bf16[2,64,512]{2,1,0:T(8,128)(2,1)S(1)} %copy-done.10), channel_id=1, source_target_pairs={{0,24},{4,28},{8,32},{12,36},{16,40},{20,44},{24,48},{28,52},{32,5... | collective-permute-start | bytes 393224 | tf_op jit(solution)/shard_map/ppermute | solution.py:17
  75.9 0.7 constant_dynamic-update-slice_fusion.5
  76.5 0.7 constant_dynamic-update-slice_fusion.4
  77.2 1.6 constant_dynamic-update-slice_fusion.3
  78.8 2.9 broadcast_in_dim.192
  81.6 12.5 %all-to-all-start.1 = ((bf16[32,512,128]{2,1,0:T(8,128)(2,1)}), bf16[32,512,128]{2,1,0:T(8,128)(2,1)}, u32[]{:S(2)}, u32[]{:S(2)}) async-start(bf16[32,512,128]{2,1,0:T(8,128)(2,1)} %broadcast_in_dim.192), calls=%async_computation.1 | async-start | bytes 8388608 | tf_op jit(solution)/shard_map/all_to_all | solution.py:162
  94.1 1.6 constant_dynamic-update-slice_fusion.2
  95.7 1.6 constant_dynamic-update-slice_fusion.1
  97.3 0.7 constant_dynamic-update-slice_fusion
  97.9 1.8 gather_fusion
  100.0 9.2 %convolution_convert_fusion.1 = bf16[1024,32,128]{2,0,1:T(8,128)(2,1)} fusion(bf16[32,512,128]{2,1,0:T(8,128)(2,1)} %all-to-all-done, bf16[1024,512]{1,0:T(8,128)(2,1)S(1)} %bitcast_select_fusion.4), kind=kOutput, calls=%fused_computation.26 | convolution fusion | flops 4299161600 | bytes 13631488 | tf_op jit(solution)/shard_map/sl,hlc->hsc/dot_general | solution.py:24
  109.2 9.1 %fusion.20 = f32[32,4,256,64]{2,3,1,0:T(8,128)} fusion(bf16[32,4,256,128]{3,2,1,0:T(8,128)(2,1)} %bitcast.110, bf16[4,64,32,128]{3,2,1,0:T(8,128)(2,1)S(1)} %bitcast.97), kind=kOutput, calls=%fused_computation.42 | convolution fusion | flops 536870912 | bytes 18874368 | tf_op jit(solution)/shard_map/qbhd,hqkd->hqbk/dot_general | solution.py:37
  118.3 10.4 %fusion.85 = (f32[32,4,64]{2,1,0:T(4,128)S(1)}, f32[32,4,64,256]{3,2,1,0:T(8,128)S(1)}) fusion(f32[32,4,256,64]{2,3,1,0:T(8,128)} %fusion.20, pred[4,64,256]{2,1,0:T(8,128)(4,1)S(1)} %compare_and_fusion), kind=kOutput, calls=%fused_computation.234 | output fusion | flops 12583167 | bytes 16875520 | tf_op jit(solution)/shard_map/sub | solution.py:42
  128.7 3.2 copy-done.5
  131.9 2.8 fusion.13
  134.7 3.1 all-to-all-done.1
  137.8 10.4 %convolution_convert_fusion = bf16[1024,32,128]{2,0,1:T(8,128)(2,1)} fusion(bf16[32,512,128]{2,1,0:T(8,128)(2,1)} %all-to-all-done.1, bf16[1024,512]{1,0:T(8,128)(2,1)} %copy-done.9), kind=kOutput, calls=%fused_computation.25 | convolution fusion | flops 4299161600 | bytes 13631488 | tf_op jit(solution)/shard_map/sl,hlc->hsc/dot_general | solution.py:24
  148.2 4.6 %convolution_convert_fusion.2 = bf16[32,4,256,128]{3,2,1,0:T(8,128)(2,1)} fusion(bf16[32,4,64,256]{3,2,1,0:T(8,128)(2,1)S(1)} %copy-done.3, bf16[32,4,64,128]{3,2,1,0:T(8,128)(2,1)S(1)} %bitcast.100), kind=kOutput, calls=%fused_computation.27 | convolution fusion | flops 541065216 | bytes 14680064 | tf_op jit(solution)/shard_map/hqbk,hqbd->hqkd/dot_general | solution.py:47
  152.8 5.4 %multiply_reduce_fusion = f32[32,4,64]{2,1,0:T(4,128)S(1)} fusion(bf16[32,4,64,128]{3,2,1,0:T(8,128)(2,1)S(1)} %bitcast.101, bf16[32,4,64,256]{3,2,1,0:T(8,128)(2,1)S(1)} %copy-done.3, bf16[32,4,256,128]{3,2,1,0:T(8,128)(2,1)} %bitcast.108), kind=kOutput, calls=%fused_computation.33 | convolution fusion | flops 540008448 | bytes 14712832 | tf_op jit(solution)/shard_map/hqbk,hqkd->hqbd/dot_general | solution.py:61
  158.2 12.6 %fusion.5 = bf16[32,4,64,256]{3,2,1,0:T(8,128)(2,1)} fusion(f32[32,4,64]{2,1,0:T(4,128)S(1)} %multiply_reduce_fusion, f32[32,4,64,256]{3,2,1,0:T(8,128)} %copy-done.5, f32[32,4,64]{2,1,0:T(4,128)S(1)} %get-tuple-element.28, bf16[32,4,256,128]{3,2,1,0:T(8,128)(2,1)} %bitcast.109, bf16[32,4,64,128]{3,2,1,0:T(8,128)(2,1)} %bitcast.99), kind=kOutput, calls=%fused_computation.18 | convolution fusion | flops 545259520 | bytes 23134208 | tf_op jit(solution)/shard_map/hqbd,hqkd->hqbk/dot_general | solution.py:65
  170.8 9.6 %multiply_convert_fusion = bf16[32,4,256,128]{3,2,1,0:T(8,128)(2,1)} fusion(bf16[32,4,64,256]{3,2,1,0:T(8,128)(2,1)} %fusion.5, bf16[4,64,32,128]{3,2,1,0:T(8,128)(2,1)S(1)} %bitcast.98), kind=kOutput, calls=%fused_computation.10 | convolution fusion | flops 545259520 | bytes 14680064 | tf_op jit(solution)/shard_map/hqbk,qbhd->hqkd/dot_general | solution.py:74
  180.5 8.4 %fusion.86 = f32[1024,512,1]{0,1,2:T(8,128)S(1)} fusion(bf16[32,1024,128]{2,1,0:T(8,128)(2,1)} %bitcast.102, bf16[32,512,128]{2,1,0:T(8,128)(2,1)} %all-to-all-done), kind=kOutput, calls=%fused_computation.235 | convolution fusion | flops 4294967296 | bytes 14680064 | tf_op jit(solution)/shard_map/hsc,hlc->sl/dot_general | solution.py:77
  188.8 8.0 %bitcast_add_fusion = f32[1024,512]{0,1:T(8,128)} fusion(f32[1024,512,1]{0,1,2:T(8,128)S(1)} %fusion.86, bf16[32,1024,128]{2,1,0:T(8,128)(2,1)S(1)} %bitcast.107, bf16[32,512,128]{2,1,0:T(8,128)(2,1)} %all-to-all-done.1), kind=kOutput, calls=%fused_computation.40 | convolution fusion | flops 4295491584 | bytes 16777216 | tf_op jit(solution)/shard_map/hsc,hlc->sl/dot_general | solution.py:79
  196.9 4.0 %all-to-all-start.2 = ((f32[4,1024,128]{1,2,0:T(8,128)}), f32[4,1024,128]{1,2,0:T(8,128)S(1)}, u32[]{:S(2)}, u32[]{:S(2)}) async-start(f32[4,1024,128]{1,2,0:T(8,128)} %bitcast.120), calls=%async_computation.2 | async-start | bytes 4194304 | tf_op jit(solution)/shard_map/all_to_all | solution.py:178
  201.1 1.0 copy-done.7
  202.1 9.6 %convert_bitcast_fusion = bf16[32,512,128]{1,2,0:T(8,128)(2,1)} fusion(bf16[32,1024,128]{2,1,0:T(8,128)(2,1)} %bitcast.104, bf16[1024,512,1]{1,0,2:T(8,128)(2,1)S(1)} %bitcast.121), kind=kOutput, calls=%fused_computation.30 | convolution fusion | flops 4297064448 | bytes 13631488 | tf_op jit(solution)/shard_map/sl,hsc->hlc/dot_general | solution.py:28
  211.7 16.4 %all-to-all-done.2 = f32[4,1024,128]{1,2,0:T(8,128)S(1)} async-done(((f32[4,1024,128]{1,2,0:T(8,128)}), f32[4,1024,128]{1,2,0:T(8,128)S(1)}, u32[]{:S(2)}, u32[]{:S(2)}) %all-to-all-start.2) | async-done | bytes 2097184 | tf_op jit(solution)/shard_map/all_to_all | solution.py:178
  228.1 13.2 %all-to-all-start.4 = ((bf16[32,512,128]{1,2,0:T(8,128)(2,1)}), bf16[32,512,128]{1,2,0:T(8,128)(2,1)}, u32[]{:S(2)}, u32[]{:S(2)}) async-start(bf16[32,512,128]{1,2,0:T(8,128)(2,1)} %convert_bitcast_fusion), calls=%async_computation.4 | async-start | bytes 8388608 | tf_op jit(solution)/shard_map/all_to_all | solution.py:165
  241.3 9.6 %convert_bitcast_fusion.1 = bf16[32,512,128]{1,2,0:T(8,128)(2,1)} fusion(bf16[32,1024,128]{2,1,0:T(8,128)(2,1)} %bitcast.103, bf16[1024,512,1]{1,0,2:T(8,128)(2,1)S(1)} %bitcast.122), kind=kOutput, calls=%fused_computation.31 | convolution fusion | flops 4297064448 | bytes 13631488 | tf_op jit(solution)/shard_map/sl,hsc->hlc/dot_general | solution.py:28
  250.9 42.0 %all-to-all-done.4 = bf16[32,512,128]{1,2,0:T(8,128)(2,1)} async-done(((bf16[32,512,128]{1,2,0:T(8,128)(2,1)}), bf16[32,512,128]{1,2,0:T(8,128)(2,1)}, u32[]{:S(2)}, u32[]{:S(2)}) %all-to-all-start.4) | async-done | bytes 4194336 | tf_op jit(solution)/shard_map/all_to_all | solution.py:165
  292.9 9.6 %all-to-all-start.3 = ((bf16[32,512,128]{1,2,0:T(8,128)(2,1)}), bf16[32,512,128]{1,2,0:T(8,128)(2,1)}, u32[]{:S(2)}, u32[]{:S(2)}) async-start(bf16[32,512,128]{1,2,0:T(8,128)(2,1)} %convert_bitcast_fusion.1), calls=%async_computation.3 | async-start | bytes 8388608 | tf_op jit(solution)/shard_map/all_to_all | solution.py:165
  302.5 6.4 %fusion.14 = bf16[4,64,32,128]{3,1,2,0:T(8,128)(2,1)S(1)} fusion(bf16[32,4,256,128]{3,2,1,0:T(8,128)(2,1)} %bitcast.111, bf16[32,4,64,256]{3,2,1,0:T(8,128)(2,1)} %fusion.5), kind=kOutput, calls=%fused_computation.39 | convolution fusion | flops 538968064 | bytes 14680064 | tf_op jit(solution)/shard_map/hqbk,hqkd->qbhd/dot_general | solution.py:70
  308.9 2.7 copy.82
  312.4 3.7 collective-permute-start.11
  316.4 1.9 collective-permute-start.10
  318.7 2.5 collective-permute-start.9
  321.5 5.2 %collective-permute-start.8 = (f32[2,8192]{1,0:T(2,128)S(1)}, f32[2,8192]{1,0:T(2,128)S(1)}, u32[]{:S(2)}, u32[]{:S(2)}) collective-permute-start(f32[2,8192]{1,0:T(2,128)S(1)} %fusion.45), channel_id=1, source_target_pairs={{12,0},{16,4},{20,8},{24,12},{28,16},{32,20},{36,24},{40,28},{44,3... | collective-permute-start | bytes 196616 | tf_op jit(solution)/shard_map/ppermute | solution.py:17
  327.0 1.9 collective-permute-start.6
  329.5 32.6 %collective-permute-done.6 = f32[2,8192]{1,0:T(2,128)S(1)} collective-permute-done((f32[2,8192]{1,0:T(2,128)S(1)}, f32[2,8192]{1,0:T(2,128)S(1)}, u32[]{:S(2)}, u32[]{:S(2)}) %collective-permute-start.6) | collective-permute-done | bytes 65568 | tf_op jit(solution)/shard_map/ppermute | solution.py:17
  362.1 1.9 collective-permute-start.7
  365.3 7.4 %collective-permute-done.7 = f32[2,8192]{1,0:T(2,128)S(1)} collective-permute-done((f32[2,8192]{1,0:T(2,128)S(1)}, f32[2,8192]{1,0:T(2,128)S(1)}, u32[]{:S(2)}, u32[]{:S(2)}) %collective-permute-start.7) | collective-permute-done | bytes 65568 | tf_op jit(solution)/shard_map/ppermute | solution.py:17
  373.1 0.7 reshape.725
  373.8 2.9 convert_reduce_fusion
  376.8 2.8 convert_reduce_fusion.1
  379.6 1.0 copy.87
  (157 shorter events, 10.7 us)
Async XLA Ops:
  0.6 108.6 %copy-start = (bf16[256,32,128]{2,1,0:T(8,128)(2,1)S(1)}, bf16[256,32,128]{2,1,0:T(8,128)(2,1)}, u32[]{:S(2)}) copy-start(bf16[256,32,128]{2,1,0:T(8,128)(2,1)} %param.9) | copy-start | bytes 6291460
  4.7 8.1 %copy-start.11 = (s32[128,4]{0,1:T(4,128)S(1)}, s32[128,4]{0,1:T(4,128)}, u32[]{:S(2)}) copy-start(s32[128,4]{0,1:T(4,128)} %param.13) | copy-start | bytes 6148
  4.7 8.9 %copy-start.6 = (bf16[256,512]{1,0:T(8,128)(2,1)S(1)}, bf16[256,512]{1,0:T(8,128)(2,1)}, u32[]{:S(2)}) copy-start(bf16[256,512]{1,0:T(8,128)(2,1)} %param.8) | copy-start | bytes 786436
  4.7 36.6 %copy-start.2 = (s32[8192]{0:T(1024)S(1)}, s32[8192]{0:T(1024)}, u32[]{:S(2)}) copy-start(s32[8192]{0:T(1024)} %param.12) | copy-start | bytes 98308
  4.7 74.1 %all-to-all-start = ((bf16[32,512,128]{2,1,0:T(8,128)(2,1)}), bf16[32,512,128]{2,1,0:T(8,128)(2,1)}, u32[]{:S(2)}, u32[]{:S(2)}) async-start(bf16[32,512,128]{2,1,0:T(8,128)(2,1)} %broadcast_in_dim.110), calls=%async_computation | async-start | bytes 8388608 | tf_op jit(solution)/shard_map/all_to_all | solution.py:162
  14.2 51.6 %collective-permute-start = (bf16[2,64,512]{2,1,0:T(8,128)(2,1)S(1)}, bf16[2,64,512]{2,1,0:T(8,128)(2,1)S(1)}, u32[]{:S(2)}, u32[]{:S(2)}) collective-permute-start(bf16[2,64,512]{2,1,0:T(8,128)(2,1)S(1)} %broadcast_select_fusion.6), channel_id=1, source_target_pairs={{0,4},{4,8},{8,12},{12,16},{16,20},{20,24},{24,28},{28,32},{32,36}... | collective-permute-start | bytes 393224 | tf_op jit(solution)/shard_map/ppermute | solution.py:17
  18.5 58.0 %collective-permute-start.1 = (bf16[2,64,512]{2,1,0:T(8,128)(2,1)S(1)}, bf16[2,64,512]{2,1,0:T(8,128)(2,1)S(1)}, u32[]{:S(2)}, u32[]{:S(2)}) collective-permute-start(bf16[2,64,512]{2,1,0:T(8,128)(2,1)S(1)} %broadcast_select_fusion.5), channel_id=1, source_target_pairs={{0,8},{4,12},{8,16},{12,20},{16,24},{20,28},{24,32},{28,36},{32,40... | collective-permute-start | bytes 393224 | tf_op jit(solution)/shard_map/ppermute | solution.py:17
  24.1 53.1 %collective-permute-start.2 = (bf16[2,64,512]{2,1,0:T(8,128)(2,1)S(1)}, bf16[2,64,512]{2,1,0:T(8,128)(2,1)}, u32[]{:S(2)}, u32[]{:S(2)}) collective-permute-start(bf16[2,64,512]{2,1,0:T(8,128)(2,1)S(1)} %broadcast_select_fusion.4), channel_id=1, source_target_pairs={{0,12},{4,16},{8,20},{12,24},{16,28},{20,32},{24,36},{28,40},{32,4... | collective-permute-start | bytes 393224 | tf_op jit(solution)/shard_map/ppermute | solution.py:17
  27.8 66.3 %collective-permute-start.3 = (bf16[2,64,512]{2,1,0:T(8,128)(2,1)S(1)}, bf16[2,64,512]{2,1,0:T(8,128)(2,1)}, u32[]{:S(2)}, u32[]{:S(2)}) collective-permute-start(bf16[2,64,512]{2,1,0:T(8,128)(2,1)S(1)} %broadcast_select_fusion.3), channel_id=1, source_target_pairs={{0,16},{4,20},{8,24},{12,28},{16,32},{20,36},{24,40},{28,44},{32,4... | collective-permute-start | bytes 393224 | tf_op jit(solution)/shard_map/ppermute | solution.py:17
  33.2 62.4 %collective-permute-start.4 = (bf16[2,64,512]{2,1,0:T(8,128)(2,1)}, bf16[2,64,512]{2,1,0:T(8,128)(2,1)}, u32[]{:S(2)}, u32[]{:S(2)}) collective-permute-start(bf16[2,64,512]{2,1,0:T(8,128)(2,1)} %broadcast_select_fusion.2), channel_id=1, source_target_pairs={{0,20},{4,24},{8,28},{12,32},{16,36},{20,40},{24,44},{28,48},{32,5... | collective-permute-start | bytes 393224 | tf_op jit(solution)/shard_map/ppermute | solution.py:17
  50.2 15.6 %copy-start.10 = (bf16[2,64,512]{2,1,0:T(8,128)(2,1)S(1)}, bf16[2,64,512]{2,1,0:T(8,128)(2,1)}, u32[]{:S(2)}) copy-start(bf16[2,64,512]{2,1,0:T(8,128)(2,1)} %broadcast_select_fusion.1) | copy-start | bytes 393220
  65.8 31.4 %collective-permute-start.5 = (bf16[2,64,512]{2,1,0:T(8,128)(2,1)S(1)}, bf16[2,64,512]{2,1,0:T(8,128)(2,1)S(1)}, u32[]{:S(2)}, u32[]{:S(2)}) collective-permute-start(bf16[2,64,512]{2,1,0:T(8,128)(2,1)S(1)} %copy-done.10), channel_id=1, source_target_pairs={{0,24},{4,28},{8,32},{12,36},{16,40},{20,44},{24,48},{28,52},{32,5... | collective-permute-start | bytes 393224 | tf_op jit(solution)/shard_map/ppermute | solution.py:17
  81.6 56.2 %all-to-all-start.1 = ((bf16[32,512,128]{2,1,0:T(8,128)(2,1)}), bf16[32,512,128]{2,1,0:T(8,128)(2,1)}, u32[]{:S(2)}, u32[]{:S(2)}) async-start(bf16[32,512,128]{2,1,0:T(8,128)(2,1)} %broadcast_in_dim.192), calls=%async_computation.1 | async-start | bytes 8388608 | tf_op jit(solution)/shard_map/all_to_all | solution.py:162
  100.0 9.2 %copy-start.9 = (bf16[1024,512]{1,0:T(8,128)(2,1)}, bf16[1024,512]{1,0:T(8,128)(2,1)S(1)}, u32[]{:S(2)}) copy-start(bf16[1024,512]{1,0:T(8,128)(2,1)S(1)} %bitcast_select_fusion.4) | copy-start | bytes 3145732
  128.7 3.2 copy-start.5
  137.8 10.4 %copy-start.3 = (bf16[32,4,64,256]{3,2,1,0:T(8,128)(2,1)S(1)}, bf16[32,4,64,256]{3,2,1,0:T(8,128)(2,1)}, u32[]{:S(2)}) copy-start(bf16[32,4,64,256]{3,2,1,0:T(8,128)(2,1)} %fusion.13) | copy-start | bytes 12582916
  137.8 10.4 %copy-start.4 = (bf16[256,32,128]{2,0,1:T(8,128)(2,1)S(1)}, bf16[256,32,128]{2,0,1:T(8,128)(2,1)}, u32[]{:S(2)}) copy-start(bf16[256,32,128]{2,0,1:T(8,128)(2,1)} %copy.79) | copy-start | bytes 6291460
  170.8 18.0 %slice-start = ((s8[8388608]{0:T(1024)(128)(4,1)}), s8[4194304]{0:T(1024)(128)(4,1)S(1)}, s32[]{:S(2)}) async-start(s8[8388608]{0:T(1024)(128)(4,1)} %bitcast.105), calls=%async_computation.5 | async-start | bytes 8388608
  180.5 8.4 %slice-start.1 = ((s8[8388608]{0:T(1024)(128)(4,1)}), s8[4194304]{0:T(1024)(128)(4,1)S(1)}, s32[]{:S(2)}) async-start(s8[8388608]{0:T(1024)(128)(4,1)} %bitcast.105), calls=%async_computation.6 | async-start | bytes 8388608
  196.9 31.2 %all-to-all-start.2 = ((f32[4,1024,128]{1,2,0:T(8,128)}), f32[4,1024,128]{1,2,0:T(8,128)S(1)}, u32[]{:S(2)}, u32[]{:S(2)}) async-start(f32[4,1024,128]{1,2,0:T(8,128)} %bitcast.120), calls=%async_computation.2 | async-start | bytes 4194304 | tf_op jit(solution)/shard_map/all_to_all | solution.py:178
  201.0 1.0 copy-start.7
  211.7 29.6 %copy-start.8 = (bf16[16,64,512]{2,1,0:T(8,128)(2,1)S(1)}, bf16[16,64,512]{2,1,0:T(8,128)(2,1)}, u32[]{:S(2)}) copy-start(bf16[16,64,512]{2,1,0:T(8,128)(2,1)} %copy-done.7) | copy-start | bytes 3145732
  228.1 64.9 %all-to-all-start.4 = ((bf16[32,512,128]{1,2,0:T(8,128)(2,1)}), bf16[32,512,128]{1,2,0:T(8,128)(2,1)}, u32[]{:S(2)}, u32[]{:S(2)}) async-start(bf16[32,512,128]{1,2,0:T(8,128)(2,1)} %convert_bitcast_fusion), calls=%async_computation.4 | async-start | bytes 8388608 | tf_op jit(solution)/shard_map/all_to_all | solution.py:165
  292.9 83.8 %all-to-all-start.3 = ((bf16[32,512,128]{1,2,0:T(8,128)(2,1)}), bf16[32,512,128]{1,2,0:T(8,128)(2,1)}, u32[]{:S(2)}, u32[]{:S(2)}) async-start(bf16[32,512,128]{1,2,0:T(8,128)(2,1)} %convert_bitcast_fusion.1), calls=%async_computation.3 | async-start | bytes 8388608 | tf_op jit(solution)/shard_map/all_to_all | solution.py:165
  312.4 51.9 %collective-permute-start.11 = (f32[2,8192]{1,0:T(2,128)S(1)}, f32[2,8192]{1,0:T(2,128)S(1)}, u32[]{:S(2)}, u32[]{:S(2)}) collective-permute-start(f32[2,8192]{1,0:T(2,128)S(1)} %fusion.39), channel_id=1, source_target_pairs={{24,0},{28,4},{32,8},{36,12},{40,16},{44,20},{48,24},{52,28},{56,3... | collective-permute-start | bytes 196616 | tf_op jit(solution)/shard_map/ppermute | solution.py:17
  316.4 48.1 %collective-permute-start.10 = (f32[2,8192]{1,0:T(2,128)S(1)}, f32[2,8192]{1,0:T(2,128)S(1)}, u32[]{:S(2)}, u32[]{:S(2)}) collective-permute-start(f32[2,8192]{1,0:T(2,128)S(1)} %fusion.41), channel_id=1, source_target_pairs={{20,0},{24,4},{28,8},{32,12},{36,16},{40,20},{44,24},{48,28},{52,3... | collective-permute-start | bytes 196616 | tf_op jit(solution)/shard_map/ppermute | solution.py:17
  318.7 46.1 %collective-permute-start.9 = (f32[2,8192]{1,0:T(2,128)S(1)}, f32[2,8192]{1,0:T(2,128)S(1)}, u32[]{:S(2)}, u32[]{:S(2)}) collective-permute-start(f32[2,8192]{1,0:T(2,128)S(1)} %fusion.43), channel_id=1, source_target_pairs={{16,0},{20,4},{24,8},{28,12},{32,16},{36,20},{40,24},{44,28},{48,3... | collective-permute-start | bytes 196616 | tf_op jit(solution)/shard_map/ppermute | solution.py:17
  321.5 43.6 %collective-permute-start.8 = (f32[2,8192]{1,0:T(2,128)S(1)}, f32[2,8192]{1,0:T(2,128)S(1)}, u32[]{:S(2)}, u32[]{:S(2)}) collective-permute-start(f32[2,8192]{1,0:T(2,128)S(1)} %fusion.45), channel_id=1, source_target_pairs={{12,0},{16,4},{20,8},{24,12},{28,16},{32,20},{36,24},{40,28},{44,3... | collective-permute-start | bytes 196616 | tf_op jit(solution)/shard_map/ppermute | solution.py:17
  327.0 35.1 %collective-permute-start.6 = (f32[2,8192]{1,0:T(2,128)S(1)}, f32[2,8192]{1,0:T(2,128)S(1)}, u32[]{:S(2)}, u32[]{:S(2)}) collective-permute-start(f32[2,8192]{1,0:T(2,128)S(1)} %fusion.49), channel_id=1, source_target_pairs={{4,0},{8,4},{12,8},{16,12},{20,16},{24,20},{28,24},{32,28},{36,32}... | collective-permute-start | bytes 196616 | tf_op jit(solution)/shard_map/ppermute | solution.py:17
  362.1 10.7 %collective-permute-start.7 = (f32[2,8192]{1,0:T(2,128)S(1)}, f32[2,8192]{1,0:T(2,128)S(1)}, u32[]{:S(2)}, u32[]{:S(2)}) collective-permute-start(f32[2,8192]{1,0:T(2,128)S(1)} %fusion.47), channel_id=1, source_target_pairs={{8,0},{12,4},{16,8},{20,12},{24,16},{28,20},{32,24},{36,28},{40,32... | collective-permute-start | bytes 196616 | tf_op jit(solution)/shard_map/ppermute | solution.py:17
  373.8 6.8 %copy-start.1 = (bf16[256,32,128]{2,1,0:T(8,128)(2,1)S(1)}, bf16[256,32,128]{2,1,0:T(8,128)(2,1)}, u32[]{:S(2)}) copy-start(bf16[256,32,128]{2,1,0:T(8,128)(2,1)} %param.9) | copy-start | bytes 6291460

commit v5 on v4

--- a/solution.py
+++ b/solution.py
@@ -43,7 +43,6 @@
     softmax_p = exp_scores / jnp.sum(exp_scores, axis=-1, keepdims=True)
     probs_low = softmax_p.astype(jnp.bfloat16)
     g_t = jnp.transpose(g_all, (2, 0, 1, 3))
-    probs_low, value_rows = lax.optimization_barrier((probs_low, value_rows))
     grad_v = jnp.einsum(
         "hqbk,hqbd->hqkd", probs_low, g_t, preferred_element_type=jnp.float32
     ).astype(jnp.bfloat16).reshape(head_count, -1, head_dim)
@@ -173,10 +172,9 @@
     value_part = reduce_runs(grad_w_values)
     key_part = reduce_runs(grad_w_keys)
     grad_weight = jnp.concatenate([key_part, value_part], axis=-1)[None, None]
-    grp_size = lax.axis_size("grp")
-    lat_pieces = jnp.moveaxis(grad_lat.reshape(-1, grp_size, lat_share), 1, 0)
-    lat_pieces = lax.all_to_all(lat_pieces, "grp", 0, 0, tiled=True)
-    lat_shares = jnp.sum(lat_pieces, axis=0).reshape(block_count * TOPK, BLK * lat_share)
+    slot_grads = grad_lat.reshape(block_count, TOPK, BLK, lat_width)
+    lat_shares = lax.psum_scatter(slot_grads, "grp", scatter_dimension=3, tiled=True)
+    lat_shares = lat_shares.reshape(block_count * TOPK, BLK * lat_share)
     flat_pool = pool_index.reshape(-1)
     own_table = (flat_pool[None, :] == jnp.arange(block_count)[:, None]).astype(jnp.float32)
     lat_total = jnp.dot(own_table, lat_shares, precision=lax.Precision.HIGHEST)

time: 386 us -> 368 us (0.953)
  waiting for transfers between devices: 112 us -> 71.4 us
  matrix products: 107 us -> 121 us
  between operations: 1.68 us -> 15 us
    ppermute x12, waiting for transfers between devices: 51.1 us -> 24.4 us  [passed_along(): return lax.ppermute(block, axis, route)]
    all_to_all x1 -> x0, waiting for transfers between devices: 16.4 us -> none  [per_device(): lat_pieces = lax.all_to_all(lat_pieces, 'grp', 0, 0, tiled=True)]
    dot_general x6, matrix products: 1.92 us -> 9.69 us  [per_device(): outgoing = jnp.dot(pick_table, lat_shares, precision=lax.Precision.HIGHEST)]
    all_to_all x1 -> x0, starting transfers between devices: 3.99 us -> none  [per_device(): lat_pieces = lax.all_to_all(lat_pieces, 'grp', 0, 0, tiled=True)]
    unnamed x38 -> x32, local copies, waits for them, and re-layouts: 15.8 us -> 13.9 us
  transfers between devices with their start and end apart: 17 -> 17, of which waited for: 6 -> 6; matrix products, arithmetic and copies ran while one was open for 27% -> 39% of each run, Pallas kernels for 0% -> 0%
where the time goes in v5:
time: 368 us; the launch traced here: 361 us
  matrix products  121 us (33%)
  starting transfers between devices  90.8 us (25%)
  waiting for transfers between devices  71.4 us (19%)
  local copies, waits for them, and re-layouts  40.2 us (11%)
  other arithmetic  22.4 us (6%)
  between operations  15 us (4%)
    ppermute x12, starting transfers between devices, passed_along(): return lax.ppermute(block, axis, route)  46.7 us
    all_to_all x2, waiting for transfers between devices, reduce_runs(): per_run = lax.all_to_all(partials, 'fsdp', 0, 0, tiled=True)  42.6 us
    ppermute x12, waiting for transfers between devices, passed_along(): return lax.ppermute(block, axis, route)  24.4 us
    all_to_all x2, starting transfers between devices, reduce_runs(): per_run = lax.all_to_all(partials, 'fsdp', 0, 0, tiled=True)  23.3 us
    all_to_all x2, starting transfers between devices, gather_heads(): return lax.all_to_all(copies, 'fsdp', 0, 0, tiled=True)  20.5 us
    dot_general x2, matrix products, weight_grad(): jnp.einsum('sl,hsc->hlc', key_lat, grad_part, preferred_element_type=jnp....  19.3 us
    dot_general x2, matrix products, expand(): jnp.einsum('sl,hlc->hsc', key_lat, w_part, preferred_element_type=jnp.flo...  18.4 us
    unnamed x32, local copies, waits for them, and re-layouts  13.9 us
  transfers between devices with their start and end apart: 17, of which 6 were waited for; matrix products, arithmetic and copies ran while one was open for 39% of the time, Pallas kernels for 0%

profile of v5, /device:TPU:120, one launch (start us, length us, event | category | flops | bytes accessed | tf_op | source)
XLA Modules:
  0.0 361.2 jit_solution(8105032255950231872)
XLA Ops:
  7.2 1.1 slice_bitcast_fusion
  8.4 2.9 broadcast_in_dim.110
  11.2 7.9 %all-to-all-start = ((bf16[32,512,128]{2,1,0:T(8,128)(2,1)}), bf16[32,512,128]{2,1,0:T(8,128)(2,1)}, u32[]{:S(2)}, u32[]{:S(2)}) async-start(bf16[32,512,128]{2,1,0:T(8,128)(2,1)} %broadcast_in_dim.110), calls=%async_computation | async-start | bytes 8388608 | tf_op jit(solution)/shard_map/all_to_all | solution.py:161
  20.6 3.4 collective-permute-start
  24.9 4.3 %collective-permute-start.1 = (bf16[2,64,512]{2,1,0:T(8,128)(2,1)S(1)}, bf16[2,64,512]{2,1,0:T(8,128)(2,1)S(1)}, u32[]{:S(2)}, u32[]{:S(2)}) collective-permute-start(bf16[2,64,512]{2,1,0:T(8,128)(2,1)S(1)} %broadcast_select_fusion.5), channel_id=1, source_target_pairs={{0,8},{4,12},{8,16},{12,20},{16,24},{20,28},{24,32},{28,36},{32,40... | collective-permute-start | bytes 393224 | tf_op jit(solution)/shard_map/ppermute | solution.py:17
  30.6 2.8 collective-permute-start.2
  34.2 0.7 broadcast_select_fusion.3
  34.9 3.4 collective-permute-start.3
  39.6 0.7 broadcast_select_fusion.2
  40.3 5.8 %collective-permute-start.4 = (bf16[2,64,512]{2,1,0:T(8,128)(2,1)}, bf16[2,64,512]{2,1,0:T(8,128)(2,1)}, u32[]{:S(2)}, u32[]{:S(2)}) collective-permute-start(bf16[2,64,512]{2,1,0:T(8,128)(2,1)} %broadcast_select_fusion.2), channel_id=1, source_target_pairs={{0,20},{4,24},{8,28},{12,32},{16,36},{20,40},{24,44},{28,48},{32,5... | collective-permute-start | bytes 393224 | tf_op jit(solution)/shard_map/ppermute | solution.py:17
  48.3 6.2 %gather_fusion.1 = s32[1024]{0:T(1024)S(1)} fusion(s32[8192]{0:T(1024)S(1)} %copy-done.1, s32[1024]{0:T(1024)S(1)} %get-tuple-element.36), kind=kCustom, calls=%fused_computation.7 | custom fusion | bytes 12288 | tf_op jit(solution)/shard_map/jit(_take)/gather | solution.py:89
  54.5 1.7 gather_fusion.2
  56.5 0.7 broadcast_select_fusion.1
  57.2 0.7 constant_dynamic-update-slice_fusion.6
  58.1 3.7 %copy.62 = bf16[256,32,128]{2,0,1:T(8,128)(2,1)} copy(bf16[256,32,128]{2,1,0:T(8,128)(2,1)} %param.10) | data formatting | bytes 4194304 | tf_op args[2]
  61.8 10.6 %collective-permute-done = bf16[2,64,512]{2,1,0:T(8,128)(2,1)S(1)} collective-permute-done((bf16[2,64,512]{2,1,0:T(8,128)(2,1)S(1)}, bf16[2,64,512]{2,1,0:T(8,128)(2,1)S(1)}, u32[]{:S(2)}, u32[]{:S(2)}) %collective-permute-start) | collective-permute-done | bytes 131104 | tf_op jit(solution)/shard_map/ppermute | solution.py:17
  72.5 9.8 %collective-permute-start.5 = (bf16[2,64,512]{2,1,0:T(8,128)(2,1)}, bf16[2,64,512]{2,1,0:T(8,128)(2,1)S(1)}, u32[]{:S(2)}, u32[]{:S(2)}) collective-permute-start(bf16[2,64,512]{2,1,0:T(8,128)(2,1)} %broadcast_select_fusion.1), channel_id=1, source_target_pairs={{0,24},{4,28},{8,32},{12,36},{16,40},{20,44},{24,48},{28,52},{32,5... | collective-permute-start | bytes 393224 | tf_op jit(solution)/shard_map/ppermute | solution.py:17
  83.0 0.7 constant_dynamic-update-slice_fusion.4
  83.6 0.7 constant_dynamic-update-slice_fusion.3
  84.3 1.6 constant_dynamic-update-slice_fusion.2
  85.9 1.6 constant_dynamic-update-slice_fusion.1
  88.1 1.8 gather_fusion
  89.9 2.9 broadcast_in_dim.192
  92.9 12.6 %all-to-all-start.1 = ((bf16[32,512,128]{2,1,0:T(8,128)(2,1)}), bf16[32,512,128]{2,1,0:T(8,128)(2,1)}, u32[]{:S(2)}, u32[]{:S(2)}) async-start(bf16[32,512,128]{2,1,0:T(8,128)(2,1)} %broadcast_in_dim.192), calls=%async_computation.1 | async-start | bytes 8388608 | tf_op jit(solution)/shard_map/all_to_all | solution.py:161
  105.4 1.1 broadcast_select_fusion
  106.8 9.2 %convolution_convert_fusion.1 = bf16[1024,32,128]{2,0,1:T(8,128)(2,1)} fusion(bf16[32,512,128]{2,1,0:T(8,128)(2,1)} %all-to-all-done, bf16[1024,512]{1,0:T(8,128)(2,1)S(1)} %bitcast_select_fusion.4), kind=kOutput, calls=%fused_computation.26 | convolution fusion | flops 4299161600 | bytes 13631488 | tf_op jit(solution)/shard_map/sl,hlc->hsc/dot_general | solution.py:24
  116.0 9.1 %fusion.20 = f32[32,4,256,64]{2,3,1,0:T(8,128)} fusion(bf16[32,4,256,128]{3,2,1,0:T(8,128)(2,1)} %bitcast.114, bf16[4,64,32,128]{3,2,1,0:T(8,128)(2,1)S(1)} %bitcast.103), kind=kOutput, calls=%fused_computation.42 | convolution fusion | flops 536870912 | bytes 18874368 | tf_op jit(solution)/shard_map/qbhd,hqkd->hqbk/dot_general | solution.py:37
  125.2 10.5 %fusion.101 = (f32[32,4,64]{2,1,0:T(4,128)S(1)}, f32[32,4,64,256]{3,2,1,0:T(8,128)S(1)}) fusion(f32[32,4,256,64]{2,3,1,0:T(8,128)} %fusion.20, pred[4,64,256]{2,1,0:T(8,128)(4,1)S(1)} %compare_and_fusion), kind=kOutput, calls=%fused_computation.248 | output fusion | flops 12583167 | bytes 16875520 | tf_op jit(solution)/shard_map/sub | solution.py:42
  135.7 3.2 copy-done.10
  138.9 6.0 %convolution_convert_fusion.2 = bf16[32,4,256,128]{3,2,1,0:T(8,128)(2,1)} fusion(bf16[32,4,64,128]{3,2,1,0:T(8,128)(2,1)S(1)} %bitcast.125, f32[32,4,64,256]{3,2,1,0:T(8,128)S(1)} %get-tuple-element.22, f32[32,4,64]{2,1,0:T(4,128)S(1)} %get-tuple-element.21), kind=kOutput, calls=%fused_computation.27 | convolution fusion | flops 545259520 | bytes 18907136 | tf_op jit(solution)/shard_map/hqbk,hqbd->hqkd/dot_general | solution.py:46
  144.9 4.4 %all-to-all-done.1 = bf16[32,512,128]{2,1,0:T(8,128)(2,1)} async-done(((bf16[32,512,128]{2,1,0:T(8,128)(2,1)}), bf16[32,512,128]{2,1,0:T(8,128)(2,1)}, u32[]{:S(2)}, u32[]{:S(2)}) %all-to-all-start.1) | async-done | bytes 4194336 | tf_op jit(solution)/shard_map/all_to_all | solution.py:161
  149.3 9.1 %convolution_convert_fusion = bf16[1024,32,128]{2,0,1:T(8,128)(2,1)} fusion(bf16[32,512,128]{2,1,0:T(8,128)(2,1)} %all-to-all-done.1, bf16[1024,512]{1,0:T(8,128)(2,1)S(1)} %copy-done.8), kind=kOutput, calls=%fused_computation.25 | convolution fusion | flops 4299161600 | bytes 13631488 | tf_op jit(solution)/shard_map/sl,hlc->hsc/dot_general | solution.py:24
  158.5 8.5 %multiply_reduce_fusion = f32[32,4,64]{2,1,0:T(4,128)S(1)} fusion(bf16[32,4,64,128]{3,2,1,0:T(8,128)(2,1)S(1)} %bitcast.126, bf16[32,4,256,128]{3,2,1,0:T(8,128)(2,1)} %bitcast.133, f32[32,4,64,256]{3,2,1,0:T(8,128)} %copy-done.10, f32[32,4,64]{2,1,0:T(4,128)S(1)} %get-tuple-element.21), kind=kOutput, calls=%fused_computation.33 | convolution fusion | flops 544202752 | bytes 18939904 | tf_op jit(solution)/shard_map/hqbk,hqkd->hqbd/dot_general | solution.py:60
  167.0 9.6 %convert_bitcast_fusion = bf16[32,512,128]{1,2,0:T(8,128)(2,1)} fusion(bf16[32,1024,128]{2,1,0:T(8,128)(2,1)} %bitcast.131, bf16[1024,512,1]{1,0,2:T(8,128)(2,1)S(1)} %bitcast.128), kind=kOutput, calls=%fused_computation.30 | convolution fusion | flops 4297064448 | bytes 13631488 | tf_op jit(solution)/shard_map/sl,hsc->hlc/dot_general | solution.py:28
  176.6 12.8 %all-to-all-start.3 = ((bf16[32,512,128]{1,2,0:T(8,128)(2,1)}), bf16[32,512,128]{1,2,0:T(8,128)(2,1)}, u32[]{:S(2)}, u32[]{:S(2)}) async-start(bf16[32,512,128]{1,2,0:T(8,128)(2,1)} %convert_bitcast_fusion), calls=%async_computation.4 | async-start | bytes 8388608 | tf_op jit(solution)/shard_map/all_to_all | solution.py:164
  189.4 12.3 %fusion.5 = bf16[32,4,64,256]{3,2,1,0:T(8,128)(2,1)} fusion(f32[32,4,64]{2,1,0:T(4,128)S(1)} %multiply_reduce_fusion, f32[32,4,64,256]{3,2,1,0:T(8,128)} %copy-done.10, f32[32,4,64]{2,1,0:T(4,128)S(1)} %get-tuple-element.21, bf16[32,4,256,128]{3,2,1,0:T(8,128)(2,1)} %bitcast.134, bf16[32,4,64,128]{3,2,1,0:T(8,128)(2,1)} %bitcast.124), kind=kOutput, calls=%fused_computation.18 | convolution fusion | flops 545259520 | bytes 23134208 | tf_op jit(solution)/shard_map/hqbd,hqkd->hqbk/dot_general | solution.py:64
  201.7 9.5 %multiply_convert_fusion = bf16[32,4,256,128]{3,2,1,0:T(8,128)(2,1)} fusion(bf16[32,4,64,256]{3,2,1,0:T(8,128)(2,1)} %fusion.5, bf16[4,64,32,128]{3,2,1,0:T(8,128)(2,1)S(1)} %bitcast.104), kind=kOutput, calls=%fused_computation.10 | convolution fusion | flops 545259520 | bytes 14680064 | tf_op jit(solution)/shard_map/hqbk,qbhd->hqkd/dot_general | solution.py:73
  211.2 9.7 %convert_bitcast_fusion.1 = bf16[32,512,128]{1,2,0:T(8,128)(2,1)} fusion(bf16[32,1024,128]{2,1,0:T(8,128)(2,1)} %bitcast.112, bf16[1024,512,1]{1,0,2:T(8,128)(2,1)S(1)} %bitcast.129), kind=kOutput, calls=%fused_computation.31 | convolution fusion | flops 4297064448 | bytes 13631488 | tf_op jit(solution)/shard_map/sl,hsc->hlc/dot_general | solution.py:28
  220.9 8.0 %fusion.102 = f32[1024,512,1]{1,0,2:T(8,128)} fusion(bf16[32,1024,128]{2,1,0:T(8,128)(2,1)S(1)} %bitcast.113, bf16[32,512,128]{2,1,0:T(8,128)(2,1)} %all-to-all-done), kind=kOutput, calls=%fused_computation.249 | convolution fusion | flops 4294967296 | bytes 14680064 | tf_op jit(solution)/shard_map/hsc,hlc->sl/dot_general | solution.py:76
  228.9 6.4 %all-to-all-done.3 = bf16[32,512,128]{1,2,0:T(8,128)(2,1)} async-done(((bf16[32,512,128]{1,2,0:T(8,128)(2,1)}), bf16[32,512,128]{1,2,0:T(8,128)(2,1)}, u32[]{:S(2)}, u32[]{:S(2)}) %all-to-all-start.3) | async-done | bytes 4194336 | tf_op jit(solution)/shard_map/all_to_all | solution.py:164
  235.3 10.5 %all-to-all-start.2 = ((bf16[32,512,128]{1,2,0:T(8,128)(2,1)}), bf16[32,512,128]{1,2,0:T(8,128)(2,1)}, u32[]{:S(2)}, u32[]{:S(2)}) async-start(bf16[32,512,128]{1,2,0:T(8,128)(2,1)} %convert_bitcast_fusion.1), calls=%async_computation.3 | async-start | bytes 8388608 | tf_op jit(solution)/shard_map/all_to_all | solution.py:164
  246.0 11.1 %bitcast_add_fusion = f32[1024,512]{1,0:T(8,128)} fusion(f32[1024,512,1]{1,0,2:T(8,128)} %fusion.102, bf16[32,1024,128]{2,1,0:T(8,128)(2,1)} %bitcast.132, bf16[32,512,128]{2,1,0:T(8,128)(2,1)} %all-to-all-done.1), kind=kOutput, calls=%fused_computation.40 | convolution fusion | flops 4295491584 | bytes 16777216 | tf_op jit(solution)/shard_map/hsc,hlc->sl/dot_general | solution.py:78
  257.2 6.4 %fusion.14 = bf16[4,64,32,128]{3,1,2,0:T(8,128)(2,1)S(1)} fusion(bf16[32,4,256,128]{3,2,1,0:T(8,128)(2,1)} %bitcast.115, bf16[32,4,64,256]{3,2,1,0:T(8,128)(2,1)} %fusion.5), kind=kOutput, calls=%fused_computation.39 | convolution fusion | flops 538968064 | bytes 14680064 | tf_op jit(solution)/shard_map/hqbk,hqkd->qbhd/dot_general | solution.py:69
  263.7 2.7 copy.65
  266.3 3.0 convert_reduce_fusion
  269.3 36.2 %all-to-all-done.2 = bf16[32,512,128]{1,2,0:T(8,128)(2,1)} async-done(((bf16[32,512,128]{1,2,0:T(8,128)(2,1)}), bf16[32,512,128]{1,2,0:T(8,128)(2,1)}, u32[]{:S(2)}, u32[]{:S(2)}) %all-to-all-start.2) | async-done | bytes 4194336 | tf_op jit(solution)/shard_map/all_to_all | solution.py:164
  305.6 2.8 convert_reduce_fusion.1
  308.4 1.0 copy.69
  309.4 1.6 fusion.36
  311.1 1.6 fusion.24
  312.7 4.8 %collective-permute-start.11 = (f32[2,8192]{1,0:T(2,128)S(1)}, f32[2,8192]{1,0:T(2,128)S(1)}, u32[]{:S(2)}, u32[]{:S(2)}) collective-permute-start(f32[2,8192]{1,0:T(2,128)S(1)} %fusion.24), channel_id=1, source_target_pairs={{24,0},{28,4},{32,8},{36,12},{40,16},{44,20},{48,24},{52,28},{56,3... | collective-permute-start | bytes 196616 | tf_op jit(solution)/shard_map/ppermute | solution.py:17
  317.5 1.6 fusion.26
  319.1 1.9 collective-permute-start.10
  321.0 1.6 fusion.28
  322.6 3.4 collective-permute-start.9
  326.1 1.6 fusion.30
  327.7 2.8 collective-permute-start.8
  330.5 1.6 fusion.34
  332.1 2.5 collective-permute-start.6
  334.6 1.6 fusion.32
  336.2 6.3 %collective-permute-done.6 = f32[2,8192]{1,0:T(2,128)S(1)} collective-permute-done((f32[2,8192]{1,0:T(2,128)S(1)}, f32[2,8192]{1,0:T(2,128)S(1)}, u32[]{:S(2)}, u32[]{:S(2)}) %collective-permute-start.6) | collective-permute-done | bytes 65568 | tf_op jit(solution)/shard_map/ppermute | solution.py:17
  342.5 1.9 collective-permute-start.7
  345.7 7.4 %collective-permute-done.7 = f32[2,8192]{1,0:T(2,128)S(1)} collective-permute-done((f32[2,8192]{1,0:T(2,128)S(1)}, f32[2,8192]{1,0:T(2,128)S(1)}, u32[]{:S(2)}, u32[]{:S(2)}) %collective-permute-start.7) | collective-permute-done | bytes 65568 | tf_op jit(solution)/shard_map/ppermute | solution.py:17
  353.5 0.7 reshape.725
  (147 shorter events, 11.5 us)
Async XLA Ops:
  7.2 108.9 %copy-start = (bf16[256,32,128]{2,1,0:T(8,128)(2,1)S(1)}, bf16[256,32,128]{2,1,0:T(8,128)(2,1)}, u32[]{:S(2)}) copy-start(bf16[256,32,128]{2,1,0:T(8,128)(2,1)} %param.9) | copy-start | bytes 6291460
  7.2 12.0 %copy-start.9 = (s32[128,4]{0,1:T(4,128)S(1)}, s32[128,4]{0,1:T(4,128)}, u32[]{:S(2)}) copy-start(s32[128,4]{0,1:T(4,128)} %param.13) | copy-start | bytes 6148
  7.2 12.8 %copy-start.3 = (bf16[256,512]{1,0:T(8,128)(2,1)S(1)}, bf16[256,512]{1,0:T(8,128)(2,1)}, u32[]{:S(2)}) copy-start(bf16[256,512]{1,0:T(8,128)(2,1)} %param.8) | copy-start | bytes 786436
  7.2 41.1 %copy-start.1 = (s32[8192]{0:T(1024)S(1)}, s32[8192]{0:T(1024)}, u32[]{:S(2)}) copy-start(s32[8192]{0:T(1024)} %param.12) | copy-start | bytes 98308
  11.2 78.7 %all-to-all-start = ((bf16[32,512,128]{2,1,0:T(8,128)(2,1)}), bf16[32,512,128]{2,1,0:T(8,128)(2,1)}, u32[]{:S(2)}, u32[]{:S(2)}) async-start(bf16[32,512,128]{2,1,0:T(8,128)(2,1)} %broadcast_in_dim.110), calls=%async_computation | async-start | bytes 8388608 | tf_op jit(solution)/shard_map/all_to_all | solution.py:161
  20.6 51.8 %collective-permute-start = (bf16[2,64,512]{2,1,0:T(8,128)(2,1)S(1)}, bf16[2,64,512]{2,1,0:T(8,128)(2,1)S(1)}, u32[]{:S(2)}, u32[]{:S(2)}) collective-permute-start(bf16[2,64,512]{2,1,0:T(8,128)(2,1)S(1)} %broadcast_select_fusion.6), channel_id=1, source_target_pairs={{0,4},{4,8},{8,12},{12,16},{16,20},{20,24},{24,28},{28,32},{32,36}... | collective-permute-start | bytes 393224 | tf_op jit(solution)/shard_map/ppermute | solution.py:17
  24.9 58.0 %collective-permute-start.1 = (bf16[2,64,512]{2,1,0:T(8,128)(2,1)S(1)}, bf16[2,64,512]{2,1,0:T(8,128)(2,1)S(1)}, u32[]{:S(2)}, u32[]{:S(2)}) collective-permute-start(bf16[2,64,512]{2,1,0:T(8,128)(2,1)S(1)} %broadcast_select_fusion.5), channel_id=1, source_target_pairs={{0,8},{4,12},{8,16},{12,20},{16,24},{20,28},{24,32},{28,36},{32,40... | collective-permute-start | bytes 393224 | tf_op jit(solution)/shard_map/ppermute | solution.py:17
  30.6 53.1 %collective-permute-start.2 = (bf16[2,64,512]{2,1,0:T(8,128)(2,1)S(1)}, bf16[2,64,512]{2,1,0:T(8,128)(2,1)S(1)}, u32[]{:S(2)}, u32[]{:S(2)}) collective-permute-start(bf16[2,64,512]{2,1,0:T(8,128)(2,1)S(1)} %broadcast_select_fusion.4), channel_id=1, source_target_pairs={{0,12},{4,16},{8,20},{12,24},{16,28},{20,32},{24,36},{28,40},{32,4... | collective-permute-start | bytes 393224 | tf_op jit(solution)/shard_map/ppermute | solution.py:17
  34.9 49.4 %collective-permute-start.3 = (bf16[2,64,512]{2,1,0:T(8,128)(2,1)}, bf16[2,64,512]{2,1,0:T(8,128)(2,1)}, u32[]{:S(2)}, u32[]{:S(2)}) collective-permute-start(bf16[2,64,512]{2,1,0:T(8,128)(2,1)} %broadcast_select_fusion.3), channel_id=1, source_target_pairs={{0,16},{4,20},{8,24},{12,28},{16,32},{20,36},{24,40},{28,44},{32,4... | collective-permute-start | bytes 393224 | tf_op jit(solution)/shard_map/ppermute | solution.py:17
  40.3 45.6 %collective-permute-start.4 = (bf16[2,64,512]{2,1,0:T(8,128)(2,1)}, bf16[2,64,512]{2,1,0:T(8,128)(2,1)}, u32[]{:S(2)}, u32[]{:S(2)}) collective-permute-start(bf16[2,64,512]{2,1,0:T(8,128)(2,1)} %broadcast_select_fusion.2), channel_id=1, source_target_pairs={{0,20},{4,24},{8,28},{12,32},{16,36},{20,40},{24,44},{28,48},{32,5... | collective-permute-start | bytes 393224 | tf_op jit(solution)/shard_map/ppermute | solution.py:17
  72.5 15.0 %collective-permute-start.5 = (bf16[2,64,512]{2,1,0:T(8,128)(2,1)}, bf16[2,64,512]{2,1,0:T(8,128)(2,1)S(1)}, u32[]{:S(2)}, u32[]{:S(2)}) collective-permute-start(bf16[2,64,512]{2,1,0:T(8,128)(2,1)} %broadcast_select_fusion.1), channel_id=1, source_target_pairs={{0,24},{4,28},{8,32},{12,36},{16,40},{20,44},{24,48},{28,52},{32,5... | collective-permute-start | bytes 393224 | tf_op jit(solution)/shard_map/ppermute | solution.py:17
  92.9 56.4 %all-to-all-start.1 = ((bf16[32,512,128]{2,1,0:T(8,128)(2,1)}), bf16[32,512,128]{2,1,0:T(8,128)(2,1)}, u32[]{:S(2)}, u32[]{:S(2)}) async-start(bf16[32,512,128]{2,1,0:T(8,128)(2,1)} %broadcast_in_dim.192), calls=%async_computation.1 | async-start | bytes 8388608 | tf_op jit(solution)/shard_map/all_to_all | solution.py:161
  106.8 9.2 %copy-start.7 = (bf16[1024,512]{1,0:T(8,128)(2,1)}, bf16[1024,512]{1,0:T(8,128)(2,1)S(1)}, u32[]{:S(2)}) copy-start(bf16[1024,512]{1,0:T(8,128)(2,1)S(1)} %bitcast_select_fusion.4) | copy-start | bytes 3145732
  125.2 13.7 %copy-start.4 = (bf16[256,32,128]{2,0,1:T(8,128)(2,1)S(1)}, bf16[256,32,128]{2,0,1:T(8,128)(2,1)}, u32[]{:S(2)}) copy-start(bf16[256,32,128]{2,0,1:T(8,128)(2,1)} %copy.62) | copy-start | bytes 6291460
  135.7 3.2 copy-start.10
  138.9 10.4 %copy-start.8 = (bf16[1024,512]{1,0:T(8,128)(2,1)S(1)}, bf16[1024,512]{1,0:T(8,128)(2,1)}, u32[]{:S(2)}) copy-start(bf16[1024,512]{1,0:T(8,128)(2,1)} %copy-done.7) | copy-start | bytes 3145732
  149.3 9.2 %copy-start.5 = (bf16[256,32,128]{2,0,1:T(8,128)(2,1)S(1)}, bf16[256,32,128]{2,0,1:T(8,128)(2,1)}, u32[]{:S(2)}) copy-start(bf16[256,32,128]{2,0,1:T(8,128)(2,1)} %copy.62) | copy-start | bytes 6291460
  158.5 8.5 %copy-start.6 = (bf16[16,64,512]{2,1,0:T(8,128)(2,1)S(1)}, bf16[16,64,512]{2,1,0:T(8,128)(2,1)}, u32[]{:S(2)}) copy-start(bf16[16,64,512]{2,1,0:T(8,128)(2,1)} %broadcast_select_fusion) | copy-start | bytes 3145732
  176.6 58.8 %all-to-all-start.3 = ((bf16[32,512,128]{1,2,0:T(8,128)(2,1)}), bf16[32,512,128]{1,2,0:T(8,128)(2,1)}, u32[]{:S(2)}, u32[]{:S(2)}) async-start(bf16[32,512,128]{1,2,0:T(8,128)(2,1)} %convert_bitcast_fusion), calls=%async_computation.4 | async-start | bytes 8388608 | tf_op jit(solution)/shard_map/all_to_all | solution.py:164
  211.2 9.8 %copy-start.2 = (bf16[32,4,256,128]{3,2,1,0:T(8,128)(2,1)S(1)}, bf16[32,4,256,128]{3,2,1,0:T(8,128)(2,1)}, u32[]{:S(2)}) copy-start(bf16[32,4,256,128]{3,2,1,0:T(8,128)(2,1)} %multiply_convert_fusion) | copy-start | bytes 25165828
  235.3 70.2 %all-to-all-start.2 = ((bf16[32,512,128]{1,2,0:T(8,128)(2,1)}), bf16[32,512,128]{1,2,0:T(8,128)(2,1)}, u32[]{:S(2)}, u32[]{:S(2)}) async-start(bf16[32,512,128]{1,2,0:T(8,128)(2,1)} %convert_bitcast_fusion.1), calls=%async_computation.3 | async-start | bytes 8388608 | tf_op jit(solution)/shard_map/all_to_all | solution.py:164
  245.8 63.6 %reduce-scatter.2.cloned.1.call-start = ((), (), s32[]{:S(2)}) async-start(), calls=%async_computation.5 | async-start | bytes 2621440 | tf_op jit(solution)/shard_map/reduce_scatter | solution.py:176
  312.7 32.0 %collective-permute-start.11 = (f32[2,8192]{1,0:T(2,128)S(1)}, f32[2,8192]{1,0:T(2,128)S(1)}, u32[]{:S(2)}, u32[]{:S(2)}) collective-permute-start(f32[2,8192]{1,0:T(2,128)S(1)} %fusion.24), channel_id=1, source_target_pairs={{24,0},{28,4},{32,8},{36,12},{40,16},{44,20},{48,24},{52,28},{56,3... | collective-permute-start | bytes 196616 | tf_op jit(solution)/shard_map/ppermute | solution.py:17
  319.1 25.9 %collective-permute-start.10 = (f32[2,8192]{1,0:T(2,128)S(1)}, f32[2,8192]{1,0:T(2,128)S(1)}, u32[]{:S(2)}, u32[]{:S(2)}) collective-permute-start(f32[2,8192]{1,0:T(2,128)S(1)} %fusion.26), channel_id=1, source_target_pairs={{20,0},{24,4},{28,8},{32,12},{36,16},{40,20},{44,24},{48,28},{52,3... | collective-permute-start | bytes 196616 | tf_op jit(solution)/shard_map/ppermute | solution.py:17
  322.6 22.6 %collective-permute-start.9 = (f32[2,8192]{1,0:T(2,128)S(1)}, f32[2,8192]{1,0:T(2,128)S(1)}, u32[]{:S(2)}, u32[]{:S(2)}) collective-permute-start(f32[2,8192]{1,0:T(2,128)S(1)} %fusion.28), channel_id=1, source_target_pairs={{16,0},{20,4},{24,8},{28,12},{32,16},{36,20},{40,24},{44,28},{48,3... | collective-permute-start | bytes 196616 | tf_op jit(solution)/shard_map/ppermute | solution.py:17
  327.7 17.8 %collective-permute-start.8 = (f32[2,8192]{1,0:T(2,128)S(1)}, f32[2,8192]{1,0:T(2,128)S(1)}, u32[]{:S(2)}, u32[]{:S(2)}) collective-permute-start(f32[2,8192]{1,0:T(2,128)S(1)} %fusion.30), channel_id=1, source_target_pairs={{12,0},{16,4},{20,8},{24,12},{28,16},{32,20},{36,24},{40,28},{44,3... | collective-permute-start | bytes 196616 | tf_op jit(solution)/shard_map/ppermute | solution.py:17
  332.1 10.4 %collective-permute-start.6 = (f32[2,8192]{1,0:T(2,128)S(1)}, f32[2,8192]{1,0:T(2,128)S(1)}, u32[]{:S(2)}, u32[]{:S(2)}) collective-permute-start(f32[2,8192]{1,0:T(2,128)S(1)} %fusion.34), channel_id=1, source_target_pairs={{4,0},{8,4},{12,8},{16,12},{20,16},{24,20},{28,24},{32,28},{36,32}... | collective-permute-start | bytes 196616 | tf_op jit(solution)/shard_map/ppermute | solution.py:17
  342.5 10.7 %collective-permute-start.7 = (f32[2,8192]{1,0:T(2,128)S(1)}, f32[2,8192]{1,0:T(2,128)S(1)}, u32[]{:S(2)}, u32[]{:S(2)}) collective-permute-start(f32[2,8192]{1,0:T(2,128)S(1)} %fusion.32), channel_id=1, source_target_pairs={{8,0},{12,4},{16,8},{20,12},{24,16},{28,20},{32,24},{36,28},{40,32... | collective-permute-start | bytes 196616 | tf_op jit(solution)/shard_map/ppermute | solution.py:17
Sparse Core Ops, SparseCore 0:
  257.3 49.1 reduce-scatter.1

commit v6 on v5

--- a/solution.py
+++ b/solution.py
@@ -172,9 +172,15 @@
     value_part = reduce_runs(grad_w_values)
     key_part = reduce_runs(grad_w_keys)
     grad_weight = jnp.concatenate([key_part, value_part], axis=-1)[None, None]
-    slot_grads = grad_lat.reshape(block_count, TOPK, BLK, lat_width)
-    lat_shares = lax.psum_scatter(slot_grads, "grp", scatter_dimension=3, tiled=True)
-    lat_shares = lat_shares.reshape(block_count * TOPK, BLK * lat_share)
+    grp_size = lax.axis_size("grp")
+    grp_pos = lax.axis_index("grp")
+    lat_pieces = grad_lat.reshape(-1, grp_size, lat_share)
+    lat_sum = lax.dynamic_index_in_dim(lat_pieces, grp_pos, 1, False)
+    for shift in range(1, grp_size):
+        piece = lax.dynamic_index_in_dim(lat_pieces, (grp_pos + shift) % grp_size, 1, False)
+        route = [(i, (i + shift) % grp_size) for i in range(grp_size)]
+        lat_sum = lat_sum + lax.ppermute(piece, "grp", route)
+    lat_shares = lat_sum.reshape(block_count * TOPK, BLK * lat_share)
     flat_pool = pool_index.reshape(-1)
     own_table = (flat_pool[None, :] == jnp.arange(block_count)[:, None]).astype(jnp.float32)
     lat_total = jnp.dot(own_table, lat_shares, precision=lax.Precision.HIGHEST)

time: 368 us -> 349 us (0.948)
  between operations: 15 us -> 1.78 us
  waiting for transfers between devices: 71.4 us -> 59.6 us
  matrix products: 121 us -> 113 us
  other arithmetic: 22.4 us -> 28.7 us
  local copies, waits for them, and re-layouts: 40.2 us -> 46.4 us
    all_to_all x2, waiting for transfers between devices: 42.6 us -> 13.7 us  [reduce_runs(): per_run = lax.all_to_all(partials, 'fsdp', 0, 0, tiled=True)]
    ppermute x12, waiting for transfers between devices: 24.4 us -> 37.6 us  [passed_along(): return lax.ppermute(block, axis, route)]
    dot_general x6, matrix products: 9.69 us -> 1.92 us  [per_device(): outgoing = jnp.dot(pick_table, lat_shares, precision=lax.Precision.HIGHEST)]
    dynamic_slice x0 -> x5, local copies, waits for them, and re-layouts: none -> 6.47 us  [the longest x3 5.11 us: per_device(): lax.dynamic_index_in_dim(lat_pieces, (grp_pos + shift) % grp_size, 1, False)]
    ppermute x0 -> x3, waiting for transfers between devices: none -> 5.25 us  [per_device(): lat_sum = lat_sum + lax.ppermute(piece, 'grp', route)]
    unnamed x32 -> x68, local copies, waits for them, and re-layouts: 13.9 us -> 13.5 us
  transfers between devices with their start and end apart: 17 -> 19, of which waited for: 6 -> 6; matrix products, arithmetic and copies ran while one was open for 39% -> 36% of each run, Pallas kernels for 0% -> 0%
where the time goes in v6:
time: 349 us; the launch traced here: 343 us
  matrix products  113 us (32%)
  starting transfers between devices  93.6 us (27%)
  waiting for transfers between devices  59.6 us (17%)
  local copies, waits for them, and re-layouts  46.4 us (13%)
  other arithmetic  28.7 us (8%)
    ppermute x12, starting transfers between devices, passed_along(): return lax.ppermute(block, axis, route)  48.7 us
    ppermute x12, waiting for transfers between devices, passed_along(): return lax.ppermute(block, axis, route)  37.6 us
    all_to_all x2, starting transfers between devices, reduce_runs(): per_run = lax.all_to_all(partials, 'fsdp', 0, 0, tiled=True)  21.3 us
    all_to_all x2, starting transfers between devices, gather_heads(): return lax.all_to_all(copies, 'fsdp', 0, 0, tiled=True)  20.6 us
    dot_general x2, matrix products, weight_grad(): jnp.einsum('sl,hsc->hlc', key_lat, grad_part, preferred_element_type=jnp....  20.1 us
    dot_general x2, matrix products, expand(): jnp.einsum('sl,hlc->hsc', key_lat, w_part, preferred_element_type=jnp.flo...  18.6 us
    all_to_all x2, waiting for transfers between devices, reduce_runs(): per_run = lax.all_to_all(partials, 'fsdp', 0, 0, tiled=True)  13.7 us
    unnamed x68, local copies, waits for them, and re-layouts  13.5 us
  transfers between devices with their start and end apart: 19, of which 6 were waited for; matrix products, arithmetic and copies ran while one was open for 36% of the time, Pallas kernels for 0%

profile of v6, /device:TPU:120, one launch (start us, length us, event | category | flops | bytes accessed | tf_op | source)
XLA Modules:
  0.0 343.0 jit_solution(4935999190761823914)
XLA Ops:
  0.7 1.1 slice_bitcast_fusion
  1.8 2.9 broadcast_in_dim.110
  4.7 7.9 %all-to-all-start = ((bf16[32,512,128]{2,1,0:T(8,128)(2,1)}), bf16[32,512,128]{2,1,0:T(8,128)(2,1)}, u32[]{:S(2)}, u32[]{:S(2)}) async-start(bf16[32,512,128]{2,1,0:T(8,128)(2,1)} %broadcast_in_dim.110), calls=%async_computation | async-start | bytes 8388608 | tf_op jit(solution)/shard_map/all_to_all | solution.py:161
  14.6 3.4 collective-permute-start
  19.4 4.3 %collective-permute-start.1 = (bf16[2,64,512]{2,1,0:T(8,128)(2,1)S(1)}, bf16[2,64,512]{2,1,0:T(8,128)(2,1)S(1)}, u32[]{:S(2)}, u32[]{:S(2)}) collective-permute-start(bf16[2,64,512]{2,1,0:T(8,128)(2,1)S(1)} %broadcast_select_fusion.5), channel_id=1, source_target_pairs={{0,8},{4,12},{8,16},{12,20},{16,24},{20,28},{24,32},{28,36},{32,40... | collective-permute-start | bytes 393224 | tf_op jit(solution)/shard_map/ppermute | solution.py:17
  25.6 2.8 collective-permute-start.2
  29.8 0.7 broadcast_select_fusion.3
  30.5 3.4 collective-permute-start.3
  35.7 0.7 broadcast_select_fusion.2
  36.5 5.8 %collective-permute-start.4 = (bf16[2,64,512]{2,1,0:T(8,128)(2,1)}, bf16[2,64,512]{2,1,0:T(8,128)(2,1)}, u32[]{:S(2)}, u32[]{:S(2)}) collective-permute-start(bf16[2,64,512]{2,1,0:T(8,128)(2,1)} %broadcast_select_fusion.2), channel_id=1, source_target_pairs={{0,20},{4,24},{8,28},{12,32},{16,36},{20,40},{24,44},{28,48},{32,5... | collective-permute-start | bytes 393224 | tf_op jit(solution)/shard_map/ppermute | solution.py:17
  44.5 6.2 %gather_fusion.1 = s32[1024]{0:T(1024)S(1)} fusion(s32[8192]{0:T(1024)S(1)} %copy-done.2, s32[1024]{0:T(1024)S(1)} %get-tuple-element.40), kind=kCustom, calls=%fused_computation.7 | custom fusion | bytes 12288 | tf_op jit(solution)/shard_map/jit(_take)/gather | solution.py:89
  50.6 1.7 gather_fusion.2
  54.6 0.7 constant_dynamic-update-slice_fusion.6
  55.3 0.8 compare_and_fusion
  57.4 3.7 %copy.70 = bf16[256,32,128]{2,0,1:T(8,128)(2,1)} copy(bf16[256,32,128]{2,1,0:T(8,128)(2,1)} %param.10) | data formatting | bytes 4194304 | tf_op args[2]
  61.1 4.9 %collective-permute-done = bf16[2,64,512]{2,1,0:T(8,128)(2,1)S(1)} collective-permute-done((bf16[2,64,512]{2,1,0:T(8,128)(2,1)S(1)}, bf16[2,64,512]{2,1,0:T(8,128)(2,1)S(1)}, u32[]{:S(2)}, u32[]{:S(2)}) %collective-permute-start) | collective-permute-done | bytes 131104 | tf_op jit(solution)/shard_map/ppermute | solution.py:17
  66.0 9.7 %collective-permute-start.5 = (bf16[2,64,512]{2,1,0:T(8,128)(2,1)S(1)}, bf16[2,64,512]{2,1,0:T(8,128)(2,1)S(1)}, u32[]{:S(2)}, u32[]{:S(2)}) collective-permute-start(bf16[2,64,512]{2,1,0:T(8,128)(2,1)S(1)} %broadcast_select_fusion.1), channel_id=1, source_target_pairs={{0,24},{4,28},{8,32},{12,36},{16,40},{20,44},{24,48},{28,52},{32,5... | collective-permute-start | bytes 393224 | tf_op jit(solution)/shard_map/ppermute | solution.py:17
  75.8 0.7 constant_dynamic-update-slice_fusion.5
  76.4 0.7 constant_dynamic-update-slice_fusion.4
  77.1 0.7 constant_dynamic-update-slice_fusion.3
  77.8 1.6 constant_dynamic-update-slice_fusion.2
  79.4 1.6 constant_dynamic-update-slice_fusion.1
  80.9 0.7 constant_dynamic-update-slice_fusion
  81.6 1.8 gather_fusion
  83.4 2.9 broadcast_in_dim.192
  86.4 12.6 %all-to-all-start.1 = ((bf16[32,512,128]{2,1,0:T(8,128)(2,1)}), bf16[32,512,128]{2,1,0:T(8,128)(2,1)}, u32[]{:S(2)}, u32[]{:S(2)}) async-start(bf16[32,512,128]{2,1,0:T(8,128)(2,1)} %broadcast_in_dim.192), calls=%async_computation.1 | async-start | bytes 8388608 | tf_op jit(solution)/shard_map/all_to_all | solution.py:161
  99.0 1.1 broadcast_select_fusion
  100.4 9.3 %convolution_convert_fusion.1 = bf16[1024,32,128]{2,0,1:T(8,128)(2,1)} fusion(bf16[32,512,128]{2,1,0:T(8,128)(2,1)} %all-to-all-done, bf16[1024,512]{1,0:T(8,128)(2,1)S(1)} %bitcast_select_fusion.4), kind=kOutput, calls=%fused_computation.26 | convolution fusion | flops 4299161600 | bytes 13631488 | tf_op jit(solution)/shard_map/sl,hlc->hsc/dot_general | solution.py:24
  109.7 9.2 %fusion.21 = f32[32,4,256,64]{2,3,1,0:T(8,128)} fusion(bf16[32,4,256,128]{3,2,1,0:T(8,128)(2,1)} %bitcast.106, bf16[4,64,32,128]{3,2,1,0:T(8,128)(2,1)S(1)} %bitcast.102), kind=kOutput, calls=%fused_computation.42 | convolution fusion | flops 536870912 | bytes 18874368 | tf_op jit(solution)/shard_map/qbhd,hqkd->hqbk/dot_general | solution.py:37
  118.8 12.7 %fusion.91 = (f32[32,4,64]{2,1,0:T(4,128)S(1)}, f32[32,4,64,256]{3,2,1,0:T(8,128)}) fusion(f32[32,4,256,64]{2,3,1,0:T(8,128)} %fusion.21, pred[4,64,256]{2,1,0:T(8,128)(4,1)S(1)} %copy-done.10), kind=kOutput, calls=%fused_computation.242 | output fusion | flops 12583167 | bytes 16875520 | tf_op jit(solution)/shard_map/sub | solution.py:42
  131.5 8.3 %convolution_convert_fusion.2 = bf16[32,4,256,128]{3,2,1,0:T(8,128)(2,1)} fusion(bf16[32,4,64,128]{3,2,1,0:T(8,128)(2,1)S(1)} %bitcast.117, f32[32,4,64,256]{3,2,1,0:T(8,128)} %get-tuple-element.26, f32[32,4,64]{2,1,0:T(4,128)S(1)} %get-tuple-element.25), kind=kOutput, calls=%fused_computation.27 | convolution fusion | flops 545259520 | bytes 18907136 | tf_op jit(solution)/shard_map/hqbk,hqbd->hqkd/dot_general | solution.py:46
  139.8 3.0 all-to-all-done.1
  142.9 9.2 %convolution_convert_fusion = bf16[1024,32,128]{2,0,1:T(8,128)(2,1)} fusion(bf16[32,512,128]{2,1,0:T(8,128)(2,1)} %all-to-all-done.1, bf16[1024,512]{1,0:T(8,128)(2,1)S(1)} %copy-done.8), kind=kOutput, calls=%fused_computation.25 | convolution fusion | flops 4299161600 | bytes 13631488 | tf_op jit(solution)/shard_map/sl,hlc->hsc/dot_general | solution.py:24
  152.1 8.4 %multiply_reduce_fusion = f32[32,4,64]{2,1,0:T(4,128)S(1)} fusion(bf16[32,4,64,128]{3,2,1,0:T(8,128)(2,1)S(1)} %bitcast.118, bf16[32,4,256,128]{3,2,1,0:T(8,128)(2,1)} %bitcast.125, f32[32,4,64,256]{3,2,1,0:T(8,128)} %get-tuple-element.26, f32[32,4,64]{2,1,0:T(4,128)S(1)} %get-tuple-element.25), kind=kOutput, calls=%fused_computation.33 | convolution fusion | flops 544202752 | bytes 18939904 | tf_op jit(solution)/shard_map/hqbk,hqkd->hqbd/dot_general | solution.py:60
  160.5 12.3 %fusion.6 = bf16[32,4,64,256]{3,2,1,0:T(8,128)(2,1)} fusion(f32[32,4,64]{2,1,0:T(4,128)S(1)} %multiply_reduce_fusion, f32[32,4,64,256]{3,2,1,0:T(8,128)} %get-tuple-element.26, f32[32,4,64]{2,1,0:T(4,128)S(1)} %get-tuple-element.25, bf16[32,4,256,128]{3,2,1,0:T(8,128)(2,1)} %bitcast.126, bf16[32,4,64,128]{3,2,1,0:T(8,128)(2,1)} %bitcast.116), kind=kOutput, calls=%fused_computation.18 | convolution fusion | flops 545259520 | bytes 23134208 | tf_op jit(solution)/shard_map/hqbd,hqkd->hqbk/dot_general | solution.py:64
  172.8 9.6 %multiply_convert_fusion = bf16[32,4,256,128]{3,2,1,0:T(8,128)(2,1)} fusion(bf16[32,4,64,256]{3,2,1,0:T(8,128)(2,1)} %fusion.6, bf16[4,64,32,128]{3,2,1,0:T(8,128)(2,1)S(1)} %bitcast.103), kind=kOutput, calls=%fused_computation.10 | convolution fusion | flops 545259520 | bytes 14680064 | tf_op jit(solution)/shard_map/hqbk,qbhd->hqkd/dot_general | solution.py:73
  182.4 10.0 %convert_bitcast_fusion = bf16[32,512,128]{1,2,0:T(8,128)(2,1)} fusion(bf16[32,1024,128]{2,1,0:T(8,128)(2,1)} %bitcast.123, bf16[1024,512,1]{1,0,2:T(8,128)(2,1)S(1)} %bitcast.121), kind=kOutput, calls=%fused_computation.30 | convolution fusion | flops 4297064448 | bytes 13631488 | tf_op jit(solution)/shard_map/sl,hsc->hlc/dot_general | solution.py:28
  192.4 12.5 %all-to-all-start.3 = ((bf16[32,512,128]{1,2,0:T(8,128)(2,1)}), bf16[32,512,128]{1,2,0:T(8,128)(2,1)}, u32[]{:S(2)}, u32[]{:S(2)}) async-start(bf16[32,512,128]{1,2,0:T(8,128)(2,1)} %convert_bitcast_fusion), calls=%async_computation.3 | async-start | bytes 8388608 | tf_op jit(solution)/shard_map/all_to_all | solution.py:164
  204.9 8.2 %fusion.92 = f32[1024,512,1]{0,1,2:T(8,128)S(1)} fusion(bf16[32,1024,128]{2,1,0:T(8,128)(2,1)} %bitcast.104, bf16[32,512,128]{2,1,0:T(8,128)(2,1)} %all-to-all-done), kind=kOutput, calls=%fused_computation.243 | convolution fusion | flops 4294967296 | bytes 14680064 | tf_op jit(solution)/shard_map/hsc,hlc->sl/dot_general | solution.py:76
  213.2 8.2 %bitcast_add_fusion = f32[1024,512]{0,1:T(8,128)S(1)} fusion(f32[1024,512,1]{0,1,2:T(8,128)S(1)} %fusion.92, bf16[32,1024,128]{2,1,0:T(8,128)(2,1)} %bitcast.124, bf16[32,512,128]{2,1,0:T(8,128)(2,1)} %all-to-all-done.1), kind=kOutput, calls=%fused_computation.40 | convolution fusion | flops 4295491584 | bytes 16777216 | tf_op jit(solution)/shard_map/hsc,hlc->sl/dot_general | solution.py:78
  221.4 1.2 constant_dynamic-slice_fusion.3
  222.6 2.1 copy.78
  224.7 2.0 copy.77
  226.7 2.7 collective-permute-start.7
  229.4 1.0 copy.76
  230.6 10.1 %convert_bitcast_fusion.1 = bf16[32,512,128]{1,2,0:T(8,128)(2,1)} fusion(bf16[32,1024,128]{2,1,0:T(8,128)(2,1)} %bitcast.105, bf16[1024,512,1]{1,0,2:T(8,128)(2,1)} %bitcast.120), kind=kOutput, calls=%fused_computation.31 | convolution fusion | flops 4297064448 | bytes 13631488 | tf_op jit(solution)/shard_map/sl,hsc->hlc/dot_general | solution.py:28
  240.8 13.7 %all-to-all-done.3 = bf16[32,512,128]{1,2,0:T(8,128)(2,1)} async-done(((bf16[32,512,128]{1,2,0:T(8,128)(2,1)}), bf16[32,512,128]{1,2,0:T(8,128)(2,1)}, u32[]{:S(2)}, u32[]{:S(2)}) %all-to-all-start.3) | async-done | bytes 4194336 | tf_op jit(solution)/shard_map/all_to_all | solution.py:164
  254.4 8.8 %all-to-all-start.2 = ((bf16[32,512,128]{1,2,0:T(8,128)(2,1)}), bf16[32,512,128]{1,2,0:T(8,128)(2,1)}, u32[]{:S(2)}, u32[]{:S(2)}) async-start(bf16[32,512,128]{1,2,0:T(8,128)(2,1)} %convert_bitcast_fusion.1), calls=%async_computation.2 | async-start | bytes 8388608 | tf_op jit(solution)/shard_map/all_to_all | solution.py:164
  263.2 6.4 %fusion.15 = bf16[4,64,32,128]{3,1,2,0:T(8,128)(2,1)S(1)} fusion(bf16[32,4,256,128]{3,2,1,0:T(8,128)(2,1)} %bitcast.107, bf16[32,4,64,256]{3,2,1,0:T(8,128)(2,1)} %fusion.6), kind=kOutput, calls=%fused_computation.39 | convolution fusion | flops 538968064 | bytes 14680064 | tf_op jit(solution)/shard_map/hqbk,hqkd->qbhd/dot_general | solution.py:69
  269.8 2.7 copy.73
  272.6 5.2 %collective-permute-done.7 = f32[1024,128]{1,0:T(8,128)} collective-permute-done((f32[1024,128]{1,0:T(8,128)}, f32[1024,128]{1,0:T(8,128)}, u32[]{:S(2)}, u32[]{:S(2)}) %collective-permute-start.7) | collective-permute-done | bytes 524320 | tf_op jit(solution)/shard_map/ppermute | solution.py:182
  277.9 1.3 fusion.26
  279.7 3.3 collective-permute-start.14
  283.3 2.5 collective-permute-start.13
  286.2 5.1 %collective-permute-start.12 = (f32[2,8192]{1,0:T(2,128)S(1)}, f32[2,8192]{1,0:T(2,128)S(1)}, u32[]{:S(2)}, u32[]{:S(2)}) collective-permute-start(f32[2,8192]{1,0:T(2,128)S(1)} %fusion.47), channel_id=1, source_target_pairs={{16,0},{20,4},{24,8},{28,12},{32,16},{36,20},{40,24},{44,28},{48,3... | collective-permute-start | bytes 196616 | tf_op jit(solution)/shard_map/ppermute | solution.py:17
  291.6 4.6 %collective-permute-start.11 = (f32[2,8192]{1,0:T(2,128)S(1)}, f32[2,8192]{1,0:T(2,128)S(1)}, u32[]{:S(2)}, u32[]{:S(2)}) collective-permute-start(f32[2,8192]{1,0:T(2,128)S(1)} %fusion.49), channel_id=1, source_target_pairs={{12,0},{16,4},{20,8},{24,12},{28,16},{32,20},{36,24},{40,28},{44,3... | collective-permute-start | bytes 196616 | tf_op jit(solution)/shard_map/ppermute | solution.py:17
  296.6 1.9 collective-permute-start.10
  298.9 25.6 %collective-permute-done.14 = f32[2,8192]{1,0:T(2,128)S(1)} collective-permute-done((f32[2,8192]{1,0:T(2,128)S(1)}, f32[2,8192]{1,0:T(2,128)S(1)}, u32[]{:S(2)}, u32[]{:S(2)}) %collective-permute-start.14) | collective-permute-done | bytes 65568 | tf_op jit(solution)/shard_map/ppermute | solution.py:17
  324.4 1.9 collective-permute-start.9
  327.7 7.1 %collective-permute-done.9 = f32[2,8192]{1,0:T(2,128)S(1)} collective-permute-done((f32[2,8192]{1,0:T(2,128)S(1)}, f32[2,8192]{1,0:T(2,128)S(1)}, u32[]{:S(2)}, u32[]{:S(2)}) %collective-permute-start.9) | collective-permute-done | bytes 65568 | tf_op jit(solution)/shard_map/ppermute | solution.py:17
  335.4 0.7 reshape.725
  336.1 2.8 convert_reduce_fusion
  338.9 2.8 convert_reduce_fusion.1
  341.8 1.0 copy.81
  (193 shorter events, 18.5 us)
Async XLA Ops:
  0.6 109.0 %copy-start = (bf16[256,32,128]{2,1,0:T(8,128)(2,1)S(1)}, bf16[256,32,128]{2,1,0:T(8,128)(2,1)}, u32[]{:S(2)}) copy-start(bf16[256,32,128]{2,1,0:T(8,128)(2,1)} %param.9) | copy-start | bytes 6291460
  0.6 12.0 %copy-start.9 = (s32[128,4]{0,1:T(4,128)S(1)}, s32[128,4]{0,1:T(4,128)}, u32[]{:S(2)}) copy-start(s32[128,4]{0,1:T(4,128)} %param.13) | copy-start | bytes 6148
  0.7 13.3 %copy-start.3 = (bf16[256,512]{1,0:T(8,128)(2,1)S(1)}, bf16[256,512]{1,0:T(8,128)(2,1)}, u32[]{:S(2)}) copy-start(bf16[256,512]{1,0:T(8,128)(2,1)} %param.8) | copy-start | bytes 786436
  0.7 43.8 %copy-start.2 = (s32[8192]{0:T(1024)S(1)}, s32[8192]{0:T(1024)}, u32[]{:S(2)}) copy-start(s32[8192]{0:T(1024)} %param.12) | copy-start | bytes 98308
  4.7 78.7 %all-to-all-start = ((bf16[32,512,128]{2,1,0:T(8,128)(2,1)}), bf16[32,512,128]{2,1,0:T(8,128)(2,1)}, u32[]{:S(2)}, u32[]{:S(2)}) async-start(bf16[32,512,128]{2,1,0:T(8,128)(2,1)} %broadcast_in_dim.110), calls=%async_computation | async-start | bytes 8388608 | tf_op jit(solution)/shard_map/all_to_all | solution.py:161
  13.4 0.5 copy-start.11
  14.6 51.4 %collective-permute-start = (bf16[2,64,512]{2,1,0:T(8,128)(2,1)S(1)}, bf16[2,64,512]{2,1,0:T(8,128)(2,1)S(1)}, u32[]{:S(2)}, u32[]{:S(2)}) collective-permute-start(bf16[2,64,512]{2,1,0:T(8,128)(2,1)S(1)} %broadcast_select_fusion.6), channel_id=1, source_target_pairs={{0,4},{4,8},{8,12},{12,16},{16,20},{20,24},{24,28},{28,32},{32,36}... | collective-permute-start | bytes 393224 | tf_op jit(solution)/shard_map/ppermute | solution.py:17
  18.2 0.5 copy-start.13
  19.4 57.0 %collective-permute-start.1 = (bf16[2,64,512]{2,1,0:T(8,128)(2,1)S(1)}, bf16[2,64,512]{2,1,0:T(8,128)(2,1)S(1)}, u32[]{:S(2)}, u32[]{:S(2)}) collective-permute-start(bf16[2,64,512]{2,1,0:T(8,128)(2,1)S(1)} %broadcast_select_fusion.5), channel_id=1, source_target_pairs={{0,8},{4,12},{8,16},{12,20},{16,24},{20,28},{24,32},{28,36},{32,40... | collective-permute-start | bytes 393224 | tf_op jit(solution)/shard_map/ppermute | solution.py:17
  24.4 0.6 copy-start.15
  25.6 51.5 %collective-permute-start.2 = (bf16[2,64,512]{2,1,0:T(8,128)(2,1)S(1)}, bf16[2,64,512]{2,1,0:T(8,128)(2,1)S(1)}, u32[]{:S(2)}, u32[]{:S(2)}) collective-permute-start(bf16[2,64,512]{2,1,0:T(8,128)(2,1)S(1)} %broadcast_select_fusion.4), channel_id=1, source_target_pairs={{0,12},{4,16},{8,20},{12,24},{16,28},{20,32},{24,36},{28,40},{32,4... | collective-permute-start | bytes 393224 | tf_op jit(solution)/shard_map/ppermute | solution.py:17
  28.6 0.6 copy-start.17
  30.5 47.3 %collective-permute-start.3 = (bf16[2,64,512]{2,1,0:T(8,128)(2,1)}, bf16[2,64,512]{2,1,0:T(8,128)(2,1)}, u32[]{:S(2)}, u32[]{:S(2)}) collective-permute-start(bf16[2,64,512]{2,1,0:T(8,128)(2,1)} %broadcast_select_fusion.3), channel_id=1, source_target_pairs={{0,16},{4,20},{8,24},{12,28},{16,32},{20,36},{24,40},{28,44},{32,4... | collective-permute-start | bytes 393224 | tf_op jit(solution)/shard_map/ppermute | solution.py:17
  34.6 0.6 copy-start.19
  36.5 42.9 %collective-permute-start.4 = (bf16[2,64,512]{2,1,0:T(8,128)(2,1)}, bf16[2,64,512]{2,1,0:T(8,128)(2,1)}, u32[]{:S(2)}, u32[]{:S(2)}) collective-permute-start(bf16[2,64,512]{2,1,0:T(8,128)(2,1)} %broadcast_select_fusion.2), channel_id=1, source_target_pairs={{0,20},{4,24},{8,28},{12,32},{16,36},{20,40},{24,44},{28,48},{32,5... | collective-permute-start | bytes 393224 | tf_op jit(solution)/shard_map/ppermute | solution.py:17
  42.7 38.2 %copy-start.21 = (s32[2]{0:T(128)}, s32[2]{0:T(128)S(1)}, u32[]{:S(2)}) copy-start(s32[2]{0:T(128)S(1)} %fusion.60) | copy-start | bytes 28
  66.0 14.9 %collective-permute-start.5 = (bf16[2,64,512]{2,1,0:T(8,128)(2,1)S(1)}, bf16[2,64,512]{2,1,0:T(8,128)(2,1)S(1)}, u32[]{:S(2)}, u32[]{:S(2)}) collective-permute-start(bf16[2,64,512]{2,1,0:T(8,128)(2,1)S(1)} %broadcast_select_fusion.1), channel_id=1, source_target_pairs={{0,24},{4,28},{8,32},{12,36},{16,40},{20,44},{24,48},{28,52},{32,5... | collective-permute-start | bytes 393224 | tf_op jit(solution)/shard_map/ppermute | solution.py:17
  86.4 56.5 %all-to-all-start.1 = ((bf16[32,512,128]{2,1,0:T(8,128)(2,1)}), bf16[32,512,128]{2,1,0:T(8,128)(2,1)}, u32[]{:S(2)}, u32[]{:S(2)}) async-start(bf16[32,512,128]{2,1,0:T(8,128)(2,1)} %broadcast_in_dim.192), calls=%async_computation.1 | async-start | bytes 8388608 | tf_op jit(solution)/shard_map/all_to_all | solution.py:161
  100.3 9.3 %copy-start.7 = (bf16[1024,512]{1,0:T(8,128)(2,1)}, bf16[1024,512]{1,0:T(8,128)(2,1)S(1)}, u32[]{:S(2)}) copy-start(bf16[1024,512]{1,0:T(8,128)(2,1)S(1)} %bitcast_select_fusion.4) | copy-start | bytes 3145732
  109.7 9.2 %copy-start.10 = (pred[4,64,256]{2,1,0:T(8,128)(4,1)S(1)}, pred[4,64,256]{2,1,0:T(8,128)(4,1)}, u32[]{:S(2)}) copy-start(pred[4,64,256]{2,1,0:T(8,128)(4,1)} %compare_and_fusion) | copy-start | bytes 196612
  118.8 12.7 %copy-start.4 = (bf16[256,32,128]{2,0,1:T(8,128)(2,1)S(1)}, bf16[256,32,128]{2,0,1:T(8,128)(2,1)}, u32[]{:S(2)}) copy-start(bf16[256,32,128]{2,0,1:T(8,128)(2,1)} %copy.70) | copy-start | bytes 6291460
  131.5 11.4 %copy-start.8 = (bf16[1024,512]{1,0:T(8,128)(2,1)S(1)}, bf16[1024,512]{1,0:T(8,128)(2,1)}, u32[]{:S(2)}) copy-start(bf16[1024,512]{1,0:T(8,128)(2,1)} %copy-done.7) | copy-start | bytes 3145732
  142.9 9.3 %copy-start.5 = (bf16[256,32,128]{2,0,1:T(8,128)(2,1)S(1)}, bf16[256,32,128]{2,0,1:T(8,128)(2,1)}, u32[]{:S(2)}) copy-start(bf16[256,32,128]{2,0,1:T(8,128)(2,1)} %copy.70) | copy-start | bytes 6291460
  172.8 9.6 %copy-start.6 = (bf16[16,64,512]{2,1,0:T(8,128)(2,1)S(1)}, bf16[16,64,512]{2,1,0:T(8,128)(2,1)}, u32[]{:S(2)}) copy-start(bf16[16,64,512]{2,1,0:T(8,128)(2,1)} %broadcast_select_fusion) | copy-start | bytes 3145732
  192.4 62.1 %all-to-all-start.3 = ((bf16[32,512,128]{1,2,0:T(8,128)(2,1)}), bf16[32,512,128]{1,2,0:T(8,128)(2,1)}, u32[]{:S(2)}, u32[]{:S(2)}) async-start(bf16[32,512,128]{1,2,0:T(8,128)(2,1)} %convert_bitcast_fusion), calls=%async_computation.3 | async-start | bytes 8388608 | tf_op jit(solution)/shard_map/all_to_all | solution.py:164
  224.7 48.0 %collective-permute-start.8 = (f32[1024,128]{1,0:T(8,128)}, f32[1024,128]{1,0:T(8,128)}, u32[]{:S(2)}, u32[]{:S(2)}) collective-permute-start(f32[1024,128]{1,0:T(8,128)} %bitcast.28), channel_id=1, source_target_pairs={{0,3},{1,0},{2,1},{3,2},{4,7},{5,4},{6,5},{7,6},{8,11},{9,8},{10,9... | collective-permute-start | bytes 1572872 | tf_op jit(solution)/shard_map/ppermute | solution.py:182
  226.7 51.2 %collective-permute-start.7 = (f32[1024,128]{1,0:T(8,128)}, f32[1024,128]{1,0:T(8,128)}, u32[]{:S(2)}, u32[]{:S(2)}) collective-permute-start(f32[1024,128]{1,0:T(8,128)} %bitcast.27), channel_id=1, source_target_pairs={{0,2},{1,3},{2,0},{3,1},{4,6},{5,7},{6,4},{7,5},{8,10},{9,11},{10,... | collective-permute-start | bytes 1572872 | tf_op jit(solution)/shard_map/ppermute | solution.py:182
  230.4 47.5 %collective-permute-start.6 = (f32[1024,128]{1,0:T(8,128)}, f32[1024,128]{1,0:T(8,128)S(1)}, u32[]{:S(2)}, u32[]{:S(2)}) collective-permute-start(f32[1024,128]{1,0:T(8,128)} %bitcast.26), channel_id=1, source_target_pairs={{0,1},{1,2},{2,3},{3,0},{4,5},{5,6},{6,7},{7,4},{8,9},{9,10},{10,1... | collective-permute-start | bytes 1572872 | tf_op jit(solution)/shard_map/ppermute | solution.py:182
  254.4 84.5 %all-to-all-start.2 = ((bf16[32,512,128]{1,2,0:T(8,128)(2,1)}), bf16[32,512,128]{1,2,0:T(8,128)(2,1)}, u32[]{:S(2)}, u32[]{:S(2)}) async-start(bf16[32,512,128]{1,2,0:T(8,128)(2,1)} %convert_bitcast_fusion.1), calls=%async_computation.2 | async-start | bytes 8388608 | tf_op jit(solution)/shard_map/all_to_all | solution.py:164
  269.6 9.7 %copy-start.26 = (s32[2]{0:T(128)S(1)}, s32[2]{0:T(128)}, u32[]{:S(2)}) copy-start(s32[2]{0:T(128)} %iota_add_fusion) | copy-start | bytes 28
  269.7 13.3 %copy-start.25 = (s32[2]{0:T(128)S(1)}, s32[2]{0:T(128)}, u32[]{:S(2)}) copy-start(s32[2]{0:T(128)} %iota_add_fusion.1) | copy-start | bytes 28
  269.7 16.2 %copy-start.24 = (s32[2]{0:T(128)S(1)}, s32[2]{0:T(128)}, u32[]{:S(2)}) copy-start(s32[2]{0:T(128)} %iota_add_fusion.2) | copy-start | bytes 28
  269.7 21.6 %copy-start.23 = (s32[2]{0:T(128)S(1)}, s32[2]{0:T(128)}, u32[]{:S(2)}) copy-start(s32[2]{0:T(128)} %iota_add_fusion.3) | copy-start | bytes 28
  269.7 26.6 %copy-start.28 = (s32[2]{0:T(128)S(1)}, s32[2]{0:T(128)}, u32[]{:S(2)}) copy-start(s32[2]{0:T(128)} %iota_add_fusion.4) | copy-start | bytes 28
  269.7 28.8 %copy-start.27 = (s32[2]{0:T(128)S(1)}, s32[2]{0:T(128)}, u32[]{:S(2)}) copy-start(s32[2]{0:T(128)} %iota_add_fusion.5) | copy-start | bytes 28
  269.7 56.6 %copy-start.22 = (s32[2]{0:T(128)S(1)}, s32[2]{0:T(128)}, u32[]{:S(2)}) copy-start(s32[2]{0:T(128)} %copy-done.21) | copy-start | bytes 28
  269.7 56.9 %copy-start.20 = (s32[2]{0:T(128)S(1)}, s32[2]{0:T(128)}, u32[]{:S(2)}) copy-start(s32[2]{0:T(128)} %copy-done.19) | copy-start | bytes 28
  269.7 57.1 %copy-start.18 = (s32[2]{0:T(128)S(1)}, s32[2]{0:T(128)}, u32[]{:S(2)}) copy-start(s32[2]{0:T(128)} %copy-done.17) | copy-start | bytes 28
  269.7 57.4 %copy-start.16 = (s32[2]{0:T(128)S(1)}, s32[2]{0:T(128)}, u32[]{:S(2)}) copy-start(s32[2]{0:T(128)} %copy-done.15) | copy-start | bytes 28
  269.7 57.7 %copy-start.14 = (s32[2]{0:T(128)S(1)}, s32[2]{0:T(128)}, u32[]{:S(2)}) copy-start(s32[2]{0:T(128)} %copy-done.13) | copy-start | bytes 28
  269.8 65.0 %copy-start.12 = (s32[2]{0:T(128)S(1)}, s32[2]{0:T(128)}, u32[]{:S(2)}) copy-start(s32[2]{0:T(128)} %copy-done.11) | copy-start | bytes 28
  279.3 63.5 %copy-start.1 = (bf16[256,32,128]{2,1,0:T(8,128)(2,1)S(1)}, bf16[256,32,128]{2,1,0:T(8,128)(2,1)}, u32[]{:S(2)}) copy-start(bf16[256,32,128]{2,1,0:T(8,128)(2,1)} %param.9) | copy-start | bytes 6291460
  279.7 44.8 %collective-permute-start.14 = (f32[2,8192]{1,0:T(2,128)S(1)}, f32[2,8192]{1,0:T(2,128)S(1)}, u32[]{:S(2)}, u32[]{:S(2)}) collective-permute-start(f32[2,8192]{1,0:T(2,128)S(1)} %fusion.43), channel_id=1, source_target_pairs={{24,0},{28,4},{32,8},{36,12},{40,16},{44,20},{48,24},{52,28},{56,3... | collective-permute-start | bytes 196616 | tf_op jit(solution)/shard_map/ppermute | solution.py:17
  283.3 43.3 %collective-permute-start.13 = (f32[2,8192]{1,0:T(2,128)S(1)}, f32[2,8192]{1,0:T(2,128)S(1)}, u32[]{:S(2)}, u32[]{:S(2)}) collective-permute-start(f32[2,8192]{1,0:T(2,128)S(1)} %fusion.45), channel_id=1, source_target_pairs={{20,0},{24,4},{28,8},{32,12},{36,16},{40,20},{44,24},{48,28},{52,3... | collective-permute-start | bytes 196616 | tf_op jit(solution)/shard_map/ppermute | solution.py:17
  286.2 40.7 %collective-permute-start.12 = (f32[2,8192]{1,0:T(2,128)S(1)}, f32[2,8192]{1,0:T(2,128)S(1)}, u32[]{:S(2)}, u32[]{:S(2)}) collective-permute-start(f32[2,8192]{1,0:T(2,128)S(1)} %fusion.47), channel_id=1, source_target_pairs={{16,0},{20,4},{24,8},{28,12},{32,16},{36,20},{40,24},{44,28},{48,3... | collective-permute-start | bytes 196616 | tf_op jit(solution)/shard_map/ppermute | solution.py:17
  291.6 35.5 %collective-permute-start.11 = (f32[2,8192]{1,0:T(2,128)S(1)}, f32[2,8192]{1,0:T(2,128)S(1)}, u32[]{:S(2)}, u32[]{:S(2)}) collective-permute-start(f32[2,8192]{1,0:T(2,128)S(1)} %fusion.49), channel_id=1, source_target_pairs={{12,0},{16,4},{20,8},{24,12},{28,16},{32,20},{36,24},{40,28},{44,3... | collective-permute-start | bytes 196616 | tf_op jit(solution)/shard_map/ppermute | solution.py:17
  296.6 30.8 %collective-permute-start.10 = (f32[2,8192]{1,0:T(2,128)S(1)}, f32[2,8192]{1,0:T(2,128)S(1)}, u32[]{:S(2)}, u32[]{:S(2)}) collective-permute-start(f32[2,8192]{1,0:T(2,128)S(1)} %fusion.51), channel_id=1, source_target_pairs={{8,0},{12,4},{16,8},{20,12},{24,16},{28,20},{32,24},{36,28},{40,32... | collective-permute-start | bytes 196616 | tf_op jit(solution)/shard_map/ppermute | solution.py:17
  324.4 10.4 %collective-permute-start.9 = (f32[2,8192]{1,0:T(2,128)S(1)}, f32[2,8192]{1,0:T(2,128)S(1)}, u32[]{:S(2)}, u32[]{:S(2)}) collective-permute-start(f32[2,8192]{1,0:T(2,128)S(1)} %fusion.53), channel_id=1, source_target_pairs={{4,0},{8,4},{12,8},{16,12},{20,16},{24,20},{28,24},{32,28},{36,32}... | collective-permute-start | bytes 196616 | tf_op jit(solution)/shard_map/ppermute | solution.py:17
